TPU v7x, 256 devices: a whole 4x4x8 slice. The times are simulated.
256 devices in a mesh: seq: 64 (over y, z_lo, x), tp: 4 (over z_hi, core).
Axes of the slice: x: 4, y: 4, z: 8 (z_hi: 2, z_lo: 4; z = z_hi * 4 + z_lo), core: 2. Of those that a mesh axis runs over, the one named last changes fastest.
Arguments:
- hidden: bfloat16 [16384, 1024], P('seq'), may hold values from -6 to 6
- segment_ids: int32 [16384], replicated, may hold values from 0 to 7, never falling along the last dimension, each value on 1 to 12288 neighbouring positions
- routes: int32 [16384, 8], P('seq'), may hold values from 0 to 31, all different within a row; in each aligned block of 128 rows (0 to 127, 128 to 255, ...) at most 64 rows name the same one
- gates: float32 [16384, 8], P('seq'), may hold values from 0.02 to 0.25
- norm_attn: bfloat16 [1024], replicated, may hold values from 0.5 to 1.5
- norm_moe: bfloat16 [1024], replicated, may hold values from 0.5 to 1.5
- w_query: bfloat16 [1024, 1024], P(None, 'tp')
- w_key: bfloat16 [1024, 512], P(None, 'tp')
- w_value: bfloat16 [1024, 512], P(None, 'tp'), may hold values from -0.1875 to 0.1875
- w_out: bfloat16 [1024, 1024], P('tp'), may hold values from -1 to 1
- w_gate: bfloat16 [64, 1024, 512], P('seq', None, 'tp'), as said below
- w_up: bfloat16 [64, 1024, 512], P('seq', None, 'tp'), as said below
- w_down: bfloat16 [64, 512, 1024], P('seq', 'tp'), as said below
Outputs:
- hidden_out: bfloat16 [16384, 1024], P('seq')
- kv_cache: bfloat16 [16384, 2, 512], P('seq', None, 'tp')
Inputs may be any that keep to these rules, and one draw needn't show every extreme that they name: `segment_ids`: segment numbers start at 0, never fall and rise by one at each new segment; no segment is longer than 12288 tokens and one has exactly 12288. `routes`: each row names 8 different experts. In each aligned block of 128 rows no expert is named by more than 64 rows, a bound that some block reaches. Slot s holds the weights of expert s mod 32: w_gate[s] equals w_gate[s mod 32]. w_up[s] equals w_up[s mod 32]. w_down[s] equals w_down[s mod 32].
All inputs are finite; a program needn't handle non-finite values.
Results may differ from a plain program's by a relative error of at most 0.018.
Values may be sent and summed in bfloat16 or wider, within the bound.
No kernel may reach another device: no remote copies, remote signals or barrier semaphores. Data moves between devices by JAX's collectives and lax.ppermute only.
A program may use at most 64 MiB of HBM per device.

v0:
```python
import jax
import jax.numpy as jnp
from jax import lax
from jax.sharding import PartitionSpec as P

HEAD_DIM = 64
EXPERTS = 32


EPS = 1e-06
SCORE_SCALE = 0.015625


def normalize(values, gain):
    widened = values.astype(jnp.float32)
    return (
        widened
        * lax.rsqrt(jnp.mean(widened * widened, axis=-1, keepdims=True) + EPS)
        * gain.astype(jnp.float32)
    )


def rotary(tensor, positions):
    half_dim = tensor.shape[-1] // 2
    frequencies = 10000.0 ** (-jnp.arange(half_dim, dtype=jnp.float32) * 2.0 / tensor.shape[-1])
    angles = positions.astype(jnp.float32)[:, None] * frequencies[None, :]
    cosine = jnp.cos(angles)[:, None, :]
    sine_part = jnp.sin(angles)[:, None, :]
    lower_half = tensor[..., :half_dim]
    upper_half = tensor[..., half_dim:]
    return jnp.concatenate(
        [
            lower_half * cosine - upper_half * sine_part,
            upper_half * cosine + lower_half * sine_part,
        ],
        axis=-1,
    )


def segment_positions(segment_ids):
    index_all = jnp.arange(segment_ids.shape[0], dtype=jnp.int32)
    changed = jnp.concatenate([jnp.ones((1,), jnp.bool_), segment_ids[1:] != segment_ids[:-1]])
    starts = lax.cummax(jnp.where(changed, index_all, 0), axis=0)
    return index_all - starts


def per_device(
    hidden,
    segment_ids,
    routes,
    gates,
    norm_attn,
    norm_moe,
    w_query,
    w_key,
    w_value,
    w_out,
    w_gate,
    w_up,
    w_down,
):
    tokens = hidden.shape[0]
    model_width = hidden.shape[1]
    first_row = lax.axis_index("seq") * tokens
    positions = lax.dynamic_slice_in_dim(segment_positions(segment_ids), first_row, tokens)
    own_segs = lax.dynamic_slice_in_dim(segment_ids, first_row, tokens)
    normed = normalize(hidden, norm_attn).astype(jnp.bfloat16)
    query_heads = w_query.shape[1] // HEAD_DIM
    kv_heads = w_key.shape[1] // HEAD_DIM
    group_size = query_heads // kv_heads
    queries = jnp.dot(normed, w_query, preferred_element_type=jnp.float32).reshape(
        tokens, query_heads, HEAD_DIM
    )
    queries = (
        rotary(queries, positions)
        .astype(jnp.bfloat16)
        .reshape(tokens, kv_heads, group_size, HEAD_DIM)
    )
    key_raw = jnp.dot(normed, w_key, preferred_element_type=jnp.float32).reshape(
        tokens, kv_heads, HEAD_DIM
    )
    value_proj = jnp.dot(normed, w_value, preferred_element_type=jnp.float32).astype(jnp.bfloat16)
    kv_cache = jnp.stack(
        [key_raw.reshape(tokens, kv_heads * HEAD_DIM).astype(jnp.bfloat16), value_proj], axis=1
    )
    key_rot = rotary(key_raw, positions).astype(jnp.bfloat16)
    value_heads = value_proj.reshape(tokens, kv_heads, HEAD_DIM)
    query_index = first_row + jnp.arange(tokens, dtype=jnp.int32)
    last_query = first_row + tokens - 1
    lowest_seg = own_segs[0]

    def attend(carried, key_rows, value_rows, key_start, key_segs):
        running_max, weight_sum, accumulated = carried
        scores = (
            jnp.einsum("tkgd,skd->kgts", queries, key_rows, preferred_element_type=jnp.float32)
            * SCORE_SCALE
        )
        key_index = key_start + jnp.arange(key_rows.shape[0], dtype=jnp.int32)
        allowed = (own_segs[:, None] == key_segs[None, :]) & (
            query_index[:, None] >= key_index[None, :]
        )
        masked = jnp.where(allowed, scores, -1e30)
        new_max = jnp.maximum(running_max, jnp.max(masked, axis=-1))
        weights = jnp.where(allowed, jnp.exp(masked - new_max[..., None]), 0.0)
        factor = jnp.exp(running_max - new_max)
        weight_sum = weight_sum * factor + jnp.sum(weights, axis=-1)
        accumulated = accumulated * factor[..., None] + jnp.einsum(
            "kgts,skd->kgtd",
            weights.astype(jnp.bfloat16),
            value_rows,
            preferred_element_type=jnp.float32,
        )
        return (new_max, weight_sum, accumulated)

    start_state = (
        jnp.full((kv_heads, group_size, tokens), -1e30, jnp.float32),
        jnp.zeros((kv_heads, group_size, tokens), jnp.float32),
        jnp.zeros((kv_heads, group_size, tokens, HEAD_DIM), jnp.float32),
    )
    keys_all = lax.all_gather(key_rot, "seq", axis=0, tiled=True)
    values_all = lax.all_gather(value_heads, "seq", axis=0, tiled=True)
    block_total = keys_all.shape[0] // tokens

    def visit_block(block_index, state_now):
        key_start = block_index * tokens
        key_rows = lax.dynamic_slice_in_dim(keys_all, block_index * tokens, tokens)
        value_rows = lax.dynamic_slice_in_dim(values_all, block_index * tokens, tokens)
        key_segs = lax.dynamic_slice_in_dim(segment_ids, key_start, tokens)
        relevant = (key_start <= last_query) & (key_segs[tokens - 1] >= lowest_seg)
        return lax.cond(
            relevant,
            lambda inner: attend(inner, key_rows, value_rows, key_start, key_segs),
            lambda inner: inner,
            state_now,
        )

    running_max, weight_sum, accumulated = lax.fori_loop(0, block_total, visit_block, start_state)
    attended = (
        (accumulated / weight_sum[..., None])
        .transpose(2, 0, 1, 3)
        .reshape(tokens, query_heads * HEAD_DIM)
    )
    attended = attended.astype(jnp.bfloat16)
    partial_out = jnp.dot(attended, w_out, preferred_element_type=jnp.float32)
    attn_mixed = lax.psum(partial_out.astype(jnp.bfloat16), "tp").astype(jnp.float32)
    residual = (hidden.astype(jnp.float32) + attn_mixed).astype(jnp.bfloat16)
    normed_moe = normalize(residual, norm_moe).astype(jnp.bfloat16)
    route_count = routes.shape[1]
    slots_dev = w_gate.shape[0]
    seq_count = lax.axis_size("seq")
    slot_total = slots_dev * seq_count
    copies = slot_total // EXPERTS
    block_rows = tokens // copies
    capacity = 2 * block_rows * route_count // EXPERTS
    copy_of = (jnp.arange(tokens, dtype=jnp.int32) // block_rows)[:, None]
    slot_of = routes + EXPERTS * copy_of
    flat_expert = routes.reshape(copies, block_rows * route_count)
    onehot = (
        flat_expert[:, :, None] == jnp.arange(EXPERTS, dtype=jnp.int32)[None, None, :]
    ).astype(jnp.int32)
    before = jnp.cumsum(onehot, axis=1) - onehot
    slot_rank = jnp.sum(before * onehot, axis=2).reshape(tokens, route_count)
    target = slot_of * capacity + slot_rank
    token_ids = jnp.broadcast_to(
        jnp.arange(tokens, dtype=jnp.int32)[:, None], (tokens, route_count)
    )
    source = (
        jnp.full((slot_total * capacity,), tokens, jnp.int32)
        .at[target.reshape(-1)]
        .set(token_ids.reshape(-1))
    )
    padded_rows = jnp.concatenate([normed_moe, jnp.zeros((1, normed_moe.shape[1]), jnp.bfloat16)])
    outbound = padded_rows[source].reshape(seq_count, slots_dev, capacity, normed_moe.shape[1])
    arrived = lax.all_to_all(outbound, "seq", split_axis=0, concat_axis=0, tiled=True)
    gate_val = jnp.einsum("jsrd,sdf->jsrf", arrived, w_gate, preferred_element_type=jnp.float32)
    up_val = jnp.einsum("jsrd,sdf->jsrf", arrived, w_up, preferred_element_type=jnp.float32)
    activated = (jax.nn.silu(gate_val) * up_val).astype(jnp.bfloat16)
    group_part = jnp.einsum("jsrf,sfd->jsrd", activated, w_down, preferred_element_type=jnp.float32)
    result = group_part.astype(jnp.bfloat16)
    returned = lax.all_to_all(result, "seq", split_axis=0, concat_axis=0, tiled=True).reshape(
        slot_total * capacity, model_width
    )
    picked = returned[target]
    combined = jnp.einsum(
        "tk,tkd->td",
        gates,
        picked,
        preferred_element_type=jnp.float32,
        precision=lax.Precision.HIGHEST,
    )
    expert_sum = lax.psum(combined.astype(jnp.bfloat16), "tp").astype(jnp.float32)
    hidden_out = (residual.astype(jnp.float32) + expert_sum).astype(jnp.bfloat16)
    return (hidden_out, kv_cache)


def solution(mesh):
    return jax.shard_map(
        per_device,
        mesh=mesh,
        in_specs=(
            P("seq", None),
            P(),
            P("seq", None),
            P("seq", None),
            P(),
            P(),
            P(None, "tp"),
            P(None, "tp"),
            P(None, "tp"),
            P("tp", None),
            P("seq", None, "tp"),
            P("seq", None, "tp"),
            P("seq", "tp", None),
        ),
        out_specs=(P("seq", None), P("seq", None, "tp")),
        check_vma=False,
    )
```

profile of v0, /device:TPU:1, one launch (start us, length us, event | category | flops | bytes accessed | tf_op | source)
XLA Modules:
  0.0 1440.4 jit_solution(9744789286985042659)
XLA Ops:
  7.3 1.0 slice_compare_fusion
  9.9 1.2 fusion.34
  11.4 1.5 fusion.59
  13.6 2.1 convolution_convert_fusion.1
  15.8 0.8 dynamic_slice.37
  17.5 18.0 %reduce-window.19 = s32[2,32,8,128]{3,2,1,0:T(8,128)S(1)} reduce-window(s32[2,32,8,128]{3,2,1,0:T(8,128)S(1)} %fusion.49, s32[]{:T(128)} %constant.107.clone.1), window={size=1x1x1x128 pad=0_0x0_0x0_0x127_0}, to_apply=%region_11.12 | reduce-window | flops 8323072 | bytes 524292 | tf_op jit(solution)/shard_map/reduce-window.2
  37.3 224.4 %all-gather.3.cloned.1.call-done = bf16[16384,2,64]{0,2,1:T(8,128)(2,1)} async-done(((bf16[256,2,64]{0,2,1:T(8,128)(2,1)}), bf16[16384,2,64]{0,2,1:T(8,128)(2,1)}) %all-gather.3.cloned.1.call-update) | async-done | bytes 4194320 | tf_op jit(solution)/shard_map/all_gather | solution.py:120
  261.8 278.6 %all-gather.5.cloned.1.call-done = bf16[16384,2,64]{0,2,1:T(8,128)(2,1)} async-done(((bf16[256,2,64]{0,2,1:T(8,128)(2,1)}), bf16[16384,2,64]{0,2,1:T(8,128)(2,1)}) %all-gather.5.cloned.1.call-update) | async-done | bytes 4194320 | tf_op jit(solution)/shard_map/all_gather | solution.py:121
  540.4 162.2 %while.18 = (s32[]{:T(128)}, f32[2,2,256]{2,1,0:T(2,128)S(1)}, f32[2,2,256]{2,1,0:T(2,128)S(1)}, f32[2,2,256,64]{2,3,1,0:T(8,128)S(1)}, s32[]{:T(128)}, /*index=...) while((s32[]{:T(128)}, f32[2,2,256]{2,1,0:T(2,128)S(1)}, ...), condition=%wide.region_8.9_spmd.clone, body=%wide.region_3.8_spmd.clone.sunk | while | flops 69798408 | bytes 4271497 | solution.py:137
  540.5 0.8 dynamic_slice.55
  542.9 2.8 conditional.3
  543.1 1.2 fusion.61
  544.5 1.2 convolution_add_fusion
  545.8 0.8 dynamic_slice.55
  548.2 0.8 dynamic_slice.55
  550.7 0.8 dynamic_slice.55
  553.2 0.8 dynamic_slice.55
  555.7 0.8 dynamic_slice.55
  558.2 0.8 dynamic_slice.55
  560.7 0.8 dynamic_slice.55
  563.2 0.8 dynamic_slice.55
  565.7 0.8 dynamic_slice.55
  568.2 0.8 dynamic_slice.55
  570.7 0.8 dynamic_slice.55
  573.1 0.8 dynamic_slice.55
  575.6 0.8 dynamic_slice.55
  578.1 0.8 dynamic_slice.55
  580.6 0.8 dynamic_slice.55
  583.1 0.8 dynamic_slice.55
  585.6 0.8 dynamic_slice.55
  588.1 0.8 dynamic_slice.55
  590.6 0.8 dynamic_slice.55
  593.1 0.8 dynamic_slice.55
  595.6 0.8 dynamic_slice.55
  598.0 0.8 dynamic_slice.55
  600.5 0.8 dynamic_slice.55
  603.0 0.8 dynamic_slice.55
  605.5 0.8 dynamic_slice.55
  608.0 0.8 dynamic_slice.55
  610.5 0.8 dynamic_slice.55
  613.0 0.8 dynamic_slice.55
  615.5 0.8 dynamic_slice.55
  618.0 0.8 dynamic_slice.55
  620.5 0.8 dynamic_slice.55
  623.0 0.8 dynamic_slice.55
  625.4 0.8 dynamic_slice.55
  702.7 1.1 convolution_convert_fusion
  703.8 8.1 scatter_custom_fusion
  711.9 213.3 %all-reduce.4.cloned.1.call-done = bf16[256,1024]{1,0:T(8,128)(2,1)} async-done(((bf16[256,1024]{1,0:T(8,128)(2,1)}), bf16[256,1024]{1,0:T(8,128)(2,1)}) %all-reduce.4.cloned.1.call-update) | async-done | bytes 524304 | tf_op jit(solution)/shard_map/psum | solution.py:145
  925.2 1.3 fusion.38
  926.5 1.3 fusion.40
  927.8 18.3 %gather_fusion = bf16[4096,1024]{1,0:T(8,128)(2,1)} fusion(bf16[257,1024]{1,0:T(8,128)(2,1)S(1)} %concatenate.27, s32[4096]{0:T(1024)S(1)} %fusion.50), kind=kCustom, calls=%fused_computation | custom fusion | bytes 16793600 | tf_op jit(solution)/shard_map/gather | solution.py:173
  946.1 194.0 %all_to_all.10 = bf16[64,1,64,1024]{3,2,1,0:T(8,128)(2,1)S(1)} all-to-all(bf16[64,1,64,1024]{3,2,1,0:T(8,128)(2,1)} %bitcast.133), channel_id=1, replica_groups=mesh['seq'=64,'tp'=4] {'seq'}, dimensions={0} | all-to-all | bytes 16777216 | tf_op jit(solution)/shard_map/all_to_all | solution.py:174
  1140.1 3.2 copy-done.1
  1143.3 2.4 fusion.19
  1145.8 12.3 convert_bitcast_fusion
  1158.1 6.7 all-to-all-start.1
  1165.5 182.4 %all-to-all-done.1 = bf16[64,1,64,1024]{3,2,1,0:T(8,128)(2,1)} async-done(((bf16[64,1,64,1024]{3,2,1,0:T(8,128)(2,1)}), bf16[64,1,64,1024]{3,2,1,0:T(8,128)(2,1)}, u32[]{:S(2)}, u32[]{:S(2)}) %all-to-all-start.1) | async-done | bytes 8388640 | tf_op jit(solution)/shard_map/all_to_all | solution.py:180
  1347.9 15.5 %gather_fusion.1 = bf16[2048,1024]{1,0:T(8,128)(2,1)} fusion(bf16[4096,1024]{1,0:T(8,128)(2,1)} %bitcast.40, s32[2048]{0:T(1024)S(1)} %broadcast_clamp_fusion), kind=kCustom, calls=%fused_computation.1 | custom fusion | bytes 8396800 | tf_op jit(solution)/shard_map/gather | solution.py:183
  1363.4 5.9 fusion.21
  1369.3 1.0 copy.64
  1370.3 0.8 copy.57
  1371.1 60.7 %all-reduce.6.cloned.1.call-done = bf16[256,1024]{1,0:T(8,128)(2,1)} async-done(((bf16[256,1024]{1,0:T(8,128)(2,1)}), bf16[256,1024]{1,0:T(8,128)(2,1)}) %all-reduce.6.cloned.1.call-update) | async-done | bytes 524304 | tf_op jit(solution)/shard_map/psum | solution.py:191
  1431.8 2.1 fusion.41
  (311 shorter events, 65.3 us)
Async XLA Ops:
  7.2 695.5 %copy-start = (bf16[256,1024]{1,0:T(8,128)(2,1)S(1)}, bf16[256,1024]{1,0:T(8,128)(2,1)}, u32[]{:S(2)}) copy-start(bf16[256,1024]{1,0:T(8,128)(2,1)} %param.26) | copy-start | bytes 1572868
  7.2 9.4 copy-start.7
  7.2 10.3 copy-start.9
  7.2 254.6 %all-gather.3.cloned.1.call-start = ((), (), s32[]{:S(2)}) async-start(), calls=%async_computation.2 | async-start | bytes 4259840 | tf_op jit(solution)/shard_map/all_gather | solution.py:120
  8.5 28.3 %copy-start.2 = (bf16[256,1024]{1,0:T(8,128)(2,1)S(1)}, bf16[256,1024]{1,0:T(8,128)(2,1)}, u32[]{:S(2)}) copy-start(bf16[256,1024]{1,0:T(8,128)(2,1)} %param.17) | copy-start | bytes 1572868
  8.5 28.3 %copy-start.10 = (bf16[1024,256]{1,0:T(8,128)(2,1)S(1)}, bf16[1024,256]{1,0:T(8,128)(2,1)}, u32[]{:S(2)}) copy-start(bf16[1024,256]{1,0:T(8,128)(2,1)} %param.23) | copy-start | bytes 1572868
  13.6 526.8 %all-gather.5.cloned.1.call-start = ((), (), s32[]{:S(2)}) async-start(), calls=%async_computation.3 | async-start | bytes 4259840 | tf_op jit(solution)/shard_map/all_gather | solution.py:121
  15.8 909.4 %all-reduce.4.cloned.1.call-start = ((), (), s32[]{:S(2)}) async-start(), calls=%async_computation.4 | async-start | bytes 1048576 | tf_op jit(solution)/shard_map/psum | solution.py:145
  946.1 197.2 %copy-start.4 = (bf16[1,1024,128]{2,1,0:T(8,128)(2,1)S(1)}, bf16[1,1024,128]{2,1,0:T(8,128)(2,1)}, u32[]{:S(2)}) copy-start(bf16[1,1024,128]{2,1,0:T(8,128)(2,1)} %param.27) | copy-start | bytes 786436
  1140.1 3.2 copy-start.1
  1143.3 2.4 copy-start.5
  1158.1 7.3 copy-start.8
  1158.1 189.8 %all-to-all-start.1 = ((bf16[64,1,64,1024]{3,2,1,0:T(8,128)(2,1)}), bf16[64,1,64,1024]{3,2,1,0:T(8,128)(2,1)}, u32[]{:S(2)}, u32[]{:S(2)}) async-start(bf16[64,1,64,1024]{3,2,1,0:T(8,128)(2,1)} %convert_bitcast_fusion), calls=%async_computation.1 | async-start | bytes 16777216 | tf_op jit(solution)/shard_map/all_to_all | solution.py:180
  1164.8 266.9 %all-reduce.6.cloned.1.call-start = ((), (), s32[]{:S(2)}) async-start(), calls=%async_computation.5 | async-start | bytes 1048576 | tf_op jit(solution)/shard_map/psum | solution.py:191
  1363.4 6.9 copy-start.6
  1363.4 68.4 %copy-start.3 = (bf16[256,1024]{1,0:T(8,128)(2,1)S(1)}, bf16[256,1024]{1,0:T(8,128)(2,1)}, u32[]{:S(2)}) copy-start(bf16[256,1024]{1,0:T(8,128)(2,1)} %all-reduce.4.cloned.1.call-done) | copy-start | bytes 1572868
Sparse Core Ops, SparseCore 0:
  13.7 248.0 all-gather.2
  263.5 276.8 all-gather.4
  703.9 221.2 all-reduce.3
  1370.4 61.3 all-reduce.5
where the time goes:
time: 1450 us; the launch traced here: 1440 us
  waiting for transfers between devices  960 us (66%)
  blocking collectives  194 us (13%)
  local copies, waits for them, and re-layouts  134 us (9%)
  loops' own time  75.3 us (5%)
  matrix products  28.2 us (2%)
  other arithmetic  27.8 us (2%)
    all_gather x1, waiting for transfers between devices, per_device(): values_all = lax.all_gather(value_heads, 'seq', axis=0, tiled=True)  279 us
    all_gather x1, waiting for transfers between devices, per_device(): keys_all = lax.all_gather(key_rot, 'seq', axis=0, tiled=True)  224 us
    psum x1, waiting for transfers between devices, per_device(): lax.psum(partial_out.astype(jnp.bfloat16), 'tp').astype(jnp.float32)  213 us
    all_to_all x1, blocking collectives, per_device(): lax.all_to_all(outbound, 'seq', split_axis=0, concat_axis=0, tiled=True)  194 us
    all_to_all x1, waiting for transfers between devices, per_device(): lax.all_to_all(result, 'seq', split_axis=0, concat_axis=0, tiled=True)  182 us
    another operation x1, loops' own time, per_device(): lax.fori_loop(0, block_total, visit_block, start_state)  74.6 us
    psum x1, waiting for transfers between devices, per_device(): lax.psum(combined.astype(jnp.bfloat16), 'tp').astype(jnp.float32)  60.7 us
    dynamic_slice x64, local copies, waits for them, and re-layouts, visit_block(): key_segs = lax.dynamic_slice_in_dim(segment_ids, key_start, tokens)  48.9 us
  transfers between devices with their start and end apart: 5, of which 5 were waited for; matrix products, arithmetic and copies ran while one was open for 2% of the time, Pallas kernels for 0%

commit v1 on v0

--- a/solution.py
+++ b/solution.py
@@ -1,14 +1,17 @@
 import jax
 import jax.numpy as jnp
 from jax import lax
+from jax.sharding import Mesh
 from jax.sharding import PartitionSpec as P
 
 HEAD_DIM = 64
 EXPERTS = 32
-
+SEG_VALUES = 8
+KEY_CHUNK = 1024
 
 EPS = 1e-06
 SCORE_SCALE = 0.015625
+SUB_AXES = ("sy", "sz", "sx")
 
 
 def normalize(values, gain):
@@ -35,13 +38,6 @@
         ],
         axis=-1,
     )
-
-
-def segment_positions(segment_ids):
-    index_all = jnp.arange(segment_ids.shape[0], dtype=jnp.int32)
-    changed = jnp.concatenate([jnp.ones((1,), jnp.bool_), segment_ids[1:] != segment_ids[:-1]])
-    starts = lax.cummax(jnp.where(changed, index_all, 0), axis=0)
-    return index_all - starts
 
 
 def per_device(
@@ -61,9 +57,15 @@
 ):
     tokens = hidden.shape[0]
     model_width = hidden.shape[1]
-    first_row = lax.axis_index("seq") * tokens
-    positions = lax.dynamic_slice_in_dim(segment_positions(segment_ids), first_row, tokens)
+    total_tokens = segment_ids.shape[0]
+    first_row = lax.axis_index(SUB_AXES) * tokens
     own_segs = lax.dynamic_slice_in_dim(segment_ids, first_row, tokens)
+    seg_starts = jnp.sum(
+        (segment_ids[None, :] < jnp.arange(SEG_VALUES, dtype=jnp.int32)[:, None]).astype(jnp.int32),
+        axis=1,
+    )
+    query_index = first_row + jnp.arange(tokens, dtype=jnp.int32)
+    positions = query_index - seg_starts[own_segs]
     normed = normalize(hidden, norm_attn).astype(jnp.bfloat16)
     query_heads = w_query.shape[1] // HEAD_DIM
     kv_heads = w_key.shape[1] // HEAD_DIM
@@ -75,6 +77,7 @@
         rotary(queries, positions)
         .astype(jnp.bfloat16)
         .reshape(tokens, kv_heads, group_size, HEAD_DIM)
+        .transpose(1, 2, 0, 3)
     )
     key_raw = jnp.dot(normed, w_key, preferred_element_type=jnp.float32).reshape(
         tokens, kv_heads, HEAD_DIM
@@ -84,18 +87,29 @@
         [key_raw.reshape(tokens, kv_heads * HEAD_DIM).astype(jnp.bfloat16), value_proj], axis=1
     )
     key_rot = rotary(key_raw, positions).astype(jnp.bfloat16)
-    value_heads = value_proj.reshape(tokens, kv_heads, HEAD_DIM)
-    query_index = first_row + jnp.arange(tokens, dtype=jnp.int32)
+    kv_width = kv_heads * HEAD_DIM
+    joined = jnp.concatenate([key_rot.reshape(tokens, kv_width), value_proj], axis=1)
+    for axis_name in SUB_AXES[::-1]:
+        joined = lax.all_gather(joined, axis_name, axis=0, tiled=True)
+    keys_all = joined[:, :kv_width].reshape(total_tokens, kv_heads, HEAD_DIM).transpose(1, 0, 2)
+    values_all = joined[:, kv_width:].reshape(total_tokens, kv_heads, HEAD_DIM).transpose(1, 0, 2)
     last_query = first_row + tokens - 1
     lowest_seg = own_segs[0]
-
-    def attend(carried, key_rows, value_rows, key_start, key_segs):
+    chunk_ends = segment_ids[KEY_CHUNK - 1 :: KEY_CHUNK]
+    first_chunk = jnp.sum((chunk_ends < lowest_seg).astype(jnp.int32))
+    last_chunk = last_query // KEY_CHUNK
+
+    def visit_chunk(chunk, carried):
         running_max, weight_sum, accumulated = carried
+        key_start = chunk * KEY_CHUNK
+        key_rows = lax.dynamic_slice_in_dim(keys_all, key_start, KEY_CHUNK, axis=1)
+        value_rows = lax.dynamic_slice_in_dim(values_all, key_start, KEY_CHUNK, axis=1)
+        key_segs = lax.dynamic_slice_in_dim(segment_ids, key_start, KEY_CHUNK)
         scores = (
-            jnp.einsum("tkgd,skd->kgts", queries, key_rows, preferred_element_type=jnp.float32)
+            jnp.einsum("kgtd,ksd->kgts", queries, key_rows, preferred_element_type=jnp.float32)
             * SCORE_SCALE
         )
-        key_index = key_start + jnp.arange(key_rows.shape[0], dtype=jnp.int32)
+        key_index = key_start + jnp.arange(KEY_CHUNK, dtype=jnp.int32)
         allowed = (own_segs[:, None] == key_segs[None, :]) & (
             query_index[:, None] >= key_index[None, :]
         )
@@ -105,7 +119,7 @@
         factor = jnp.exp(running_max - new_max)
         weight_sum = weight_sum * factor + jnp.sum(weights, axis=-1)
         accumulated = accumulated * factor[..., None] + jnp.einsum(
-            "kgts,skd->kgtd",
+            "kgts,ksd->kgtd",
             weights.astype(jnp.bfloat16),
             value_rows,
             preferred_element_type=jnp.float32,
@@ -117,24 +131,9 @@
         jnp.zeros((kv_heads, group_size, tokens), jnp.float32),
         jnp.zeros((kv_heads, group_size, tokens, HEAD_DIM), jnp.float32),
     )
-    keys_all = lax.all_gather(key_rot, "seq", axis=0, tiled=True)
-    values_all = lax.all_gather(value_heads, "seq", axis=0, tiled=True)
-    block_total = keys_all.shape[0] // tokens
-
-    def visit_block(block_index, state_now):
-        key_start = block_index * tokens
-        key_rows = lax.dynamic_slice_in_dim(keys_all, block_index * tokens, tokens)
-        value_rows = lax.dynamic_slice_in_dim(values_all, block_index * tokens, tokens)
-        key_segs = lax.dynamic_slice_in_dim(segment_ids, key_start, tokens)
-        relevant = (key_start <= last_query) & (key_segs[tokens - 1] >= lowest_seg)
-        return lax.cond(
-            relevant,
-            lambda inner: attend(inner, key_rows, value_rows, key_start, key_segs),
-            lambda inner: inner,
-            state_now,
-        )
-
-    running_max, weight_sum, accumulated = lax.fori_loop(0, block_total, visit_block, start_state)
+    running_max, weight_sum, accumulated = lax.fori_loop(
+        first_chunk, last_chunk + 1, visit_chunk, start_state
+    )
     attended = (
         (accumulated / weight_sum[..., None])
         .transpose(2, 0, 1, 3)
@@ -147,7 +146,7 @@
     normed_moe = normalize(residual, norm_moe).astype(jnp.bfloat16)
     route_count = routes.shape[1]
     slots_dev = w_gate.shape[0]
-    seq_count = lax.axis_size("seq")
+    seq_count = lax.axis_size(SUB_AXES)
     slot_total = slots_dev * seq_count
     copies = slot_total // EXPERTS
     block_rows = tokens // copies
@@ -171,13 +170,13 @@
     )
     padded_rows = jnp.concatenate([normed_moe, jnp.zeros((1, normed_moe.shape[1]), jnp.bfloat16)])
     outbound = padded_rows[source].reshape(seq_count, slots_dev, capacity, normed_moe.shape[1])
-    arrived = lax.all_to_all(outbound, "seq", split_axis=0, concat_axis=0, tiled=True)
+    arrived = lax.all_to_all(outbound, SUB_AXES, split_axis=0, concat_axis=0, tiled=True)
     gate_val = jnp.einsum("jsrd,sdf->jsrf", arrived, w_gate, preferred_element_type=jnp.float32)
     up_val = jnp.einsum("jsrd,sdf->jsrf", arrived, w_up, preferred_element_type=jnp.float32)
     activated = (jax.nn.silu(gate_val) * up_val).astype(jnp.bfloat16)
     group_part = jnp.einsum("jsrf,sfd->jsrd", activated, w_down, preferred_element_type=jnp.float32)
     result = group_part.astype(jnp.bfloat16)
-    returned = lax.all_to_all(result, "seq", split_axis=0, concat_axis=0, tiled=True).reshape(
+    returned = lax.all_to_all(result, SUB_AXES, split_axis=0, concat_axis=0, tiled=True).reshape(
         slot_total * capacity, model_width
     )
     picked = returned[target]
@@ -194,24 +193,27 @@
 
 
 def solution(mesh):
+    seq_size, tp_size = mesh.devices.shape
+    side = round(seq_size ** (1 / 3))
+    sub_mesh = Mesh(mesh.devices.reshape(side, side, seq_size // side // side, tp_size), SUB_AXES + ("tp",))
     return jax.shard_map(
         per_device,
-        mesh=mesh,
+        mesh=sub_mesh,
         in_specs=(
-            P("seq", None),
+            P(SUB_AXES, None),
             P(),
-            P("seq", None),
-            P("seq", None),
+            P(SUB_AXES, None),
+            P(SUB_AXES, None),
             P(),
             P(),
             P(None, "tp"),
             P(None, "tp"),
             P(None, "tp"),
             P("tp", None),
-            P("seq", None, "tp"),
-            P("seq", None, "tp"),
-            P("seq", "tp", None),
+            P(SUB_AXES, None, "tp"),
+            P(SUB_AXES, None, "tp"),
+            P(SUB_AXES, "tp", None),
         ),
-        out_specs=(P("seq", None), P("seq", None, "tp")),
+        out_specs=(P(SUB_AXES, None), P(SUB_AXES, None, "tp")),
         check_vma=False,
     )

time: 1450 us -> 870 us (0.60)
  waiting for transfers between devices: 960 us -> 513 us
  local copies, waits for them, and re-layouts: 134 us -> 57.2 us
  loops' own time: 75.3 us -> 3.39 us
    all_gather x2, waiting for transfers between devices: 503 us -> 119 us  [per_device(): joined = lax.all_gather(joined, axis_name, axis=0, tiled=True)]
    another operation x65 -> x1, loops' own time: 75.3 us -> 3.39 us  [per_device(): lax.fori_loop(first_chunk, last_chunk + 1, visit_chunk, start_state)]
    psum x1, waiting for transfers between devices: 213 us -> 151 us  [per_device(): lax.psum(partial_out.astype(jnp.bfloat16), 'tp').astype(jnp.float32)]
    dynamic_slice x65 -> x1, local copies, waits for them, and re-layouts: 49.7 us -> 0.69 us  [visit_chunk(): key_segs = lax.dynamic_slice_in_dim(segment_ids, key_start, KEY_CHUNK)]
    slice x64 -> x4, local copies, waits for them, and re-layouts: 35.1 us -> 7.01 us  [the longest x1 5.79 us: per_device(): joined[:, kv_width:].reshape(total_tokens, kv_heads, HEAD_DIM)]
  transfers between devices with their start and end apart: 5 -> 5, of which waited for: 5 -> 5; matrix products, arithmetic and copies ran while one was open for 2% -> 4% of each run, Pallas kernels for 0% -> 0%
where the time goes in v1:
time: 870 us; the launch traced here: 866 us
  waiting for transfers between devices  513 us (59%)
  blocking collectives  207 us (24%)
  local copies, waits for them, and re-layouts  57.2 us (7%)
  other arithmetic  34.8 us (4%)
  matrix products  29.1 us (3%)
  between operations  14.2 us (2%)
    all_to_all x1, blocking collectives, per_device(): lax.all_to_all(outbound, SUB_AXES, split_axis=0, concat_axis=0, tiled=True)  194 us
    all_to_all x1, waiting for transfers between devices, per_device(): lax.all_to_all(result, SUB_AXES, split_axis=0, concat_axis=0, tiled=True)  182 us
    psum x1, waiting for transfers between devices, per_device(): lax.psum(partial_out.astype(jnp.bfloat16), 'tp').astype(jnp.float32)  151 us
    all_gather x2, waiting for transfers between devices, per_device(): joined = lax.all_gather(joined, axis_name, axis=0, tiled=True)  119 us
    psum x1, waiting for transfers between devices, per_device(): lax.psum(combined.astype(jnp.bfloat16), 'tp').astype(jnp.float32)  60.6 us
    gather x1, local copies, waits for them, and re-layouts, per_device(): padded_rows[source]  18.3 us
    another operation x5, other arithmetic  18.3 us
  transfers between devices with their start and end apart: 5, of which 5 were waited for; matrix products, arithmetic and copies ran while one was open for 4% of the time, Pallas kernels for 0%

profile of v1, /device:TPU:1, one launch (start us, length us, event | category | flops | bytes accessed | tf_op | source)
XLA Modules:
  0.0 866.0 jit_solution(6917786490866685563)
XLA Ops:
  7.2 0.0 all-gather.3.cloned.1.call-start
  7.3 1.1 convert_reduce_fusion
  8.4 0.7 fusion.68
  9.1 0.7 convert_element_type.101
  9.7 1.2 fusion.38
  11.0 1.5 fusion.65
  12.5 1.5 convolution_convert_fusion.1
  14.0 5.7 fusion.59
  19.8 0.2 multiply_cosine_fusion
  20.0 12.9 %all_gather.9 = bf16[1024,256]{0,1:T(8,128)(2,1)} all-gather(bf16[256,256]{0,1:T(8,128)(2,1)S(1)} %pad_maximum_fusion), channel_id=1, replica_groups=mesh['sy'=4,'sz'=4,'sx'=4,'tp'=4] {'sx'}, dimensions={0}, use_global_device_ids=true | all-gather | bytes 655360 | tf_op jit(solution)/shard_map/all_gather | solution.py:93
  32.9 0.0 all-gather.3.cloned.1.call-update
  33.0 0.0 all-gather.5.cloned.1.call-start
  33.0 54.5 %all-gather.3.cloned.1.call-done = bf16[4096,256]{0,1:T(8,128)(2,1)} async-done(((bf16[1024,256]{0,1:T(8,128)(2,1)}), bf16[4096,256]{0,1:T(8,128)(2,1)}) %all-gather.3.cloned.1.call-update) | async-done | bytes 2097168 | tf_op jit(solution)/shard_map/all_gather | solution.py:93
  87.5 0.0 all-gather.5.cloned.1.call-update
  87.6 0.0 all-reduce.4.cloned.1.call-start
  87.6 0.9 slice.30
  88.5 0.1 copy.49
  88.7 0.1 eq.42
  88.8 0.1 eq.38
  88.9 0.5 slice.31
  89.5 18.0 %reduce-window.6 = s32[2,32,8,128]{3,2,1,0:T(8,128)S(1)} reduce-window(s32[2,32,8,128]{3,2,1,0:T(8,128)S(1)} %fusion.53, s32[]{:T(128)} %constant.95.clone.1), window={size=1x1x1x128 pad=0_0x0_0x0_0x127_0}, to_apply=%region_9.10 | reduce-window | flops 8323072 | bytes 524292 | tf_op jit(solution)/shard_map/reduce-window
  107.5 0.1 slice.59
  107.6 0.2 copy.51
  107.8 0.1 copy.52
  107.9 0.1 broadcast_add_fusion
  108.1 0.1 fusion.52
  108.2 0.1 reshape.211
  108.3 0.1 copy.53
  108.4 0.1 copy.54
  108.5 0.1 reshape.212
  108.6 0.1 reshape.256
  108.8 1.4 fusion.60
  110.1 0.5 fusion.62
  110.6 64.3 %all-gather.5.cloned.1.call-done = bf16[16384,256]{0,1:T(8,128)(2,1)} async-done(((bf16[4096,256]{0,1:T(8,128)(2,1)}), bf16[16384,256]{0,1:T(8,128)(2,1)}) %all-gather.5.cloned.1.call-update) | async-done | bytes 8388624 | tf_op jit(solution)/shard_map/all_gather | solution.py:93
  174.9 5.8 fusion.67
  180.8 9.5 %while.15 = (s32[]{:T(128)}, f32[2,2,256]{2,1,0:T(2,128)S(1)}, f32[2,2,256]{2,1,0:T(2,128)S(1)}, f32[2,2,256,64]{2,3,1,0:T(8,128)S(1)}, s32[]{:T(128)}, /*index=...) while((s32[]{:T(128)}, f32[2,2,256]{2,1,0:T(2,128)S(1)}, ...), condition=%wide.region_6.7_spmd.clone, body=%wide.region_3.6_spmd.clone.sunk | while | flops 282987776 | bytes 14900431 | solution.py:134
  182.2 0.7 dynamic_slice.32
  182.9 0.3 compare_and_fusion.2
  183.2 1.8 fusion.85
  185.1 1.0 fusion.86
  186.1 2.1 fusion.87
  190.3 1.1 convolution_convert_fusion
  191.4 0.0 all-reduce.4.cloned.1.call-update
  191.5 8.1 scatter_custom_fusion
  199.5 151.2 %all-reduce.4.cloned.1.call-done = bf16[256,1024]{1,0:T(8,128)(2,1)} async-done(((bf16[256,1024]{1,0:T(8,128)(2,1)}), bf16[256,1024]{1,0:T(8,128)(2,1)}) %all-reduce.4.cloned.1.call-update) | async-done | bytes 524304 | tf_op jit(solution)/shard_map/psum | solution.py:144
  350.7 1.3 fusion.42
  352.0 1.2 fusion.44
  353.3 18.3 %gather_fusion = bf16[4096,1024]{1,0:T(8,128)(2,1)} fusion(bf16[257,1024]{1,0:T(8,128)(2,1)S(1)} %concatenate.24, s32[4096]{0:T(1024)S(1)} %fusion.54), kind=kCustom, calls=%fused_computation | custom fusion | bytes 16793600 | tf_op jit(solution)/shard_map/gather | solution.py:172
  371.6 194.0 %all_to_all.10 = bf16[64,1,64,1024]{3,2,1,0:T(8,128)(2,1)S(1)} all-to-all(bf16[64,1,64,1024]{3,2,1,0:T(8,128)(2,1)} %bitcast.162), channel_id=1, replica_groups=mesh['sy'=4,'sz'=4,'sx'=4,'tp'=4] {'sy','sz','sx'}, dimensions={0} | all-to-all | bytes 16777216 | tf_op jit(solution)/shard_map/all_to_all | solution.py:173
  565.6 3.2 copy-done.2
  568.9 2.4 fusion.23
  571.3 12.3 %convert_bitcast_fusion = bf16[64,1,64,1024]{3,2,1,0:T(8,128)(2,1)} fusion(bf16[64,1,64,1024]{3,2,1,0:T(8,128)(2,1)} %copy-done.2, f32[64,64,128]{2,1,0:T(8,128)S(1)} %fusion.23, bf16[1,128,1024]{2,1,0:T(8,128)(2,1)S(1)} %copy-done.6, bf16[1,1024,128]{2,1,0:T(8,128)(2,1)S(1)} %copy-done.7), kind=kOutput, calls=%fused_computation.31 | convolution fusion | flops 2154823680 | bytes 19398656 | tf_op jit(solution)/shard_map/jsrf,sfd->jsrd/dot_general | solution.py:177
  583.6 6.7 all-to-all-start.1
  590.4 0.3 all-reduce.6.cloned.1.call-start
  590.7 0.1 copy.57
  590.8 0.1 reshape.246
  590.9 0.1 copy.62
  591.1 182.5 %all-to-all-done.1 = bf16[64,1,64,1024]{3,2,1,0:T(8,128)(2,1)} async-done(((bf16[64,1,64,1024]{3,2,1,0:T(8,128)(2,1)}), bf16[64,1,64,1024]{3,2,1,0:T(8,128)(2,1)}, u32[]{:S(2)}, u32[]{:S(2)}) %all-to-all-start.1) | async-done | bytes 8388640 | tf_op jit(solution)/shard_map/all_to_all | solution.py:179
  773.5 15.5 %gather_fusion.1 = bf16[2048,1024]{1,0:T(8,128)(2,1)} fusion(bf16[4096,1024]{1,0:T(8,128)(2,1)} %bitcast.46, s32[2048]{0:T(1024)S(1)} %broadcast_clamp_fusion), kind=kCustom, calls=%fused_computation.1 | custom fusion | bytes 8396800 | tf_op jit(solution)/shard_map/gather | solution.py:182
  789.0 5.9 fusion.25
  794.9 1.0 copy.65
  795.9 0.8 copy.58
  796.7 60.6 %all-reduce.6.cloned.1.call-done = bf16[256,1024]{1,0:T(8,128)(2,1)} async-done(((bf16[256,1024]{1,0:T(8,128)(2,1)}), bf16[256,1024]{1,0:T(8,128)(2,1)}) %all-reduce.6.cloned.1.call-update) | async-done | bytes 524304 | tf_op jit(solution)/shard_map/psum | solution.py:190
  857.3 2.1 fusion.45
  (59 shorter events, 0.5 us)
Async XLA Ops:
  7.2 183.1 %copy-start = (bf16[256,1024]{1,0:T(8,128)(2,1)S(1)}, bf16[256,1024]{1,0:T(8,128)(2,1)}, u32[]{:S(2)}) copy-start(bf16[256,1024]{1,0:T(8,128)(2,1)} %param.24) | copy-start | bytes 1572868
  7.2 81.4 %copy-start.10 = (s32[256,8]{0,1:T(8,128)S(1)}, s32[256,8]{0,1:T(8,128)}, u32[]{:S(2)}) copy-start(s32[256,8]{0,1:T(8,128)} %param.17) | copy-start | bytes 24580
  7.2 82.2 %copy-start.12 = (bf16[1024]{0:T(1024)(128)(2,1)S(1)}, bf16[1024]{0:T(1024)(128)(2,1)}, u32[]{:S(2)}) copy-start(bf16[1024]{0:T(1024)(128)(2,1)} %param.20) | copy-start | bytes 6148
  7.2 80.3 %all-gather.3.cloned.1.call-start = ((), (), s32[]{:S(2)}) async-start(), calls=%async_computation.2 | async-start | bytes 2621440 | tf_op jit(solution)/shard_map/all_gather | solution.py:93
  14.0 73.6 %copy-start.8 = (bf16[256,128]{0,1:T(8,128)(2,1)}, bf16[256,128]{0,1:T(8,128)(2,1)S(1)}, u32[]{:S(2)}) copy-start(bf16[256,128]{0,1:T(8,128)(2,1)S(1)} %convolution_convert_fusion.1) | copy-start | bytes 196612
  19.7 90.4 %copy-start.3 = (bf16[256,1024]{1,0:T(8,128)(2,1)S(1)}, bf16[256,1024]{1,0:T(8,128)(2,1)}, u32[]{:S(2)}) copy-start(bf16[256,1024]{1,0:T(8,128)(2,1)} %param.15) | copy-start | bytes 1572868
  19.7 90.4 %copy-start.13 = (bf16[1024,256]{1,0:T(8,128)(2,1)S(1)}, bf16[1024,256]{1,0:T(8,128)(2,1)}, u32[]{:S(2)}) copy-start(bf16[1024,256]{1,0:T(8,128)(2,1)} %param.21) | copy-start | bytes 1572868
  33.0 142.0 %all-gather.5.cloned.1.call-start = ((), (), s32[]{:S(2)}) async-start(), calls=%async_computation.3 | async-start | bytes 10485760 | tf_op jit(solution)/shard_map/all_gather | solution.py:93
  87.6 263.2 %all-reduce.4.cloned.1.call-start = ((), (), s32[]{:S(2)}) async-start(), calls=%async_computation.4 | async-start | bytes 1048576 | tf_op jit(solution)/shard_map/psum | solution.py:144
  371.6 197.2 %copy-start.5 = (bf16[1,1024,128]{2,1,0:T(8,128)(2,1)S(1)}, bf16[1,1024,128]{2,1,0:T(8,128)(2,1)}, u32[]{:S(2)}) copy-start(bf16[1,1024,128]{2,1,0:T(8,128)(2,1)} %param.25) | copy-start | bytes 786436
  565.6 3.2 copy-start.2
  568.9 2.4 copy-start.6
  568.9 2.4 copy-start.7
  583.6 7.3 copy-start.11
  583.6 189.9 %all-to-all-start.1 = ((bf16[64,1,64,1024]{3,2,1,0:T(8,128)(2,1)}), bf16[64,1,64,1024]{3,2,1,0:T(8,128)(2,1)}, u32[]{:S(2)}, u32[]{:S(2)}) async-start(bf16[64,1,64,1024]{3,2,1,0:T(8,128)(2,1)} %convert_bitcast_fusion), calls=%async_computation.1 | async-start | bytes 16777216 | tf_op jit(solution)/shard_map/all_to_all | solution.py:179
  590.4 266.9 %all-reduce.6.cloned.1.call-start = ((), (), s32[]{:S(2)}) async-start(), calls=%async_computation.5 | async-start | bytes 1048576 | tf_op jit(solution)/shard_map/psum | solution.py:190
  773.5 85.9 %copy-start.1 = (bf16[256,1024]{1,0:T(8,128)(2,1)S(1)}, bf16[256,1024]{1,0:T(8,128)(2,1)}, u32[]{:S(2)}) copy-start(bf16[256,1024]{1,0:T(8,128)(2,1)} %param.24) | copy-start | bytes 1572868
  789.0 6.9 copy-start.9
  789.0 68.3 %copy-start.4 = (bf16[256,1024]{1,0:T(8,128)(2,1)S(1)}, bf16[256,1024]{1,0:T(8,128)(2,1)}, u32[]{:S(2)}) copy-start(bf16[256,1024]{1,0:T(8,128)(2,1)} %all-reduce.4.cloned.1.call-done) | copy-start | bytes 1572868
Sparse Core Ops, SparseCore 0:
  33.1 54.4 all-gather.2
  89.3 85.5 all-gather.4
  191.6 159.1 all-reduce.3
  796.0 61.2 all-reduce.5

commit v2 on v1

--- a/solution.py
+++ b/solution.py
@@ -12,6 +12,7 @@
 EPS = 1e-06
 SCORE_SCALE = 0.015625
 SUB_AXES = ("sy", "sz", "sx")
+TP_AXES = ("tz", "tc")
 
 
 def normalize(values, gain):
@@ -141,7 +142,7 @@
     )
     attended = attended.astype(jnp.bfloat16)
     partial_out = jnp.dot(attended, w_out, preferred_element_type=jnp.float32)
-    attn_mixed = lax.psum(partial_out.astype(jnp.bfloat16), "tp").astype(jnp.float32)
+    attn_mixed = lax.psum(partial_out.astype(jnp.bfloat16), TP_AXES).astype(jnp.float32)
     residual = (hidden.astype(jnp.float32) + attn_mixed).astype(jnp.bfloat16)
     normed_moe = normalize(residual, norm_moe).astype(jnp.bfloat16)
     route_count = routes.shape[1]
@@ -168,18 +169,33 @@
         .at[target.reshape(-1)]
         .set(token_ids.reshape(-1))
     )
+    half = capacity // 2
+    core = lax.axis_index("tc")
+    swap = [(0, 1), (1, 0)]
+    own_source = lax.dynamic_slice_in_dim(
+        source.reshape(seq_count, slots_dev, capacity), core * half, half, axis=2
+    )
     padded_rows = jnp.concatenate([normed_moe, jnp.zeros((1, normed_moe.shape[1]), jnp.bfloat16)])
-    outbound = padded_rows[source].reshape(seq_count, slots_dev, capacity, normed_moe.shape[1])
-    arrived = lax.all_to_all(outbound, SUB_AXES, split_axis=0, concat_axis=0, tiled=True)
+    outbound = padded_rows[own_source]
+    arrived_own = lax.all_to_all(outbound, SUB_AXES, split_axis=0, concat_axis=0, tiled=True)
+    arrived_other = lax.ppermute(arrived_own, "tc", swap)
+    arrived = jnp.concatenate([arrived_own, arrived_other], axis=2)
     gate_val = jnp.einsum("jsrd,sdf->jsrf", arrived, w_gate, preferred_element_type=jnp.float32)
     up_val = jnp.einsum("jsrd,sdf->jsrf", arrived, w_up, preferred_element_type=jnp.float32)
     activated = (jax.nn.silu(gate_val) * up_val).astype(jnp.bfloat16)
     group_part = jnp.einsum("jsrf,sfd->jsrd", activated, w_down, preferred_element_type=jnp.float32)
     result = group_part.astype(jnp.bfloat16)
-    returned = lax.all_to_all(result, SUB_AXES, split_axis=0, concat_axis=0, tiled=True).reshape(
-        slot_total * capacity, model_width
-    )
-    picked = returned[target]
+    sibling_part = lax.ppermute(result[:, :, half:], "tc", swap)
+    pair_sum = (result[:, :, :half].astype(jnp.float32) + sibling_part.astype(jnp.float32)).astype(
+        jnp.bfloat16
+    )
+    returned = lax.all_to_all(pair_sum, SUB_AXES, split_axis=0, concat_axis=0, tiled=True).reshape(
+        slot_total * half, model_width
+    )
+    returned = jnp.concatenate([returned, jnp.zeros((1, model_width), jnp.bfloat16)])
+    own_route = (slot_rank // half) == core
+    local_target = jnp.where(own_route, slot_of * half + slot_rank - core * half, slot_total * half)
+    picked = returned[local_target]
     combined = jnp.einsum(
         "tk,tkd->td",
         gates,
@@ -187,7 +203,7 @@
         preferred_element_type=jnp.float32,
         precision=lax.Precision.HIGHEST,
     )
-    expert_sum = lax.psum(combined.astype(jnp.bfloat16), "tp").astype(jnp.float32)
+    expert_sum = lax.psum(combined.astype(jnp.bfloat16), TP_AXES).astype(jnp.float32)
     hidden_out = (residual.astype(jnp.float32) + expert_sum).astype(jnp.bfloat16)
     return (hidden_out, kv_cache)
 
@@ -195,7 +211,9 @@
 def solution(mesh):
     seq_size, tp_size = mesh.devices.shape
     side = round(seq_size ** (1 / 3))
-    sub_mesh = Mesh(mesh.devices.reshape(side, side, seq_size // side // side, tp_size), SUB_AXES + ("tp",))
+    sub_mesh = Mesh(
+        mesh.devices.reshape(side, side, seq_size // side // side, tp_size // 2, 2), SUB_AXES + TP_AXES
+    )
     return jax.shard_map(
         per_device,
         mesh=sub_mesh,
@@ -206,14 +224,14 @@
             P(SUB_AXES, None),
             P(),
             P(),
-            P(None, "tp"),
-            P(None, "tp"),
-            P(None, "tp"),
-            P("tp", None),
-            P(SUB_AXES, None, "tp"),
-            P(SUB_AXES, None, "tp"),
-            P(SUB_AXES, "tp", None),
+            P(None, TP_AXES),
+            P(None, TP_AXES),
+            P(None, TP_AXES),
+            P(TP_AXES, None),
+            P(SUB_AXES, None, TP_AXES),
+            P(SUB_AXES, None, TP_AXES),
+            P(SUB_AXES, TP_AXES, None),
         ),
-        out_specs=(P(SUB_AXES, None), P(SUB_AXES, None, "tp")),
+        out_specs=(P(SUB_AXES, None), P(SUB_AXES, None, TP_AXES)),
         check_vma=False,
     )

time: 870 us -> 698 us (0.80)
  blocking collectives: 207 us -> 117 us
  waiting for transfers between devices: 513 us -> 429 us
    all_to_all x1, blocking collectives: 194 us -> 104 us  [per_device(): lax.all_to_all(outbound, SUB_AXES, split_axis=0, concat_axis=0, tiled=True)]
    all_to_all x1, waiting for transfers between devices: 182 us -> 92.9 us  [per_device(): lax.all_to_all(pair_sum, SUB_AXES, split_axis=0, concat_axis=0, tiled=True)]
    ppermute x0 -> x2, waiting for transfers between devices: none -> 13.6 us  [the longest x1 6.79 us: per_device(): sibling_part = lax.ppermute(result[:, :, half:], 'tc', swap)]
    gather x2, local copies, waits for them, and re-layouts: 33.8 us -> 23.4 us  [the longest x1 13.8 us: per_device(): picked = returned[local_target]]
  transfers between devices with their start and end apart: 5 -> 7, of which waited for: 5 -> 7; matrix products, arithmetic and copies ran while one was open for 4% -> 5% of each run, Pallas kernels for 0% -> 0%
where the time goes in v2:
time: 698 us; the launch traced here: 695 us
  waiting for transfers between devices  429 us (61%)
  blocking collectives  117 us (17%)
  local copies, waits for them, and re-layouts  53.1 us (8%)
  other arithmetic  39.2 us (6%)
  matrix products  30.6 us (4%)
  between operations  14.2 us (2%)
  starting transfers between devices  9.06 us (1%)
    psum x1, waiting for transfers between devices, per_device(): lax.psum(partial_out.astype(jnp.bfloat16), TP_AXES).astype(jnp.float32)  149 us
    all_gather x2, waiting for transfers between devices, per_device(): joined = lax.all_gather(joined, axis_name, axis=0, tiled=True)  119 us
    all_to_all x1, blocking collectives, per_device(): lax.all_to_all(outbound, SUB_AXES, split_axis=0, concat_axis=0, tiled=True)  104 us
    all_to_all x1, waiting for transfers between devices, per_device(): lax.all_to_all(pair_sum, SUB_AXES, split_axis=0, concat_axis=0, tiled=True)  92.9 us
    psum x1, waiting for transfers between devices, per_device(): lax.psum(combined.astype(jnp.bfloat16), TP_AXES).astype(jnp.float32)  54.7 us
    another operation x5, other arithmetic  18.3 us
  transfers between devices with their start and end apart: 7, of which 7 were waited for; matrix products, arithmetic and copies ran while one was open for 5% of the time, Pallas kernels for 0%

profile of v2, /device:TPU:1, one launch (start us, length us, event | category | flops | bytes accessed | tf_op | source)
XLA Modules:
  0.0 695.4 jit_solution(16472206100202499687)
XLA Ops:
  7.3 1.1 convert_reduce_fusion
  8.4 0.7 fusion.66
  9.0 0.7 convert_element_type.110
  9.7 1.2 fusion.31
  10.9 1.5 fusion.63
  12.5 1.5 convolution_convert_fusion.1
  14.0 5.9 fusion.54
  19.9 0.2 multiply_cosine_fusion
  20.1 12.8 %all_gather.9 = bf16[1024,256]{0,1:T(8,128)(2,1)} all-gather(bf16[256,256]{0,1:T(8,128)(2,1)S(1)} %pad_maximum_fusion), channel_id=1, replica_groups=mesh['sy'=4,'sz'=4,'sx'=4,'tz'=2,'tc'=2] {'sx'}, dimensions={0}, use_global_device_ids=true | all-gather | bytes 655360 | tf_op jit(solution)/shard_map/all_gather | solution.py:94
  33.0 54.5 %all-gather.3.cloned.1.call-done = bf16[4096,256]{0,1:T(8,128)(2,1)} async-done(((bf16[1024,256]{0,1:T(8,128)(2,1)}), bf16[4096,256]{0,1:T(8,128)(2,1)}) %all-gather.3.cloned.1.call-update) | async-done | bytes 2097168 | tf_op jit(solution)/shard_map/all_gather | solution.py:94
  87.6 0.9 slice.36
  88.5 0.1 copy.59
  88.7 0.1 eq.48
  88.8 0.1 eq.44
  88.9 0.5 slice.37
  89.4 18.0 %reduce-window.6 = s32[2,32,8,128]{3,2,1,0:T(8,128)S(1)} reduce-window(s32[2,32,8,128]{3,2,1,0:T(8,128)S(1)} %fusion.46, s32[]{:T(128)} %constant.112.clone.1), window={size=1x1x1x128 pad=0_0x0_0x0_0x127_0}, to_apply=%region_9.10 | reduce-window | flops 8323072 | bytes 524292 | tf_op jit(solution)/shard_map/reduce-window
  107.4 0.1 slice.67
  107.6 0.2 copy.61
  107.8 0.1 copy.62
  107.9 0.1 broadcast_add_fusion
  108.1 0.1 reshape.211
  108.4 0.1 copy.64
  108.5 0.1 reshape.212
  108.6 1.3 fusion.55
  109.9 0.5 fusion.60
  110.4 64.6 %all-gather.5.cloned.1.call-done = bf16[16384,256]{0,1:T(8,128)(2,1)} async-done(((bf16[4096,256]{0,1:T(8,128)(2,1)}), bf16[16384,256]{0,1:T(8,128)(2,1)}) %all-gather.5.cloned.1.call-update) | async-done | bytes 8388624 | tf_op jit(solution)/shard_map/all_gather | solution.py:94
  175.0 5.8 fusion.65
  180.8 9.2 %while.15 = (s32[]{:T(128)}, f32[2,2,256]{2,1,0:T(2,128)S(1)}, f32[2,2,256]{2,1,0:T(2,128)S(1)}, f32[2,2,256,64]{2,3,1,0:T(8,128)S(1)}, s32[]{:T(128)}, /*index=...) while((s32[]{:T(128)}, f32[2,2,256]{2,1,0:T(2,128)S(1)}, ...), condition=%wide.region_6.7_spmd.clone, body=%wide.region_3.6_spmd.clone.sunk | while | flops 282987776 | bytes 14900431 | solution.py:135
  182.2 0.7 dynamic_slice.37
  182.9 0.3 compare_and_fusion.2
  183.2 1.8 fusion.83
  185.0 1.0 fusion.84
  186.1 2.1 fusion.85
  190.1 1.1 convolution_convert_fusion
  191.3 0.1 reshape.256
  191.4 8.1 %scatter_custom_fusion = s32[4096]{0:T(1024)S(1)} fusion(s32[2048]{0:T(1024)S(1)} %bitcast.181, s32[2048]{0:T(1024)S(1)} %reshape.256, s32[]{:T(128)} %constant.111.clone.1), kind=kCustom, calls=%fused_computation.96 | custom fusion | bytes 16388 | tf_op jit(solution)/shard_map/scatter | solution.py:170
  199.6 0.1 compare_select_fusion
  199.7 148.8 %all-reduce.5.cloned.1.call-done = bf16[256,1024]{1,0:T(8,128)(2,1)} async-done(((bf16[256,1024]{1,0:T(8,128)(2,1)}), bf16[256,1024]{1,0:T(8,128)(2,1)}) %all-reduce.5.cloned.1.call-update) | async-done | bytes 524304 | tf_op jit(solution)/shard_map/psum | solution.py:145
  348.5 1.3 fusion.35
  349.8 1.3 fusion.37
  351.1 9.6 %gather_fusion = bf16[2048,1024]{1,0:T(8,128)(2,1)} fusion(bf16[257,1024]{1,0:T(8,128)(2,1)S(1)} %concatenate.30, s32[2048]{0:T(1024)S(1)} %broadcast_clamp_fusion.1), kind=kCustom, calls=%fused_computation | custom fusion | bytes 8396800 | tf_op jit(solution)/shard_map/gather | solution.py:179
  360.7 104.1 %all_to_all.10 = bf16[64,1,32,1024]{3,2,1,0:T(8,128)(2,1)S(1)} all-to-all(bf16[64,1,32,1024]{3,2,1,0:T(8,128)(2,1)} %bitcast.165), channel_id=1, replica_groups=mesh['sy'=4,'sz'=4,'sx'=4,'tz'=2,'tc'=2] {'sy','sz','sx'}, dimensions={0} | all-to-all | bytes 8388608 | tf_op jit(solution)/shard_map/all_to_all | solution.py:180
  464.8 2.4 collective-permute-start
  467.3 6.8 collective-permute-done
  474.1 2.0 copy-done.9
  476.0 3.6 fusion.22
  479.6 12.7 %convert_bitcast_fusion = bf16[64,1,64,1024]{3,2,0,1:T(8,128)(2,1)} fusion(bf16[64,1,32,1024]{3,2,0,1:T(8,128)(2,1)} %copy-done.9, bf16[64,1,32,1024]{3,2,0,1:T(8,128)(2,1)} %bitcast.168, f32[64,64,128]{2,1,0:T(8,128)} %fusion.22, bf16[1,128,1024]{2,1,0:T(8,128)(2,1)S(1)} %copy-done.12, bf16[1,1024,128]{2,1,0:T(8,128)(2,1)S(1)} %copy-done.13), kind=kOutput, calls=%fused_computation.29 | convolution fusion | flops 2171600896 | bytes 19398656 | tf_op jit(solution)/shard_map/jsrf,sfd->jsrd/dot_general | solution.py:186
  492.3 2.9 slice.70
  495.1 0.5 collective-permute-start.1
  495.6 6.8 collective-permute-done.1
  502.4 4.2 fusion.23
  506.6 5.8 all-to-all-start.1
  512.4 0.3 all-reduce.7.cloned.1.call-start
  512.7 0.1 copy.74
  512.8 0.1 reshape.246
  513.0 0.1 copy.79
  513.1 92.9 %all-to-all-done.1 = bf16[64,1,32,1024]{3,2,1,0:T(8,128)(2,1)} async-done(((bf16[64,1,32,1024]{3,2,1,0:T(8,128)(2,1)}), bf16[64,1,32,1024]{3,2,1,0:T(8,128)(2,1)}, u32[]{:S(2)}, u32[]{:S(2)}) %all-to-all-start.1) | async-done | bytes 4194336 | tf_op jit(solution)/shard_map/all_to_all | solution.py:192
  606.0 4.6 concatenate.32
  610.6 13.8 %gather_fusion.1 = bf16[2048,1024]{1,0:T(8,128)(2,1)} fusion(bf16[2049,1024]{1,0:T(8,128)(2,1)} %concatenate.32, s32[2048]{0:T(1024)S(1)} %broadcast_clamp_fusion), kind=kCustom, calls=%fused_computation.1 | custom fusion | bytes 8396800 | tf_op jit(solution)/shard_map/gather | solution.py:198
  624.4 5.9 fusion.24
  630.3 1.0 copy.82
  631.3 0.8 copy.75
  632.1 54.7 %all-reduce.7.cloned.1.call-done = bf16[256,1024]{1,0:T(8,128)(2,1)} async-done(((bf16[256,1024]{1,0:T(8,128)(2,1)}), bf16[256,1024]{1,0:T(8,128)(2,1)}) %all-reduce.7.cloned.1.call-update) | async-done | bytes 524304 | tf_op jit(solution)/shard_map/psum | solution.py:206
  686.7 2.1 fusion.38
  (69 shorter events, 1.0 us)
Async XLA Ops:
  7.2 182.9 %copy-start = (bf16[256,1024]{1,0:T(8,128)(2,1)S(1)}, bf16[256,1024]{1,0:T(8,128)(2,1)}, u32[]{:S(2)}) copy-start(bf16[256,1024]{1,0:T(8,128)(2,1)} %param.24) | copy-start | bytes 1572868
  7.2 81.3 %copy-start.6 = (s32[256,8]{0,1:T(8,128)S(1)}, s32[256,8]{0,1:T(8,128)}, u32[]{:S(2)}) copy-start(s32[256,8]{0,1:T(8,128)} %param.17) | copy-start | bytes 24580
  7.2 80.3 %all-gather.3.cloned.1.call-start = ((), (), s32[]{:S(2)}) async-start(), calls=%async_computation.2 | async-start | bytes 2621440 | tf_op jit(solution)/shard_map/all_gather | solution.py:94
  14.0 95.9 %copy-start.3 = (bf16[256,1024]{1,0:T(8,128)(2,1)S(1)}, bf16[256,1024]{1,0:T(8,128)(2,1)}, u32[]{:S(2)}) copy-start(bf16[256,1024]{1,0:T(8,128)(2,1)} %param.15) | copy-start | bytes 1572868
  14.0 95.9 %copy-start.10 = (bf16[1024,256]{1,0:T(8,128)(2,1)S(1)}, bf16[1024,256]{1,0:T(8,128)(2,1)}, u32[]{:S(2)}) copy-start(bf16[1024,256]{1,0:T(8,128)(2,1)} %param.21) | copy-start | bytes 1572868
  32.9 142.0 %all-gather.5.cloned.1.call-start = ((), (), s32[]{:S(2)}) async-start(), calls=%async_computation.3 | async-start | bytes 10485760 | tf_op jit(solution)/shard_map/all_gather | solution.py:94
  87.5 261.0 %all-reduce.5.cloned.1.call-start = ((), (), s32[]{:S(2)}) async-start(), calls=%async_computation.4 | async-start | bytes 1048576 | tf_op jit(solution)/shard_map/psum | solution.py:145
  180.8 10.4 %copy-start.8 = (bf16[1024]{0:T(1024)(128)(2,1)S(1)}, bf16[1024]{0:T(1024)(128)(2,1)}, u32[]{:S(2)}) copy-start(bf16[1024]{0:T(1024)(128)(2,1)} %param.20) | copy-start | bytes 6148
  360.7 115.3 %copy-start.11 = (bf16[1,1024,128]{2,1,0:T(8,128)(2,1)S(1)}, bf16[1,1024,128]{2,1,0:T(8,128)(2,1)}, u32[]{:S(2)}) copy-start(bf16[1,1024,128]{2,1,0:T(8,128)(2,1)} %param.25) | copy-start | bytes 786436
  464.8 9.2 %copy-start.5 = (bf16[64,1,32,1024]{3,2,1,0:T(8,128)(2,1)}, bf16[64,1,32,1024]{3,2,1,0:T(8,128)(2,1)S(1)}, u32[]{:S(2)}) copy-start(bf16[64,1,32,1024]{3,2,1,0:T(8,128)(2,1)S(1)} %all_to_all.10) | copy-start | bytes 12582916
  464.8 14.8 %copy-start.12 = (bf16[1,128,1024]{2,1,0:T(8,128)(2,1)S(1)}, bf16[1,128,1024]{2,1,0:T(8,128)(2,1)}, u32[]{:S(2)}) copy-start(bf16[1,128,1024]{2,1,0:T(8,128)(2,1)} %param.27) | copy-start | bytes 786436
  464.8 14.8 %copy-start.13 = (bf16[1,1024,128]{2,1,0:T(8,128)(2,1)S(1)}, bf16[1,1024,128]{2,1,0:T(8,128)(2,1)}, u32[]{:S(2)}) copy-start(bf16[1,1024,128]{2,1,0:T(8,128)(2,1)} %param.26) | copy-start | bytes 786436
  464.8 9.2 %collective-permute-start = (bf16[64,1,32,1024]{3,2,0,1:T(8,128)(2,1)S(1)}, bf16[64,1,32,1024]{3,2,0,1:T(8,128)(2,1)S(1)}, u32[]{:S(2)}, u32[]{:S(2)}) collective-permute-start(bf16[64,1,32,1024]{3,2,0,1:T(8,128)(2,1)S(1)} %bitcast.166), channel_id=1, source_target_pairs={{0,1},{1,0},{2,3},{3,2},{4,5},{5,4},{6,7},{7,6},{8,9},{9,8},{10,11... | collective-permute-start | bytes 12582920 | tf_op jit(solution)/shard_map/ppermute | solution.py:181
  474.0 2.0 copy-start.9
  492.2 10.1 %copy-start.2 = (bf16[64,1,64,1024]{3,2,0,1:T(8,128)(2,1)S(1)}, bf16[64,1,64,1024]{3,2,0,1:T(8,128)(2,1)}, u32[]{:S(2)}) copy-start(bf16[64,1,64,1024]{3,2,0,1:T(8,128)(2,1)} %convert_bitcast_fusion) | copy-start | bytes 25165828
  495.1 7.2 %collective-permute-start.1 = (bf16[64,1,32,1024]{3,2,0,1:T(8,128)(2,1)S(1)}, bf16[64,1,32,1024]{3,2,0,1:T(8,128)(2,1)S(1)}, u32[]{:S(2)}, u32[]{:S(2)}) collective-permute-start(bf16[64,1,32,1024]{3,2,0,1:T(8,128)(2,1)S(1)} %slice.70), channel_id=1, source_target_pairs={{0,1},{1,0},{2,3},{3,2},{4,5},{5,4},{6,7},{7,6},{8,9},{9,8},{10,11... | collective-permute-start | bytes 12582920 | tf_op jit(solution)/shard_map/ppermute | solution.py:188
  506.6 6.3 copy-start.7
  506.6 99.4 %all-to-all-start.1 = ((bf16[64,1,32,1024]{3,2,1,0:T(8,128)(2,1)}), bf16[64,1,32,1024]{3,2,1,0:T(8,128)(2,1)}, u32[]{:S(2)}, u32[]{:S(2)}) async-start(bf16[64,1,32,1024]{3,2,1,0:T(8,128)(2,1)} %fusion.23), calls=%async_computation.1 | async-start | bytes 8388608 | tf_op jit(solution)/shard_map/all_to_all | solution.py:192
  512.4 174.3 %all-reduce.7.cloned.1.call-start = ((), (), s32[]{:S(2)}) async-start(), calls=%async_computation.5 | async-start | bytes 1048576 | tf_op jit(solution)/shard_map/psum | solution.py:206
  610.6 78.3 %copy-start.1 = (bf16[256,1024]{1,0:T(8,128)(2,1)S(1)}, bf16[256,1024]{1,0:T(8,128)(2,1)}, u32[]{:S(2)}) copy-start(bf16[256,1024]{1,0:T(8,128)(2,1)} %param.24) | copy-start | bytes 1572868
  624.4 62.3 %copy-start.4 = (bf16[256,1024]{1,0:T(8,128)(2,1)S(1)}, bf16[256,1024]{1,0:T(8,128)(2,1)}, u32[]{:S(2)}) copy-start(bf16[256,1024]{1,0:T(8,128)(2,1)} %all-reduce.5.cloned.1.call-done) | copy-start | bytes 1572868
Sparse Core Ops, SparseCore 0:
  33.1 54.4 all-gather.2
  89.3 85.6 all-gather.4
  191.4 157.1 all-reduce.4
  631.4 55.3 all-reduce.6

commit v3 on v2

--- a/solution.py
+++ b/solution.py
@@ -39,6 +39,13 @@
         ],
         axis=-1,
     )
+
+
+def tp_sum(partial):
+    swap = [(0, 1), (1, 0)]
+    pair = partial.astype(jnp.float32) + lax.ppermute(partial, "tc", swap).astype(jnp.float32)
+    pair = pair.astype(jnp.bfloat16)
+    return pair.astype(jnp.float32) + lax.ppermute(pair, "tz", swap).astype(jnp.float32)
 
 
 def per_device(
@@ -142,7 +149,7 @@
     )
     attended = attended.astype(jnp.bfloat16)
     partial_out = jnp.dot(attended, w_out, preferred_element_type=jnp.float32)
-    attn_mixed = lax.psum(partial_out.astype(jnp.bfloat16), TP_AXES).astype(jnp.float32)
+    attn_mixed = tp_sum(partial_out.astype(jnp.bfloat16))
     residual = (hidden.astype(jnp.float32) + attn_mixed).astype(jnp.bfloat16)
     normed_moe = normalize(residual, norm_moe).astype(jnp.bfloat16)
     route_count = routes.shape[1]
@@ -203,7 +210,7 @@
         preferred_element_type=jnp.float32,
         precision=lax.Precision.HIGHEST,
     )
-    expert_sum = lax.psum(combined.astype(jnp.bfloat16), TP_AXES).astype(jnp.float32)
+    expert_sum = tp_sum(combined.astype(jnp.bfloat16))
     hidden_out = (residual.astype(jnp.float32) + expert_sum).astype(jnp.bfloat16)
     return (hidden_out, kv_cache)
 

time: 698 us -> 633 us (0.907)
  waiting for transfers between devices: 429 us -> 256 us
  blocking collectives: 117 us -> 216 us
  starting transfers between devices: 9.06 us -> 21.9 us
    psum x2 -> x0, waiting for transfers between devices: 203 us -> none  [the longest x1 149 us: per_device(): lax.psum(partial_out.astype(jnp.bfloat16), TP_AXES).astype(jnp.float32)]
    all_to_all x1, blocking collectives: 104 us -> 203 us  [per_device(): lax.all_to_all(outbound, SUB_AXES, split_axis=0, concat_axis=0, tiled=True)]
    ppermute x0 -> x4, waiting for transfers between devices: none -> 29.3 us  [the longest x2 27.1 us: tp_sum(): lax.ppermute(pair, 'tz', swap).astype(jnp.float32)]
    ppermute x0 -> x4, starting transfers between devices: none -> 12.7 us  [the longest x2 9.34 us: tp_sum(): lax.ppermute(pair, 'tz', swap).astype(jnp.float32)]
  transfers between devices with their start and end apart: 7 -> 9, of which waited for: 7 -> 9; matrix products, arithmetic and copies ran while one was open for 5% -> 5% of each run, Pallas kernels for 0% -> 0%
where the time goes in v3:
time: 633 us; the launch traced here: 630 us
  waiting for transfers between devices  256 us (40%)
  blocking collectives  216 us (34%)
  local copies, waits for them, and re-layouts  52.3 us (8%)
  other arithmetic  36.6 us (6%)
  matrix products  29.9 us (5%)
  starting transfers between devices  21.9 us (3%)
  between operations  14.5 us (2%)
    all_to_all x1, blocking collectives, per_device(): lax.all_to_all(outbound, SUB_AXES, split_axis=0, concat_axis=0, tiled=True)  203 us
    all_gather x2, waiting for transfers between devices, per_device(): joined = lax.all_gather(joined, axis_name, axis=0, tiled=True)  120 us
    all_to_all x1, waiting for transfers between devices, per_device(): lax.all_to_all(pair_sum, SUB_AXES, split_axis=0, concat_axis=0, tiled=True)  93 us
    ppermute x2, waiting for transfers between devices, tp_sum(): lax.ppermute(pair, 'tz', swap).astype(jnp.float32)  27.1 us
    another operation x5, other arithmetic  18.2 us
    gather x1, local copies, waits for them, and re-layouts, per_device(): picked = returned[local_target]  13.8 us
    all_gather x1, blocking collectives, per_device(): joined = lax.all_gather(joined, axis_name, axis=0, tiled=True)  12.8 us
  transfers between devices with their start and end apart: 9, of which 9 were waited for; matrix products, arithmetic and copies ran while one was open for 5% of the time, Pallas kernels for 0%

profile of v3, /device:TPU:1, one launch (start us, length us, event | category | flops | bytes accessed | tf_op | source)
XLA Modules:
  0.0 630.2 jit_solution(9800846350214259561)
XLA Ops:
  7.3 1.1 convert_reduce_fusion
  8.4 0.7 fusion.67
  9.0 0.7 convert_element_type.134
  9.7 1.2 fusion.31
  11.0 1.6 fusion.63
  12.6 1.5 convolution_convert_fusion.1
  14.1 5.8 fusion.54
  19.8 0.2 multiply_cosine_fusion
  20.1 12.8 %all_gather.9 = bf16[1024,256]{0,1:T(8,128)(2,1)} all-gather(bf16[256,256]{0,1:T(8,128)(2,1)S(1)} %pad_maximum_fusion), channel_id=1, replica_groups=mesh['sy'=4,'sz'=4,'sx'=4,'tz'=2,'tc'=2] {'sx'}, dimensions={0}, use_global_device_ids=true | all-gather | bytes 655360 | tf_op jit(solution)/shard_map/all_gather | solution.py:101
  32.9 54.5 %all-gather.3.cloned.1.call-done = bf16[4096,256]{0,1:T(8,128)(2,1)} async-done(((bf16[1024,256]{0,1:T(8,128)(2,1)}), bf16[4096,256]{0,1:T(8,128)(2,1)}) %all-gather.3.cloned.1.call-update) | async-done | bytes 2097168 | tf_op jit(solution)/shard_map/all_gather | solution.py:101
  87.5 0.9 slice.36
  88.4 0.5 slice.37
  88.9 0.1 copy.59
  89.2 18.0 %reduce-window.6 = s32[2,32,8,128]{3,2,1,0:T(8,128)S(1)} reduce-window(s32[2,32,8,128]{3,2,1,0:T(8,128)S(1)} %fusion.46, s32[]{:T(128)} %constant.112.clone.1), window={size=1x1x1x128 pad=0_0x0_0x0_0x127_0}, to_apply=%region_8.9 | reduce-window | flops 8323072 | bytes 524292 | tf_op jit(solution)/shard_map/reduce-window
  107.2 0.1 slice.67
  107.4 0.2 copy.61
  107.7 1.3 fusion.55
  108.9 0.5 fusion.60
  109.5 65.4 %all-gather.5.cloned.1.call-done = bf16[16384,256]{0,1:T(8,128)(2,1)} async-done(((bf16[4096,256]{0,1:T(8,128)(2,1)}), bf16[16384,256]{0,1:T(8,128)(2,1)}) %all-gather.5.cloned.1.call-update) | async-done | bytes 8388624 | tf_op jit(solution)/shard_map/all_gather | solution.py:101
  174.9 5.8 fusion.66
  180.7 9.2 %while.15 = (s32[]{:T(128)}, f32[2,2,256]{2,1,0:T(2,128)S(1)}, f32[2,2,256]{2,1,0:T(2,128)S(1)}, f32[2,2,256,64]{2,3,1,0:T(8,128)S(1)}, s32[]{:T(128)}, /*index=...) while((s32[]{:T(128)}, f32[2,2,256]{2,1,0:T(2,128)S(1)}, ...), condition=%wide.region_6.7_spmd.clone, body=%wide.region_3.6_spmd.clone.sunk | while | flops 282987776 | bytes 14900431 | solution.py:142
  182.0 0.7 dynamic_slice.37
  182.7 0.3 compare_and_fusion.2
  183.1 1.8 fusion.84
  184.9 1.0 fusion.85
  186.0 2.2 fusion.86
  190.0 0.3 convolution_convert_fusion
  190.4 0.9 collective-permute-start
  191.3 0.1 broadcast_add_fusion
  191.9 0.1 copy.64
  192.0 0.1 reshape.212
  192.1 0.7 collective-permute-done
  192.8 0.2 add_convert_fusion.2
  193.0 5.6 collective-permute-start.1
  198.7 8.1 %scatter_custom_fusion = s32[4096]{0:T(1024)S(1)} fusion(s32[2048]{0:T(1024)S(1)} %bitcast.183, s32[2048]{0:T(1024)S(1)} %reshape.256, s32[]{:T(128)} %constant.111.clone.1), kind=kCustom, calls=%fused_computation.98 | custom fusion | bytes 16388 | tf_op jit(solution)/shard_map/scatter | solution.py:177
  207.0 3.3 collective-permute-done.1
  210.3 0.3 fusion.35
  210.7 0.2 fusion.37
  210.9 9.6 %gather_fusion = bf16[2048,1024]{1,0:T(8,128)(2,1)} fusion(bf16[257,1024]{1,0:T(8,128)(2,1)S(1)} %concatenate.30, s32[2048]{0:T(1024)S(1)} %broadcast_clamp_fusion.1), kind=kCustom, calls=%fused_computation | custom fusion | bytes 8396800 | tf_op jit(solution)/shard_map/gather | solution.py:186
  220.5 203.3 %all_to_all.10 = bf16[64,1,32,1024]{3,2,1,0:T(8,128)(2,1)S(1)} all-to-all(bf16[64,1,32,1024]{3,2,1,0:T(8,128)(2,1)} %bitcast.167), channel_id=1, replica_groups=mesh['sy'=4,'sz'=4,'sx'=4,'tz'=2,'tc'=2] {'sy','sz','sx'}, dimensions={0} | all-to-all | bytes 8388608 | tf_op jit(solution)/shard_map/all_to_all | solution.py:187
  423.8 2.7 collective-permute-start.2
  426.5 6.8 %collective-permute-done.2 = bf16[64,1,32,1024]{3,2,0,1:T(8,128)(2,1)S(1)} collective-permute-done((bf16[64,1,32,1024]{3,2,0,1:T(8,128)(2,1)S(1)}, bf16[64,1,32,1024]{3,2,0,1:T(8,128)(2,1)S(1)}, u32[]{:S(2)}, u32[]{:S(2)}) %collective-permute-start.2) | collective-permute-done | bytes 4194336 | tf_op jit(solution)/shard_map/ppermute | solution.py:188
  433.3 2.0 copy-done.8
  435.3 3.6 fusion.22
  438.8 12.7 %convert_bitcast_fusion = bf16[64,1,64,1024]{3,2,0,1:T(8,128)(2,1)} fusion(bf16[64,1,32,1024]{3,2,0,1:T(8,128)(2,1)} %copy-done.8, bf16[64,1,32,1024]{3,2,0,1:T(8,128)(2,1)} %bitcast.170, f32[64,64,128]{2,1,0:T(8,128)} %fusion.22, bf16[1,128,1024]{2,1,0:T(8,128)(2,1)S(1)} %copy-done.11, bf16[1,1024,128]{2,1,0:T(8,128)(2,1)S(1)} %copy-done.12), kind=kOutput, calls=%fused_computation.29 | convolution fusion | flops 2171600896 | bytes 19398656 | tf_op jit(solution)/shard_map/jsrf,sfd->jsrd/dot_general | solution.py:193
  451.5 2.9 slice.70
  454.4 0.5 collective-permute-start.3
  454.9 6.8 %collective-permute-done.3 = bf16[64,1,32,1024]{3,2,0,1:T(8,128)(2,1)S(1)} collective-permute-done((bf16[64,1,32,1024]{3,2,0,1:T(8,128)(2,1)S(1)}, bf16[64,1,32,1024]{3,2,0,1:T(8,128)(2,1)S(1)}, u32[]{:S(2)}, u32[]{:S(2)}) %collective-permute-start.3) | collective-permute-done | bytes 4194336 | tf_op jit(solution)/shard_map/ppermute | solution.py:195
  461.6 4.3 fusion.23
  465.9 6.0 all-to-all-start.1
  471.9 0.1 copy.74
  472.2 0.1 copy.79
  472.3 93.0 %all-to-all-done.1 = bf16[64,1,32,1024]{3,2,1,0:T(8,128)(2,1)} async-done(((bf16[64,1,32,1024]{3,2,1,0:T(8,128)(2,1)}), bf16[64,1,32,1024]{3,2,1,0:T(8,128)(2,1)}, u32[]{:S(2)}, u32[]{:S(2)}) %all-to-all-start.1) | async-done | bytes 4194336 | tf_op jit(solution)/shard_map/all_to_all | solution.py:199
  565.3 4.6 concatenate.32
  569.9 13.8 %gather_fusion.1 = bf16[2048,1024]{1,0:T(8,128)(2,1)} fusion(bf16[2049,1024]{1,0:T(8,128)(2,1)} %concatenate.32, s32[2048]{0:T(1024)S(1)} %broadcast_clamp_fusion), kind=kCustom, calls=%fused_computation.1 | custom fusion | bytes 8396800 | tf_op jit(solution)/shard_map/gather | solution.py:205
  583.6 5.8 fusion.24
  589.5 0.2 copy.84
  589.7 2.4 collective-permute-start.4
  592.1 1.5 collective-permute-done.4
  593.6 0.3 add_convert_fusion.1
  594.0 3.8 collective-permute-start.5
  597.8 0.8 copy.75
  598.5 23.8 %collective-permute-done.5 = bf16[256,1024]{1,0:T(8,128)(2,1)S(1)} collective-permute-done((bf16[256,1024]{1,0:T(8,128)(2,1)S(1)}, bf16[256,1024]{1,0:T(8,128)(2,1)S(1)}, u32[]{:S(2)}, u32[]{:S(2)}) %collective-permute-start.5) | collective-permute-done | bytes 524320 | tf_op jit(solution)/shard_map/ppermute | solution.py:48
  622.3 1.1 fusion.38
  (71 shorter events, 1.6 us)
Async XLA Ops:
  7.2 182.9 %copy-start = (bf16[256,1024]{1,0:T(8,128)(2,1)S(1)}, bf16[256,1024]{1,0:T(8,128)(2,1)}, u32[]{:S(2)}) copy-start(bf16[256,1024]{1,0:T(8,128)(2,1)} %param.24) | copy-start | bytes 1572868
  7.2 81.8 %copy-start.5 = (s32[256,8]{0,1:T(8,128)S(1)}, s32[256,8]{0,1:T(8,128)}, u32[]{:S(2)}) copy-start(s32[256,8]{0,1:T(8,128)} %param.17) | copy-start | bytes 24580
  7.2 80.3 %all-gather.3.cloned.1.call-start = ((), (), s32[]{:S(2)}) async-start(), calls=%async_computation.2 | async-start | bytes 2621440 | tf_op jit(solution)/shard_map/all_gather | solution.py:101
  10.9 98.0 %copy-start.4 = (bf16[256,1024]{1,0:T(8,128)(2,1)S(1)}, bf16[256,1024]{1,0:T(8,128)(2,1)}, u32[]{:S(2)}) copy-start(bf16[256,1024]{1,0:T(8,128)(2,1)} %param.15) | copy-start | bytes 1572868
  10.9 98.0 %copy-start.9 = (bf16[1024,256]{1,0:T(8,128)(2,1)S(1)}, bf16[1024,256]{1,0:T(8,128)(2,1)}, u32[]{:S(2)}) copy-start(bf16[1024,256]{1,0:T(8,128)(2,1)} %param.21) | copy-start | bytes 1572868
  32.9 142.0 %all-gather.5.cloned.1.call-start = ((), (), s32[]{:S(2)}) async-start(), calls=%async_computation.3 | async-start | bytes 10485760 | tf_op jit(solution)/shard_map/all_gather | solution.py:101
  190.0 8.6 %copy-start.7 = (bf16[1024]{0:T(1024)(128)(2,1)S(1)}, bf16[1024]{0:T(1024)(128)(2,1)}, u32[]{:S(2)}) copy-start(bf16[1024]{0:T(1024)(128)(2,1)} %param.20) | copy-start | bytes 6148
  190.4 2.5 collective-permute-start
  193.0 17.3 %collective-permute-start.1 = (bf16[256,1024]{1,0:T(8,128)(2,1)S(1)}, bf16[256,1024]{1,0:T(8,128)(2,1)S(1)}, u32[]{:S(2)}, u32[]{:S(2)}) collective-permute-start(bf16[256,1024]{1,0:T(8,128)(2,1)S(1)} %add_convert_fusion.2), channel_id=1, source_target_pairs={{0,2},{2,0},{1,3},{3,1},{4,6},{6,4},{5,7},{7,5},{8,10},{10,8},{9,1... | collective-permute-start | bytes 1572872 | tf_op jit(solution)/shard_map/ppermute | solution.py:48
  220.5 214.7 %copy-start.10 = (bf16[1,1024,128]{2,1,0:T(8,128)(2,1)S(1)}, bf16[1,1024,128]{2,1,0:T(8,128)(2,1)}, u32[]{:S(2)}) copy-start(bf16[1,1024,128]{2,1,0:T(8,128)(2,1)} %param.25) | copy-start | bytes 786436
  423.8 9.5 %copy-start.3 = (bf16[64,1,32,1024]{3,2,1,0:T(8,128)(2,1)}, bf16[64,1,32,1024]{3,2,1,0:T(8,128)(2,1)S(1)}, u32[]{:S(2)}) copy-start(bf16[64,1,32,1024]{3,2,1,0:T(8,128)(2,1)S(1)} %all_to_all.10) | copy-start | bytes 12582916
  423.8 15.0 %copy-start.11 = (bf16[1,128,1024]{2,1,0:T(8,128)(2,1)S(1)}, bf16[1,128,1024]{2,1,0:T(8,128)(2,1)}, u32[]{:S(2)}) copy-start(bf16[1,128,1024]{2,1,0:T(8,128)(2,1)} %param.27) | copy-start | bytes 786436
  423.8 15.0 %copy-start.12 = (bf16[1,1024,128]{2,1,0:T(8,128)(2,1)S(1)}, bf16[1,1024,128]{2,1,0:T(8,128)(2,1)}, u32[]{:S(2)}) copy-start(bf16[1,1024,128]{2,1,0:T(8,128)(2,1)} %param.26) | copy-start | bytes 786436
  423.8 9.5 %collective-permute-start.2 = (bf16[64,1,32,1024]{3,2,0,1:T(8,128)(2,1)S(1)}, bf16[64,1,32,1024]{3,2,0,1:T(8,128)(2,1)S(1)}, u32[]{:S(2)}, u32[]{:S(2)}) collective-permute-start(bf16[64,1,32,1024]{3,2,0,1:T(8,128)(2,1)S(1)} %bitcast.168), channel_id=1, source_target_pairs={{0,1},{1,0},{2,3},{3,2},{4,5},{5,4},{6,7},{7,6},{8,9},{9,8},{10,11... | collective-permute-start | bytes 12582920 | tf_op jit(solution)/shard_map/ppermute | solution.py:188
  433.3 2.0 copy-start.8
  451.5 10.1 %copy-start.2 = (bf16[64,1,64,1024]{3,2,0,1:T(8,128)(2,1)S(1)}, bf16[64,1,64,1024]{3,2,0,1:T(8,128)(2,1)}, u32[]{:S(2)}) copy-start(bf16[64,1,64,1024]{3,2,0,1:T(8,128)(2,1)} %convert_bitcast_fusion) | copy-start | bytes 25165828
  454.4 7.2 %collective-permute-start.3 = (bf16[64,1,32,1024]{3,2,0,1:T(8,128)(2,1)S(1)}, bf16[64,1,32,1024]{3,2,0,1:T(8,128)(2,1)S(1)}, u32[]{:S(2)}, u32[]{:S(2)}) collective-permute-start(bf16[64,1,32,1024]{3,2,0,1:T(8,128)(2,1)S(1)} %slice.70), channel_id=1, source_target_pairs={{0,1},{1,0},{2,3},{3,2},{4,5},{5,4},{6,7},{7,6},{8,9},{9,8},{10,11... | collective-permute-start | bytes 12582920 | tf_op jit(solution)/shard_map/ppermute | solution.py:195
  465.9 6.3 copy-start.6
  465.9 99.4 %all-to-all-start.1 = ((bf16[64,1,32,1024]{3,2,1,0:T(8,128)(2,1)}), bf16[64,1,32,1024]{3,2,1,0:T(8,128)(2,1)}, u32[]{:S(2)}, u32[]{:S(2)}) async-start(bf16[64,1,32,1024]{3,2,1,0:T(8,128)(2,1)} %fusion.23), calls=%async_computation.1 | async-start | bytes 8388608 | tf_op jit(solution)/shard_map/all_to_all | solution.py:199
  583.6 39.8 %copy-start.1 = (bf16[256,1024]{1,0:T(8,128)(2,1)S(1)}, bf16[256,1024]{1,0:T(8,128)(2,1)}, u32[]{:S(2)}) copy-start(bf16[256,1024]{1,0:T(8,128)(2,1)} %param.24) | copy-start | bytes 1572868
  589.7 4.0 collective-permute-start.4
  594.0 28.4 %collective-permute-start.5 = (bf16[256,1024]{1,0:T(8,128)(2,1)S(1)}, bf16[256,1024]{1,0:T(8,128)(2,1)S(1)}, u32[]{:S(2)}, u32[]{:S(2)}) collective-permute-start(bf16[256,1024]{1,0:T(8,128)(2,1)S(1)} %add_convert_fusion.1), channel_id=1, source_target_pairs={{0,2},{2,0},{1,3},{3,1},{4,6},{6,4},{5,7},{7,5},{8,10},{10,8},{9,1... | collective-permute-start | bytes 1572872 | tf_op jit(solution)/shard_map/ppermute | solution.py:48
Sparse Core Ops, SparseCore 0:
  33.0 54.4 all-gather.2
  89.3 85.5 all-gather.4

commit v4 on v3

--- a/solution.py
+++ b/solution.py
@@ -1,6 +1,8 @@
 import jax
 import jax.numpy as jnp
 from jax import lax
+from jax.experimental import pallas as pl
+from jax.experimental.pallas import tpu as pltpu
 from jax.sharding import Mesh
 from jax.sharding import PartitionSpec as P
 
@@ -39,6 +41,108 @@
         ],
         axis=-1,
     )
+
+
+def attention_kernel(bounds_ref, q_ref, k_ref, v_ref, kseg_ref, qseg_ref, qidx_ref, o_ref, m_sc, l_sc, acc_sc):
+    step = pl.program_id(0)
+    kv_heads, group_size = q_ref.shape[0], q_ref.shape[1]
+
+    @pl.when(step == 0)
+    def _():
+        m_sc[...] = jnp.full(m_sc.shape, -1e30, jnp.float32)
+        l_sc[...] = jnp.zeros(l_sc.shape, jnp.float32)
+        acc_sc[...] = jnp.zeros(acc_sc.shape, jnp.float32)
+
+    chunk = bounds_ref[0] + step
+
+    @pl.when(chunk <= bounds_ref[1])
+    def _():
+        key_index = chunk * KEY_CHUNK + lax.broadcasted_iota(jnp.int32, (1, KEY_CHUNK), 1)
+        allowed = (qseg_ref[...] == kseg_ref[0]) & (qidx_ref[...] >= key_index)
+        for head in range(kv_heads):
+            key_rows = k_ref[head]
+            value_rows = v_ref[head]
+            for member in range(group_size):
+                slot = head * group_size + member
+                scores = (
+                    lax.dot_general(
+                        q_ref[head, member],
+                        key_rows,
+                        (((1,), (1,)), ((), ())),
+                        preferred_element_type=jnp.float32,
+                    )
+                    * SCORE_SCALE
+                )
+                masked = jnp.where(allowed, scores, -1e30)
+                running_max = m_sc[slot]
+                new_max = jnp.maximum(running_max, jnp.max(masked, axis=-1, keepdims=True))
+                weights = jnp.where(allowed, jnp.exp(masked - new_max), 0.0)
+                factor = jnp.exp(running_max - new_max)
+                l_sc[slot] = l_sc[slot] * factor + jnp.sum(weights, axis=-1, keepdims=True)
+                acc_sc[slot] = acc_sc[slot] * factor + jnp.dot(
+                    weights.astype(jnp.bfloat16), value_rows, preferred_element_type=jnp.float32
+                )
+                m_sc[slot] = new_max
+
+    @pl.when(step == pl.num_programs(0) - 1)
+    def _():
+        o_ref[...] = acc_sc[...] / l_sc[...]
+
+
+def chunk_attention(queries, keys_all, values_all, segment_ids, own_segs, query_index, first_chunk, last_chunk):
+    kv_heads, group_size, tokens, head_dim = queries.shape
+    total = keys_all.shape[1]
+    chunks = total // KEY_CHUNK
+    bounds = jnp.stack([first_chunk, last_chunk]).astype(jnp.int32)
+
+    def chunk_map(step, bounds_ref):
+        return (0, jnp.minimum(bounds_ref[0] + step, bounds_ref[1]), 0)
+
+    def seg_map(step, bounds_ref):
+        return (jnp.minimum(bounds_ref[0] + step, bounds_ref[1]), 0, 0)
+
+    def whole(step, bounds_ref):
+        return (0, 0, 0, 0)
+
+    def whole2(step, bounds_ref):
+        return (0, 0)
+
+    def whole3(step, bounds_ref):
+        return (0, 0, 0)
+
+    spec = pltpu.PrefetchScalarGridSpec(
+        num_scalar_prefetch=1,
+        grid=(chunks,),
+        in_specs=[
+            pl.BlockSpec((kv_heads, group_size, tokens, head_dim), whole),
+            pl.BlockSpec((kv_heads, KEY_CHUNK, head_dim), chunk_map),
+            pl.BlockSpec((kv_heads, KEY_CHUNK, head_dim), chunk_map),
+            pl.BlockSpec((1, 1, KEY_CHUNK), seg_map),
+            pl.BlockSpec((tokens, 1), whole2),
+            pl.BlockSpec((tokens, 1), whole2),
+        ],
+        out_specs=pl.BlockSpec((kv_heads * group_size, tokens, head_dim), whole3),
+        scratch_shapes=[
+            pltpu.VMEM((kv_heads * group_size, tokens, 1), jnp.float32),
+            pltpu.VMEM((kv_heads * group_size, tokens, 1), jnp.float32),
+            pltpu.VMEM((kv_heads * group_size, tokens, head_dim), jnp.float32),
+        ],
+    )
+    out = pl.pallas_call(
+        attention_kernel,
+        grid_spec=spec,
+        out_shape=jax.ShapeDtypeStruct((kv_heads * group_size, tokens, head_dim), jnp.float32),
+        compiler_params=pltpu.CompilerParams(dimension_semantics=("arbitrary",)),
+    )(
+        bounds,
+        queries,
+        keys_all,
+        values_all,
+        segment_ids.reshape(chunks, 1, KEY_CHUNK),
+        own_segs.reshape(tokens, 1),
+        query_index.reshape(tokens, 1),
+    )
+    return out.reshape(kv_heads, group_size, tokens, head_dim)
 
 
 def tp_sum(partial):
@@ -107,44 +211,11 @@
     first_chunk = jnp.sum((chunk_ends < lowest_seg).astype(jnp.int32))
     last_chunk = last_query // KEY_CHUNK
 
-    def visit_chunk(chunk, carried):
-        running_max, weight_sum, accumulated = carried
-        key_start = chunk * KEY_CHUNK
-        key_rows = lax.dynamic_slice_in_dim(keys_all, key_start, KEY_CHUNK, axis=1)
-        value_rows = lax.dynamic_slice_in_dim(values_all, key_start, KEY_CHUNK, axis=1)
-        key_segs = lax.dynamic_slice_in_dim(segment_ids, key_start, KEY_CHUNK)
-        scores = (
-            jnp.einsum("kgtd,ksd->kgts", queries, key_rows, preferred_element_type=jnp.float32)
-            * SCORE_SCALE
-        )
-        key_index = key_start + jnp.arange(KEY_CHUNK, dtype=jnp.int32)
-        allowed = (own_segs[:, None] == key_segs[None, :]) & (
-            query_index[:, None] >= key_index[None, :]
-        )
-        masked = jnp.where(allowed, scores, -1e30)
-        new_max = jnp.maximum(running_max, jnp.max(masked, axis=-1))
-        weights = jnp.where(allowed, jnp.exp(masked - new_max[..., None]), 0.0)
-        factor = jnp.exp(running_max - new_max)
-        weight_sum = weight_sum * factor + jnp.sum(weights, axis=-1)
-        accumulated = accumulated * factor[..., None] + jnp.einsum(
-            "kgts,ksd->kgtd",
-            weights.astype(jnp.bfloat16),
-            value_rows,
-            preferred_element_type=jnp.float32,
-        )
-        return (new_max, weight_sum, accumulated)
-
-    start_state = (
-        jnp.full((kv_heads, group_size, tokens), -1e30, jnp.float32),
-        jnp.zeros((kv_heads, group_size, tokens), jnp.float32),
-        jnp.zeros((kv_heads, group_size, tokens, HEAD_DIM), jnp.float32),
-    )
-    running_max, weight_sum, accumulated = lax.fori_loop(
-        first_chunk, last_chunk + 1, visit_chunk, start_state
+    attended = chunk_attention(
+        queries, keys_all, values_all, segment_ids, own_segs, query_index, first_chunk, last_chunk
     )
     attended = (
-        (accumulated / weight_sum[..., None])
-        .transpose(2, 0, 1, 3)
+        attended.transpose(2, 0, 1, 3)
         .reshape(tokens, query_heads * HEAD_DIM)
     )
     attended = attended.astype(jnp.bfloat16)

time: 633 us -> 590 us (0.932)
  blocking collectives: 216 us -> 162 us
  local copies, waits for them, and re-layouts: 52.3 us -> 70 us
  Pallas kernels: 0 us -> 7.51 us
    all_to_all x1, blocking collectives: 203 us -> 149 us  [per_device(): lax.all_to_all(outbound, SUB_AXES, split_axis=0, concat_axis=0, tiled=True)]
    reshape x0 -> x3, local copies, waits for them, and re-layouts: none -> 17.6 us  [the longest x1 8.45 us: per_device(): joined[:, kv_width:].reshape(total_tokens, kv_heads, HEAD_DIM)]
    pallas_call x0 -> x1, Pallas kernels: none -> 7.51 us  [chunk_attention(): pl.pallas_call(attention_kernel, grid_spec=spec, out_shape=jax.ShapeDtype...]
    another operation x5 -> x6, other arithmetic: 18.2 us -> 19.6 us
  transfers between devices with their start and end apart: 9 -> 9, of which waited for: 9 -> 9; matrix products, arithmetic and copies ran while one was open for 5% -> 6% of each run, Pallas kernels for 0% -> 0%
where the time goes in v4:
time: 590 us
  waiting for transfers between devices  253 us (43%)
  blocking collectives  162 us (27%)
  local copies, waits for them, and re-layouts  70 us (12%)
  other arithmetic  39.1 us (7%)
  matrix products  25.8 us (4%)
  starting transfers between devices  18.8 us (3%)
  between operations  14.5 us (2%)
  Pallas kernels  7.51 us (1%)
    all_to_all x1, blocking collectives, per_device(): lax.all_to_all(outbound, SUB_AXES, split_axis=0, concat_axis=0, tiled=True)  149 us
    all_gather x2, waiting for transfers between devices, per_device(): joined = lax.all_gather(joined, axis_name, axis=0, tiled=True)  116 us
    all_to_all x1, waiting for transfers between devices, per_device(): lax.all_to_all(pair_sum, SUB_AXES, split_axis=0, concat_axis=0, tiled=True)  93 us
    ppermute x2, waiting for transfers between devices, tp_sum(): lax.ppermute(pair, 'tz', swap).astype(jnp.float32)  28.6 us
    another operation x5, other arithmetic  18.3 us
    gather x1, local copies, waits for them, and re-layouts, per_device(): picked = returned[local_target]  13.8 us
    all_gather x1, blocking collectives, per_device(): joined = lax.all_gather(joined, axis_name, axis=0, tiled=True)  12.8 us
    dot_general x1, matrix products, per_device(): jnp.einsum('jsrf,sfd->jsrd', activated, w_down, preferred_element_type=jn...  12.7 us
  transfers between devices with their start and end apart: 9, of which 9 were waited for; matrix products, arithmetic and copies ran while one was open for 6% of the time, Pallas kernels for 0%

profile of v4, /device:TPU:1, one launch (start us, length us, event | category | flops | bytes accessed | tf_op | source)
XLA Modules:
  0.0 590.4 jit_solution(8901154409163354196)
XLA Ops:
  7.3 1.2 convert_reduce_fusion
  8.5 0.7 fusion.47
  9.2 0.7 convert_element_type.134
  9.8 1.2 fusion.10
  11.1 1.5 fusion.40
  12.6 1.5 convolution_convert_fusion.1
  14.1 5.7 fusion.33
  19.8 0.2 multiply_cosine_fusion
  20.1 12.8 %all_gather.9 = bf16[1024,256]{0,1:T(8,128)(2,1)} all-gather(bf16[256,256]{0,1:T(8,128)(2,1)S(1)} %pad_maximum_fusion), channel_id=1, replica_groups=mesh['sy'=4,'sz'=4,'sx'=4,'tz'=2,'tc'=2] {'sx'}, dimensions={0}, use_global_device_ids=true | all-gather | bytes 655360 | tf_op jit(solution)/shard_map/all_gather | solution.py:205
  32.9 54.5 %all-gather.3.cloned.1.call-done = bf16[4096,256]{0,1:T(8,128)(2,1)} async-done(((bf16[1024,256]{0,1:T(8,128)(2,1)}), bf16[4096,256]{0,1:T(8,128)(2,1)}) %all-gather.3.cloned.1.call-update) | async-done | bytes 2097168 | tf_op jit(solution)/shard_map/all_gather | solution.py:205
  87.7 0.9 slice.36
  88.7 0.4 fusion.42
  89.1 0.2 copy.109
  89.3 0.2 copy.110
  89.5 0.5 slice.37
  90.1 0.8 copy.88.qseg_ref
  91.1 18.0 %reduce-window.6 = s32[2,32,8,128]{3,2,1,0:T(8,128)S(1)} reduce-window(s32[2,32,8,128]{3,2,1,0:T(8,128)S(1)} %fusion.25, s32[]{:T(128)} %constant.93.clone.1), window={size=1x1x1x128 pad=0_0x0_0x0_0x127_0}, to_apply=%region_4.5 | reduce-window | flops 8323072 | bytes 524292 | tf_op jit(solution)/shard_map/reduce-window
  109.3 0.2 copy.92
  109.6 1.3 fusion.34
  110.9 1.2 pad_add_fusion.bounds_ref
  112.1 0.7 iota_add_fusion.qidx_ref
  112.7 0.1 subtract_convert_fusion
  112.9 0.8 maximum_bitcast_fusion.9.q_ref
  113.7 61.2 %all-gather.5.cloned.1.call-done = bf16[16384,256]{0,1:T(8,128)(2,1)} async-done(((bf16[4096,256]{0,1:T(8,128)(2,1)}), bf16[16384,256]{0,1:T(8,128)(2,1)}) %all-gather.5.cloned.1.call-update) | async-done | bytes 8388624 | tf_op jit(solution)/shard_map/all_gather | solution.py:205
  174.9 5.8 fusion.45
  180.8 8.4 %copy.86 = bf16[16384,2,64]{2,0,1:T(8,128)(2,1)} copy(bf16[16384,2,64]{0,2,1:T(8,128)(2,1)} %bitcast.135) | data formatting | bytes 8388608 | tf_op jit(solution)/shard_map/reshape | solution.py:206
  189.1 8.5 %copy.87 = bf16[16384,2,64]{2,0,1:T(8,128)(2,1)} copy(bf16[16384,2,64]{0,2,1:T(8,128)(2,1)} %bitcast.134) | data formatting | bytes 8388608 | tf_op jit(solution)/shard_map/reshape | solution.py:207
  197.6 7.5 %shard_map.140 = f32[4,256,64]{2,1,0:T(8,128)} custom-call(s32[2]{0:T(128)} %pad_add_fusion.bounds_ref, bf16[2,2,256,64]{3,2,1,0:T(8,128)(2,1)} %maximum_bitcast_fusion.9.q_ref, bf16[2,16384,64]{2,1,0:T(8,128)(2,1)} %bitcast.132, bf16[2,16384,64]{2,1,0:T(8,128)(2,1)} %bitcast.133, s32[16,1,1024]{2,1,0:T(1,128)} %bitcast.146, s32[256,1]{1,0:T(8,128)} %copy.88.qseg_ref, ...), custom_call_target="tpu_custom_call" | custom-call | tf_op jit(solution)/shard_map/pallas_call | solution.py:131
  205.1 1.1 convert_element_type.140
  206.2 0.1 copy.89
  206.4 0.3 convolution_convert_fusion
  206.7 0.9 collective-permute-start
  207.6 0.1 broadcast_add_fusion
  208.4 0.7 collective-permute-done
  209.1 0.2 add_convert_fusion.2
  209.3 5.5 collective-permute-start.1
  215.0 8.1 %scatter_custom_fusion = s32[4096]{0:T(1024)S(1)} fusion(s32[2048]{0:T(1024)S(1)} %bitcast.152, s32[2048]{0:T(1024)S(1)} %reshape.262, s32[]{:T(128)} %constant.92.clone.1), kind=kCustom, calls=%fused_computation.74 | custom fusion | bytes 16388 | tf_op jit(solution)/shard_map/scatter | solution.py:248
  223.3 3.3 collective-permute-done.1
  226.6 0.3 fusion.14
  227.0 0.2 fusion.16
  227.2 9.6 %gather_fusion = bf16[2048,1024]{1,0:T(8,128)(2,1)} fusion(bf16[257,1024]{1,0:T(8,128)(2,1)S(1)} %concatenate.30, s32[2048]{0:T(1024)S(1)} %broadcast_clamp_fusion.1), kind=kCustom, calls=%fused_computation | custom fusion | bytes 8396800 | tf_op jit(solution)/shard_map/gather | solution.py:257
  236.9 148.8 %all_to_all.10 = bf16[64,1,32,1024]{3,2,1,0:T(8,128)(2,1)S(1)} all-to-all(bf16[64,1,32,1024]{3,2,1,0:T(8,128)(2,1)} %bitcast.136), channel_id=1, replica_groups=mesh['sy'=4,'sz'=4,'sx'=4,'tz'=2,'tc'=2] {'sy','sz','sx'}, dimensions={0} | all-to-all | bytes 8388608 | tf_op jit(solution)/shard_map/all_to_all | solution.py:258
  385.7 2.4 collective-permute-start.2
  388.1 6.8 %collective-permute-done.2 = bf16[64,1,32,1024]{3,2,0,1:T(8,128)(2,1)S(1)} collective-permute-done((bf16[64,1,32,1024]{3,2,0,1:T(8,128)(2,1)S(1)}, bf16[64,1,32,1024]{3,2,0,1:T(8,128)(2,1)S(1)}, u32[]{:S(2)}, u32[]{:S(2)}) %collective-permute-start.2) | collective-permute-done | bytes 4194336 | tf_op jit(solution)/shard_map/ppermute | solution.py:259
  394.9 2.0 copy-done.8
  396.8 3.6 fusion.1
  400.4 12.7 %convert_bitcast_fusion = bf16[64,1,64,1024]{3,2,0,1:T(8,128)(2,1)} fusion(bf16[64,1,32,1024]{3,2,0,1:T(8,128)(2,1)} %copy-done.8, bf16[64,1,32,1024]{3,2,0,1:T(8,128)(2,1)} %bitcast.139, f32[64,64,128]{2,1,0:T(8,128)} %fusion.1, bf16[1,128,1024]{2,1,0:T(8,128)(2,1)S(1)} %copy-done.11, bf16[1,1024,128]{2,1,0:T(8,128)(2,1)S(1)} %copy-done.12), kind=kOutput, calls=%fused_computation.5 | convolution fusion | flops 2171600896 | bytes 19398656 | tf_op jit(solution)/shard_map/jsrf,sfd->jsrd/dot_general | solution.py:264
  413.1 2.9 slice.70
  415.9 0.5 collective-permute-start.3
  416.4 6.8 %collective-permute-done.3 = bf16[64,1,32,1024]{3,2,0,1:T(8,128)(2,1)S(1)} collective-permute-done((bf16[64,1,32,1024]{3,2,0,1:T(8,128)(2,1)S(1)}, bf16[64,1,32,1024]{3,2,0,1:T(8,128)(2,1)S(1)}, u32[]{:S(2)}, u32[]{:S(2)}) %collective-permute-start.3) | collective-permute-done | bytes 4194336 | tf_op jit(solution)/shard_map/ppermute | solution.py:266
  423.2 4.3 fusion.2
  427.5 6.0 %all-to-all-start.1 = ((bf16[64,1,32,1024]{3,2,1,0:T(8,128)(2,1)}), bf16[64,1,32,1024]{3,2,1,0:T(8,128)(2,1)}, u32[]{:S(2)}, u32[]{:S(2)}) async-start(bf16[64,1,32,1024]{3,2,1,0:T(8,128)(2,1)} %fusion.2), calls=%async_computation.1 | async-start | bytes 8388608 | tf_op jit(solution)/shard_map/all_to_all | solution.py:270
  433.9 93.0 %all-to-all-done.1 = bf16[64,1,32,1024]{3,2,1,0:T(8,128)(2,1)} async-done(((bf16[64,1,32,1024]{3,2,1,0:T(8,128)(2,1)}), bf16[64,1,32,1024]{3,2,1,0:T(8,128)(2,1)}, u32[]{:S(2)}, u32[]{:S(2)}) %all-to-all-start.1) | async-done | bytes 4194336 | tf_op jit(solution)/shard_map/all_to_all | solution.py:270
  526.8 4.6 concatenate.32
  531.4 13.8 %gather_fusion.1 = bf16[2048,1024]{1,0:T(8,128)(2,1)} fusion(bf16[2049,1024]{1,0:T(8,128)(2,1)} %concatenate.32, s32[2048]{0:T(1024)S(1)} %broadcast_clamp_fusion), kind=kCustom, calls=%fused_computation.1 | custom fusion | bytes 8396800 | tf_op jit(solution)/shard_map/gather | solution.py:276
  545.2 5.9 fusion.3
  551.0 0.2 copy.114
  551.2 2.4 collective-permute-start.4
  553.6 1.5 collective-permute-done.4
  555.2 0.3 add_convert_fusion.1
  555.5 0.9 collective-permute-start.5
  556.5 0.8 copy.106
  557.3 25.2 %collective-permute-done.5 = bf16[256,1024]{1,0:T(8,128)(2,1)S(1)} collective-permute-done((bf16[256,1024]{1,0:T(8,128)(2,1)S(1)}, bf16[256,1024]{1,0:T(8,128)(2,1)S(1)}, u32[]{:S(2)}, u32[]{:S(2)}) %collective-permute-start.5) | collective-permute-done | bytes 524320 | tf_op jit(solution)/shard_map/ppermute | solution.py:152
  582.5 1.1 fusion.17
  (69 shorter events, 2.4 us)
Async XLA Ops:
  7.2 199.2 %copy-start = (bf16[256,1024]{1,0:T(8,128)(2,1)S(1)}, bf16[256,1024]{1,0:T(8,128)(2,1)}, u32[]{:S(2)}) copy-start(bf16[256,1024]{1,0:T(8,128)(2,1)} %param.22) | copy-start | bytes 1572868
  7.2 81.5 %copy-start.4 = (bf16[256,1024]{1,0:T(8,128)(2,1)S(1)}, bf16[256,1024]{1,0:T(8,128)(2,1)}, u32[]{:S(2)}) copy-start(bf16[256,1024]{1,0:T(8,128)(2,1)} %param.13) | copy-start | bytes 1572868
  7.2 81.5 %copy-start.9 = (bf16[1024,256]{1,0:T(8,128)(2,1)S(1)}, bf16[1024,256]{1,0:T(8,128)(2,1)}, u32[]{:S(2)}) copy-start(bf16[1024,256]{1,0:T(8,128)(2,1)} %param.19) | copy-start | bytes 1572868
  7.2 80.3 %all-gather.3.cloned.1.call-start = ((), (), s32[]{:S(2)}) async-start(), calls=%async_computation.2 | async-start | bytes 2621440 | tf_op jit(solution)/shard_map/all_gather | solution.py:205
  14.1 76.8 %copy-start.5 = (s32[256,8]{0,1:T(8,128)S(1)}, s32[256,8]{0,1:T(8,128)}, u32[]{:S(2)}) copy-start(s32[256,8]{0,1:T(8,128)} %param.15) | copy-start | bytes 24580
  32.9 142.0 %all-gather.5.cloned.1.call-start = ((), (), s32[]{:S(2)}) async-start(), calls=%async_computation.3 | async-start | bytes 10485760 | tf_op jit(solution)/shard_map/all_gather | solution.py:205
  205.1 9.7 %copy-start.7 = (bf16[1024]{0:T(1024)(128)(2,1)S(1)}, bf16[1024]{0:T(1024)(128)(2,1)}, u32[]{:S(2)}) copy-start(bf16[1024]{0:T(1024)(128)(2,1)} %param.18) | copy-start | bytes 6148
  206.7 2.4 collective-permute-start
  209.3 17.3 %collective-permute-start.1 = (bf16[256,1024]{1,0:T(8,128)(2,1)S(1)}, bf16[256,1024]{1,0:T(8,128)(2,1)S(1)}, u32[]{:S(2)}, u32[]{:S(2)}) collective-permute-start(bf16[256,1024]{1,0:T(8,128)(2,1)S(1)} %add_convert_fusion.2), channel_id=1, source_target_pairs={{0,2},{2,0},{1,3},{3,1},{4,6},{6,4},{5,7},{7,5},{8,10},{10,8},{9,1... | collective-permute-start | bytes 1572872 | tf_op jit(solution)/shard_map/ppermute | solution.py:152
  236.9 160.0 %copy-start.10 = (bf16[1,1024,128]{2,1,0:T(8,128)(2,1)S(1)}, bf16[1,1024,128]{2,1,0:T(8,128)(2,1)}, u32[]{:S(2)}) copy-start(bf16[1,1024,128]{2,1,0:T(8,128)(2,1)} %param.23) | copy-start | bytes 786436
  385.7 9.2 %copy-start.3 = (bf16[64,1,32,1024]{3,2,1,0:T(8,128)(2,1)}, bf16[64,1,32,1024]{3,2,1,0:T(8,128)(2,1)S(1)}, u32[]{:S(2)}) copy-start(bf16[64,1,32,1024]{3,2,1,0:T(8,128)(2,1)S(1)} %all_to_all.10) | copy-start | bytes 12582916
  385.7 14.7 %copy-start.11 = (bf16[1,128,1024]{2,1,0:T(8,128)(2,1)S(1)}, bf16[1,128,1024]{2,1,0:T(8,128)(2,1)}, u32[]{:S(2)}) copy-start(bf16[1,128,1024]{2,1,0:T(8,128)(2,1)} %param.25) | copy-start | bytes 786436
  385.7 14.7 %copy-start.12 = (bf16[1,1024,128]{2,1,0:T(8,128)(2,1)S(1)}, bf16[1,1024,128]{2,1,0:T(8,128)(2,1)}, u32[]{:S(2)}) copy-start(bf16[1,1024,128]{2,1,0:T(8,128)(2,1)} %param.24) | copy-start | bytes 786436
  385.7 9.2 %collective-permute-start.2 = (bf16[64,1,32,1024]{3,2,0,1:T(8,128)(2,1)S(1)}, bf16[64,1,32,1024]{3,2,0,1:T(8,128)(2,1)S(1)}, u32[]{:S(2)}, u32[]{:S(2)}) collective-permute-start(bf16[64,1,32,1024]{3,2,0,1:T(8,128)(2,1)S(1)} %bitcast.137), channel_id=1, source_target_pairs={{0,1},{1,0},{2,3},{3,2},{4,5},{5,4},{6,7},{7,6},{8,9},{9,8},{10,11... | collective-permute-start | bytes 12582920 | tf_op jit(solution)/shard_map/ppermute | solution.py:259
  394.9 2.0 copy-start.8
  413.0 10.2 %copy-start.2 = (bf16[64,1,64,1024]{3,2,0,1:T(8,128)(2,1)S(1)}, bf16[64,1,64,1024]{3,2,0,1:T(8,128)(2,1)}, u32[]{:S(2)}) copy-start(bf16[64,1,64,1024]{3,2,0,1:T(8,128)(2,1)} %convert_bitcast_fusion) | copy-start | bytes 25165828
  415.9 7.3 %collective-permute-start.3 = (bf16[64,1,32,1024]{3,2,0,1:T(8,128)(2,1)S(1)}, bf16[64,1,32,1024]{3,2,0,1:T(8,128)(2,1)S(1)}, u32[]{:S(2)}, u32[]{:S(2)}) collective-permute-start(bf16[64,1,32,1024]{3,2,0,1:T(8,128)(2,1)S(1)} %slice.70), channel_id=1, source_target_pairs={{0,1},{1,0},{2,3},{3,2},{4,5},{5,4},{6,7},{7,6},{8,9},{9,8},{10,11... | collective-permute-start | bytes 12582920 | tf_op jit(solution)/shard_map/ppermute | solution.py:266
  427.5 6.3 %copy-start.6 = (f32[256,8]{0,1:T(8,128)S(1)}, f32[256,8]{0,1:T(8,128)}, u32[]{:S(2)}) copy-start(f32[256,8]{0,1:T(8,128)} %param.16) | copy-start | bytes 24580
  427.5 99.4 %all-to-all-start.1 = ((bf16[64,1,32,1024]{3,2,1,0:T(8,128)(2,1)}), bf16[64,1,32,1024]{3,2,1,0:T(8,128)(2,1)}, u32[]{:S(2)}, u32[]{:S(2)}) async-start(bf16[64,1,32,1024]{3,2,1,0:T(8,128)(2,1)} %fusion.2), calls=%async_computation.1 | async-start | bytes 8388608 | tf_op jit(solution)/shard_map/all_to_all | solution.py:270
  545.2 38.4 %copy-start.1 = (bf16[256,1024]{1,0:T(8,128)(2,1)S(1)}, bf16[256,1024]{1,0:T(8,128)(2,1)}, u32[]{:S(2)}) copy-start(bf16[256,1024]{1,0:T(8,128)(2,1)} %param.22) | copy-start | bytes 1572868
  551.2 4.0 collective-permute-start.4
  555.5 27.0 %collective-permute-start.5 = (bf16[256,1024]{1,0:T(8,128)(2,1)S(1)}, bf16[256,1024]{1,0:T(8,128)(2,1)S(1)}, u32[]{:S(2)}, u32[]{:S(2)}) collective-permute-start(bf16[256,1024]{1,0:T(8,128)(2,1)S(1)} %add_convert_fusion.1), channel_id=1, source_target_pairs={{0,2},{2,0},{1,3},{3,1},{4,6},{6,4},{5,7},{7,5},{8,10},{10,8},{9,1... | collective-permute-start | bytes 1572872 | tf_op jit(solution)/shard_map/ppermute | solution.py:152
Sparse Core Ops, SparseCore 0:
  33.0 54.4 all-gather.2
  89.3 85.6 all-gather.4

commit v5 on v4

--- a/solution.py
+++ b/solution.py
@@ -59,9 +59,9 @@
     def _():
         key_index = chunk * KEY_CHUNK + lax.broadcasted_iota(jnp.int32, (1, KEY_CHUNK), 1)
         allowed = (qseg_ref[...] == kseg_ref[0]) & (qidx_ref[...] >= key_index)
+        key_rows = k_ref[...]
+        value_rows = v_ref[...]
         for head in range(kv_heads):
-            key_rows = k_ref[head]
-            value_rows = v_ref[head]
             for member in range(group_size):
                 slot = head * group_size + member
                 scores = (
@@ -89,14 +89,22 @@
         o_ref[...] = acc_sc[...] / l_sc[...]
 
 
-def chunk_attention(queries, keys_all, values_all, segment_ids, own_segs, query_index, first_chunk, last_chunk):
+def chunk_attention(queries, joined, segment_ids, own_segs, query_index, first_chunk, last_chunk):
     kv_heads, group_size, tokens, head_dim = queries.shape
-    total = keys_all.shape[1]
+    total, both_width = joined.shape
+    kv_width = both_width // 2
     chunks = total // KEY_CHUNK
+    head_mask = jnp.eye(kv_heads, dtype=jnp.bool_)[:, None, None, :, None]
+    padded_queries = jnp.where(head_mask, queries[:, :, :, None, :], jnp.zeros((), queries.dtype)).reshape(
+        kv_heads, group_size, tokens, kv_width
+    )
     bounds = jnp.stack([first_chunk, last_chunk]).astype(jnp.int32)
 
-    def chunk_map(step, bounds_ref):
-        return (0, jnp.minimum(bounds_ref[0] + step, bounds_ref[1]), 0)
+    def key_map(step, bounds_ref):
+        return (jnp.minimum(bounds_ref[0] + step, bounds_ref[1]), 0)
+
+    def value_map(step, bounds_ref):
+        return (jnp.minimum(bounds_ref[0] + step, bounds_ref[1]), 1)
 
     def seg_map(step, bounds_ref):
         return (jnp.minimum(bounds_ref[0] + step, bounds_ref[1]), 0, 0)
@@ -114,35 +122,36 @@
         num_scalar_prefetch=1,
         grid=(chunks,),
         in_specs=[
-            pl.BlockSpec((kv_heads, group_size, tokens, head_dim), whole),
-            pl.BlockSpec((kv_heads, KEY_CHUNK, head_dim), chunk_map),
-            pl.BlockSpec((kv_heads, KEY_CHUNK, head_dim), chunk_map),
+            pl.BlockSpec((kv_heads, group_size, tokens, kv_width), whole),
+            pl.BlockSpec((KEY_CHUNK, kv_width), key_map),
+            pl.BlockSpec((KEY_CHUNK, kv_width), value_map),
             pl.BlockSpec((1, 1, KEY_CHUNK), seg_map),
             pl.BlockSpec((tokens, 1), whole2),
             pl.BlockSpec((tokens, 1), whole2),
         ],
-        out_specs=pl.BlockSpec((kv_heads * group_size, tokens, head_dim), whole3),
+        out_specs=pl.BlockSpec((kv_heads * group_size, tokens, kv_width), whole3),
         scratch_shapes=[
             pltpu.VMEM((kv_heads * group_size, tokens, 1), jnp.float32),
             pltpu.VMEM((kv_heads * group_size, tokens, 1), jnp.float32),
-            pltpu.VMEM((kv_heads * group_size, tokens, head_dim), jnp.float32),
+            pltpu.VMEM((kv_heads * group_size, tokens, kv_width), jnp.float32),
         ],
     )
     out = pl.pallas_call(
         attention_kernel,
         grid_spec=spec,
-        out_shape=jax.ShapeDtypeStruct((kv_heads * group_size, tokens, head_dim), jnp.float32),
+        out_shape=jax.ShapeDtypeStruct((kv_heads * group_size, tokens, kv_width), jnp.float32),
         compiler_params=pltpu.CompilerParams(dimension_semantics=("arbitrary",)),
     )(
         bounds,
-        queries,
-        keys_all,
-        values_all,
+        padded_queries,
+        joined,
+        joined,
         segment_ids.reshape(chunks, 1, KEY_CHUNK),
         own_segs.reshape(tokens, 1),
         query_index.reshape(tokens, 1),
     )
-    return out.reshape(kv_heads, group_size, tokens, head_dim)
+    out = out.reshape(kv_heads, group_size, tokens, kv_heads, head_dim)
+    return jnp.stack([out[head, :, :, head] for head in range(kv_heads)])
 
 
 def tp_sum(partial):
@@ -203,8 +212,6 @@
     joined = jnp.concatenate([key_rot.reshape(tokens, kv_width), value_proj], axis=1)
     for axis_name in SUB_AXES[::-1]:
         joined = lax.all_gather(joined, axis_name, axis=0, tiled=True)
-    keys_all = joined[:, :kv_width].reshape(total_tokens, kv_heads, HEAD_DIM).transpose(1, 0, 2)
-    values_all = joined[:, kv_width:].reshape(total_tokens, kv_heads, HEAD_DIM).transpose(1, 0, 2)
     last_query = first_row + tokens - 1
     lowest_seg = own_segs[0]
     chunk_ends = segment_ids[KEY_CHUNK - 1 :: KEY_CHUNK]
@@ -212,7 +219,7 @@
     last_chunk = last_query // KEY_CHUNK
 
     attended = chunk_attention(
-        queries, keys_all, values_all, segment_ids, own_segs, query_index, first_chunk, last_chunk
+        queries, joined, segment_ids, own_segs, query_index, first_chunk, last_chunk
     )
     attended = (
         attended.transpose(2, 0, 1, 3)
@@ -270,13 +277,13 @@
     returned = lax.all_to_all(pair_sum, SUB_AXES, split_axis=0, concat_axis=0, tiled=True).reshape(
         slot_total * half, model_width
     )
-    returned = jnp.concatenate([returned, jnp.zeros((1, model_width), jnp.bfloat16)])
     own_route = (slot_rank // half) == core
-    local_target = jnp.where(own_route, slot_of * half + slot_rank - core * half, slot_total * half)
+    local_target = jnp.where(own_route, slot_of * half + slot_rank - core * half, 0)
+    own_gates = jnp.where(own_route, gates, 0.0)
     picked = returned[local_target]
     combined = jnp.einsum(
         "tk,tkd->td",
-        gates,
+        own_gates,
         picked,
         preferred_element_type=jnp.float32,
         precision=lax.Precision.HIGHEST,

time: 590 us -> 559 us (0.947)
  local copies, waits for them, and re-layouts: 70 us -> 42.8 us
    reshape x2 -> x0, local copies, waits for them, and re-layouts: 16.8 us -> none  [the longest x1 8.45 us: per_device(): joined[:, kv_width:].reshape(total_tokens, kv_heads, HEAD_DIM)]
    another operation x5 -> x7, other arithmetic: 18.3 us -> 19.4 us
where the time goes in v5:
time: 559 us
  waiting for transfers between devices  253 us (45%)
  blocking collectives  158 us (28%)
  local copies, waits for them, and re-layouts  42.8 us (8%)
  other arithmetic  38.9 us (7%)
  matrix products  25.8 us (5%)
  starting transfers between devices  18.7 us (3%)
  between operations  14.5 us (3%)
  Pallas kernels  7.05 us (1%)
    all_to_all x1, blocking collectives, per_device(): lax.all_to_all(outbound, SUB_AXES, split_axis=0, concat_axis=0, tiled=True)  145 us
    all_gather x2, waiting for transfers between devices, per_device(): joined = lax.all_gather(joined, axis_name, axis=0, tiled=True)  116 us
    all_to_all x1, waiting for transfers between devices, per_device(): lax.all_to_all(pair_sum, SUB_AXES, split_axis=0, concat_axis=0, tiled=True)  92.9 us
    ppermute x2, waiting for transfers between devices, tp_sum(): lax.ppermute(pair, 'tz', swap).astype(jnp.float32)  28.4 us
    another operation x6, other arithmetic  19.3 us
    gather x1, local copies, waits for them, and re-layouts, per_device(): picked = returned[local_target]  13.7 us
    all_gather x1, blocking collectives, per_device(): joined = lax.all_gather(joined, axis_name, axis=0, tiled=True)  12.8 us
    dot_general x1, matrix products, per_device(): jnp.einsum('jsrf,sfd->jsrd', activated, w_down, preferred_element_type=jn...  12.6 us
  transfers between devices with their start and end apart: 9, of which 9 were waited for; matrix products, arithmetic and copies ran while one was open for 6% of the time, Pallas kernels for 0%

profile of v5, /device:TPU:1, one launch (start us, length us, event | category | flops | bytes accessed | tf_op | source)
XLA Modules:
  0.0 559.4 jit_solution(4516371094311132430)
XLA Ops:
  7.3 1.2 convert_reduce_fusion
  8.5 0.7 fusion.45
  9.1 0.7 convert_element_type.129
  9.8 1.2 fusion.10
  11.0 5.7 %fusion.33 = (f32[256]{0:T(256)S(1)}, s32[256]{0:T(256)S(1)}) fusion(s32[]{:T(128)} %bitcast.4, s32[]{:T(128)} %bitcast.5, s32[]{:T(128)} %bitcast.6, s32[]{:T(128)} %bitcast.7, s32[]{:T(128)} %bitcast.8, s32[]{:T(128)} %bitcast.9, s32[]{:T(128)} %bitcast.10, s32[]{:T(128)} %bitcast.11, s32[]{:T(128)S(6)} %mul.170, s32[16384]{0:T(1024)} %param.14, ...), kind=kLoop, calls=%fused_computation.100 | loop fusion | flops 5120 | bytes 3112 | tf_op jit(solution)/shard_map/convert_element_type | solution.py:32
  16.7 0.2 multiply_cosine_fusion
  16.9 1.5 fusion.40
  18.6 1.5 convolution_convert_fusion.1
  20.1 12.8 %all_gather.9 = bf16[1024,256]{1,0:T(8,128)(2,1)} all-gather(bf16[256,256]{1,0:T(8,128)(2,1)S(1)} %pad_maximum_fusion), channel_id=1, replica_groups=mesh['sy'=4,'sz'=4,'sx'=4,'tz'=2,'tc'=2] {'sx'}, dimensions={0}, use_global_device_ids=true | all-gather | bytes 655360 | tf_op jit(solution)/shard_map/all_gather | solution.py:214
  33.0 54.5 %all-gather.3.cloned.1.call-done = bf16[4096,256]{1,0:T(8,128)(2,1)} async-done(((bf16[1024,256]{1,0:T(8,128)(2,1)}), bf16[4096,256]{1,0:T(8,128)(2,1)}) %all-gather.3.cloned.1.call-update) | async-done | bytes 2097168 | tf_op jit(solution)/shard_map/all_gather | solution.py:214
  87.5 0.9 slice.38
  88.5 0.4 fusion.42
  89.0 0.2 copy.84
  89.4 0.5 slice.39
  89.9 0.8 copy.87.qseg_ref
  90.7 0.1 copy.89
  90.9 18.0 %reduce-window.6 = s32[2,32,8,128]{3,2,1,0:T(8,128)S(1)} reduce-window(s32[2,32,8,128]{3,2,1,0:T(8,128)S(1)} %fusion.25, s32[]{:T(128)} %constant.93.clone.1), window={size=1x1x1x128 pad=0_0x0_0x0_0x127_0}, to_apply=%region_3.4 | reduce-window | flops 8323072 | bytes 524292 | tf_op jit(solution)/shard_map/reduce-window
  109.0 0.1 slice.69
  109.1 0.2 copy.91
  109.4 1.2 fusion.34
  110.6 1.2 pad_add_fusion.bounds_ref
  111.8 0.7 iota_add_fusion.qidx_ref
  112.5 0.7 broadcast_select_fusion.q_ref
  113.2 61.8 %all-gather.5.cloned.1.call-done.k_ref.v_ref = bf16[16384,256]{1,0:T(8,128)(2,1)} async-done(((bf16[4096,256]{1,0:T(8,128)(2,1)}), bf16[16384,256]{1,0:T(8,128)(2,1)}) %all-gather.5.cloned.1.call-update) | async-done | bytes 8388624 | tf_op jit(solution)/shard_map/all_gather | solution.py:214
  175.0 7.1 %shard_map.140 = f32[4,256,128]{2,1,0:T(8,128)} custom-call(s32[2]{0:T(128)} %pad_add_fusion.bounds_ref, bf16[2,2,256,128]{3,2,1,0:T(8,128)(2,1)} %broadcast_select_fusion.q_ref, bf16[16384,256]{1,0:T(8,128)(2,1)} %all-gather.5.cloned.1.call-done.k_ref.v_ref, bf16[16384,256]{1,0:T(8,128)(2,1)} %all-gather.5.cloned.1.call-done.k_ref.v_ref, ...), custom_call_target="tpu_custom_call" | custom-call | tf_op jit(solution)/shard_map/pallas_call | solution.py:139
  182.1 1.1 convert.27
  183.2 0.1 copy.88
  183.4 0.3 convolution_convert_fusion
  183.7 0.8 collective-permute-start
  184.5 0.1 broadcast_add_fusion
  185.1 0.1 copy.98
  185.3 0.1 reshape.223
  185.4 0.7 collective-permute-done
  186.1 0.2 add_convert_fusion.2
  186.3 5.5 collective-permute-start.1
  191.9 8.1 %scatter_custom_fusion = s32[4096]{0:T(1024)S(1)} fusion(s32[2048]{0:T(1024)S(1)} %bitcast.152, s32[2048]{0:T(1024)S(1)} %reshape.268, s32[]{:T(128)} %constant.92.clone.1), kind=kCustom, calls=%fused_computation.77 | custom fusion | bytes 16388 | tf_op jit(solution)/shard_map/scatter | solution.py:255
  200.2 3.3 collective-permute-done.1
  203.6 0.3 fusion.14
  203.9 0.2 fusion.16
  204.2 9.7 %gather_fusion = bf16[2048,1024]{1,0:T(8,128)(2,1)} fusion(bf16[257,1024]{1,0:T(8,128)(2,1)S(1)} %concatenate.27, s32[2048]{0:T(1024)S(1)} %broadcast_clamp_fusion.1), kind=kCustom, calls=%fused_computation | custom fusion | bytes 8396800 | tf_op jit(solution)/shard_map/gather | solution.py:264
  213.9 145.5 %all_to_all.10 = bf16[64,1,32,1024]{3,2,1,0:T(8,128)(2,1)S(1)} all-to-all(bf16[64,1,32,1024]{3,2,1,0:T(8,128)(2,1)} %bitcast.135), channel_id=1, replica_groups=mesh['sy'=4,'sz'=4,'sx'=4,'tz'=2,'tc'=2] {'sy','sz','sx'}, dimensions={0} | all-to-all | bytes 8388608 | tf_op jit(solution)/shard_map/all_to_all | solution.py:265
  359.3 2.4 collective-permute-start.2
  361.7 6.8 %collective-permute-done.2 = bf16[64,1,32,1024]{3,2,0,1:T(8,128)(2,1)S(1)} collective-permute-done((bf16[64,1,32,1024]{3,2,0,1:T(8,128)(2,1)S(1)}, bf16[64,1,32,1024]{3,2,0,1:T(8,128)(2,1)S(1)}, u32[]{:S(2)}, u32[]{:S(2)}) %collective-permute-start.2) | collective-permute-done | bytes 4194336 | tf_op jit(solution)/shard_map/ppermute | solution.py:266
  368.5 2.0 copy-done.8
  370.5 3.6 fusion.1
  374.1 12.6 %convert_bitcast_fusion = bf16[64,1,64,1024]{3,2,0,1:T(8,128)(2,1)} fusion(bf16[64,1,32,1024]{3,2,0,1:T(8,128)(2,1)} %copy-done.8, bf16[64,1,32,1024]{3,2,0,1:T(8,128)(2,1)} %bitcast.138, f32[64,64,128]{2,1,0:T(8,128)} %fusion.1, bf16[1,128,1024]{2,1,0:T(8,128)(2,1)S(1)} %copy-done.11, bf16[1,1024,128]{2,1,0:T(8,128)(2,1)S(1)} %copy-done.12), kind=kOutput, calls=%fused_computation.5 | convolution fusion | flops 2171600896 | bytes 19398656 | tf_op jit(solution)/shard_map/jsrf,sfd->jsrd/dot_general | solution.py:271
  386.7 2.9 slice.72
  389.6 0.5 collective-permute-start.3
  390.1 6.8 %collective-permute-done.3 = bf16[64,1,32,1024]{3,2,0,1:T(8,128)(2,1)S(1)} collective-permute-done((bf16[64,1,32,1024]{3,2,0,1:T(8,128)(2,1)S(1)}, bf16[64,1,32,1024]{3,2,0,1:T(8,128)(2,1)S(1)}, u32[]{:S(2)}, u32[]{:S(2)}) %collective-permute-start.3) | collective-permute-done | bytes 4194336 | tf_op jit(solution)/shard_map/ppermute | solution.py:273
  396.8 4.3 fusion.2
  401.1 6.0 %all-to-all-start.1 = ((bf16[64,1,32,1024]{3,2,1,0:T(8,128)(2,1)}), bf16[64,1,32,1024]{3,2,1,0:T(8,128)(2,1)}, u32[]{:S(2)}, u32[]{:S(2)}) async-start(bf16[64,1,32,1024]{3,2,1,0:T(8,128)(2,1)} %fusion.2), calls=%async_computation.1 | async-start | bytes 8388608 | tf_op jit(solution)/shard_map/all_to_all | solution.py:277
  407.2 0.1 copy.104
  407.4 0.1 copy.108
  407.6 92.9 %all-to-all-done.1 = bf16[64,1,32,1024]{3,2,1,0:T(8,128)(2,1)} async-done(((bf16[64,1,32,1024]{3,2,1,0:T(8,128)(2,1)}), bf16[64,1,32,1024]{3,2,1,0:T(8,128)(2,1)}, u32[]{:S(2)}, u32[]{:S(2)}) %all-to-all-start.1) | async-done | bytes 4194336 | tf_op jit(solution)/shard_map/all_to_all | solution.py:277
  500.5 13.7 %gather_fusion.1 = bf16[2048,1024]{1,0:T(8,128)(2,1)} fusion(bf16[2048,1024]{1,0:T(8,128)(2,1)} %bitcast.55, s32[2048]{0:T(1024)S(1)} %broadcast_clamp_fusion), kind=kCustom, calls=%fused_computation.1 | custom fusion | bytes 8396800 | tf_op jit(solution)/shard_map/gather | solution.py:283
  514.2 5.8 %fusion.3 = bf16[256,1,1024]{2,1,0:T(2,128)(2,1)S(1)} fusion(f32[256,8,1]{1,2,0:T(1,128)S(1)} %copy.108, bf16[2048,1024]{1,0:T(8,128)(2,1)} %gather_fusion.1), kind=kOutput, calls=%fused_computation.9 | convolution fusion | flops 25165824 | bytes 4726784 | tf_op jit(solution)/shard_map/tk,tkd->td/dot_general | solution.py:284
  520.1 0.2 copy.113
  520.3 2.4 collective-permute-start.4
  522.7 1.5 collective-permute-done.4
  524.2 0.3 add_convert_fusion.1
  524.6 0.9 collective-permute-start.5
  525.6 0.8 copy.106
  526.4 25.0 %collective-permute-done.5 = bf16[256,1024]{1,0:T(8,128)(2,1)S(1)} collective-permute-done((bf16[256,1024]{1,0:T(8,128)(2,1)S(1)}, bf16[256,1024]{1,0:T(8,128)(2,1)S(1)}, u32[]{:S(2)}, u32[]{:S(2)}) %collective-permute-start.5) | collective-permute-done | bytes 524320 | tf_op jit(solution)/shard_map/ppermute | solution.py:161
  551.5 1.1 fusion.17
  (70 shorter events, 1.9 us)
Async XLA Ops:
  7.2 176.2 %copy-start = (bf16[256,1024]{1,0:T(8,128)(2,1)S(1)}, bf16[256,1024]{1,0:T(8,128)(2,1)}, u32[]{:S(2)}) copy-start(bf16[256,1024]{1,0:T(8,128)(2,1)} %param.22) | copy-start | bytes 1572868
  7.2 81.3 %copy-start.4 = (bf16[256,1024]{1,0:T(8,128)(2,1)S(1)}, bf16[256,1024]{1,0:T(8,128)(2,1)}, u32[]{:S(2)}) copy-start(bf16[256,1024]{1,0:T(8,128)(2,1)} %param.13) | copy-start | bytes 1572868
  7.2 81.3 %copy-start.9 = (bf16[1024,256]{1,0:T(8,128)(2,1)S(1)}, bf16[1024,256]{1,0:T(8,128)(2,1)}, u32[]{:S(2)}) copy-start(bf16[1024,256]{1,0:T(8,128)(2,1)} %param.19) | copy-start | bytes 1572868
  7.2 80.3 %all-gather.3.cloned.1.call-start = ((), (), s32[]{:S(2)}) async-start(), calls=%async_computation.2 | async-start | bytes 2621440 | tf_op jit(solution)/shard_map/all_gather | solution.py:214
  18.5 72.2 %copy-start.5 = (s32[256,8]{0,1:T(8,128)S(1)}, s32[256,8]{0,1:T(8,128)}, u32[]{:S(2)}) copy-start(s32[256,8]{0,1:T(8,128)} %param.15) | copy-start | bytes 24580
  32.9 142.1 %all-gather.5.cloned.1.call-start = ((), (), s32[]{:S(2)}) async-start(), calls=%async_computation.3 | async-start | bytes 10485760 | tf_op jit(solution)/shard_map/all_gather | solution.py:214
  182.1 9.7 %copy-start.7 = (bf16[1024]{0:T(1024)(128)(2,1)S(1)}, bf16[1024]{0:T(1024)(128)(2,1)}, u32[]{:S(2)}) copy-start(bf16[1024]{0:T(1024)(128)(2,1)} %param.18) | copy-start | bytes 6148
  183.7 2.4 collective-permute-start
  186.3 17.3 %collective-permute-start.1 = (bf16[256,1024]{1,0:T(8,128)(2,1)S(1)}, bf16[256,1024]{1,0:T(8,128)(2,1)S(1)}, u32[]{:S(2)}, u32[]{:S(2)}) collective-permute-start(bf16[256,1024]{1,0:T(8,128)(2,1)S(1)} %add_convert_fusion.2), channel_id=1, source_target_pairs={{0,2},{2,0},{1,3},{3,1},{4,6},{6,4},{5,7},{7,5},{8,10},{10,8},{9,1... | collective-permute-start | bytes 1572872 | tf_op jit(solution)/shard_map/ppermute | solution.py:161
  213.9 156.6 %copy-start.10 = (bf16[1,1024,128]{2,1,0:T(8,128)(2,1)S(1)}, bf16[1,1024,128]{2,1,0:T(8,128)(2,1)}, u32[]{:S(2)}) copy-start(bf16[1,1024,128]{2,1,0:T(8,128)(2,1)} %param.23) | copy-start | bytes 786436
  359.3 9.2 %copy-start.3 = (bf16[64,1,32,1024]{3,2,1,0:T(8,128)(2,1)}, bf16[64,1,32,1024]{3,2,1,0:T(8,128)(2,1)S(1)}, u32[]{:S(2)}) copy-start(bf16[64,1,32,1024]{3,2,1,0:T(8,128)(2,1)S(1)} %all_to_all.10) | copy-start | bytes 12582916
  359.3 14.7 %copy-start.11 = (bf16[1,128,1024]{2,1,0:T(8,128)(2,1)S(1)}, bf16[1,128,1024]{2,1,0:T(8,128)(2,1)}, u32[]{:S(2)}) copy-start(bf16[1,128,1024]{2,1,0:T(8,128)(2,1)} %param.25) | copy-start | bytes 786436
  359.3 14.7 %copy-start.12 = (bf16[1,1024,128]{2,1,0:T(8,128)(2,1)S(1)}, bf16[1,1024,128]{2,1,0:T(8,128)(2,1)}, u32[]{:S(2)}) copy-start(bf16[1,1024,128]{2,1,0:T(8,128)(2,1)} %param.24) | copy-start | bytes 786436
  359.3 9.2 %collective-permute-start.2 = (bf16[64,1,32,1024]{3,2,0,1:T(8,128)(2,1)S(1)}, bf16[64,1,32,1024]{3,2,0,1:T(8,128)(2,1)S(1)}, u32[]{:S(2)}, u32[]{:S(2)}) collective-permute-start(bf16[64,1,32,1024]{3,2,0,1:T(8,128)(2,1)S(1)} %bitcast.136), channel_id=1, source_target_pairs={{0,1},{1,0},{2,3},{3,2},{4,5},{5,4},{6,7},{7,6},{8,9},{9,8},{10,11... | collective-permute-start | bytes 12582920 | tf_op jit(solution)/shard_map/ppermute | solution.py:266
  368.5 2.0 copy-start.8
  386.7 10.1 %copy-start.2 = (bf16[64,1,64,1024]{3,2,0,1:T(8,128)(2,1)S(1)}, bf16[64,1,64,1024]{3,2,0,1:T(8,128)(2,1)}, u32[]{:S(2)}) copy-start(bf16[64,1,64,1024]{3,2,0,1:T(8,128)(2,1)} %convert_bitcast_fusion) | copy-start | bytes 25165828
  389.6 7.2 %collective-permute-start.3 = (bf16[64,1,32,1024]{3,2,0,1:T(8,128)(2,1)S(1)}, bf16[64,1,32,1024]{3,2,0,1:T(8,128)(2,1)S(1)}, u32[]{:S(2)}, u32[]{:S(2)}) collective-permute-start(bf16[64,1,32,1024]{3,2,0,1:T(8,128)(2,1)S(1)} %slice.72), channel_id=1, source_target_pairs={{0,1},{1,0},{2,3},{3,2},{4,5},{5,4},{6,7},{7,6},{8,9},{9,8},{10,11... | collective-permute-start | bytes 12582920 | tf_op jit(solution)/shard_map/ppermute | solution.py:273
  401.1 6.3 %copy-start.6 = (f32[256,8]{0,1:T(8,128)S(1)}, f32[256,8]{0,1:T(8,128)}, u32[]{:S(2)}) copy-start(f32[256,8]{0,1:T(8,128)} %param.16) | copy-start | bytes 24580
  401.1 99.4 %all-to-all-start.1 = ((bf16[64,1,32,1024]{3,2,1,0:T(8,128)(2,1)}), bf16[64,1,32,1024]{3,2,1,0:T(8,128)(2,1)}, u32[]{:S(2)}, u32[]{:S(2)}) async-start(bf16[64,1,32,1024]{3,2,1,0:T(8,128)(2,1)} %fusion.2), calls=%async_computation.1 | async-start | bytes 8388608 | tf_op jit(solution)/shard_map/all_to_all | solution.py:277
  514.2 38.3 %copy-start.1 = (bf16[256,1024]{1,0:T(8,128)(2,1)S(1)}, bf16[256,1024]{1,0:T(8,128)(2,1)}, u32[]{:S(2)}) copy-start(bf16[256,1024]{1,0:T(8,128)(2,1)} %param.22) | copy-start | bytes 1572868
  520.3 4.0 collective-permute-start.4
  524.6 26.9 %collective-permute-start.5 = (bf16[256,1024]{1,0:T(8,128)(2,1)S(1)}, bf16[256,1024]{1,0:T(8,128)(2,1)S(1)}, u32[]{:S(2)}, u32[]{:S(2)}) collective-permute-start(bf16[256,1024]{1,0:T(8,128)(2,1)S(1)} %add_convert_fusion.1), channel_id=1, source_target_pairs={{0,2},{2,0},{1,3},{3,1},{4,6},{6,4},{5,7},{7,5},{8,10},{10,8},{9,1... | collective-permute-start | bytes 1572872 | tf_op jit(solution)/shard_map/ppermute | solution.py:161
Sparse Core Ops, SparseCore 0:
  33.0 54.4 all-gather.2
  89.3 85.6 all-gather.4

commit v6 on v5

--- a/solution.py
+++ b/solution.py
@@ -154,6 +154,13 @@
     return jnp.stack([out[head, :, :, head] for head in range(kv_heads)])
 
 
+def seq_all_to_all(blocks):
+    grid = blocks.reshape((4, 4, 4) + blocks.shape[1:])
+    for position, axis_name in ((2, "sx"), (1, "sz"), (0, "sy")):
+        grid = lax.all_to_all(grid, axis_name, split_axis=position, concat_axis=position, tiled=True)
+    return grid.reshape(blocks.shape)
+
+
 def tp_sum(partial):
     swap = [(0, 1), (1, 0)]
     pair = partial.astype(jnp.float32) + lax.ppermute(partial, "tc", swap).astype(jnp.float32)
@@ -262,7 +269,7 @@
     )
     padded_rows = jnp.concatenate([normed_moe, jnp.zeros((1, normed_moe.shape[1]), jnp.bfloat16)])
     outbound = padded_rows[own_source]
-    arrived_own = lax.all_to_all(outbound, SUB_AXES, split_axis=0, concat_axis=0, tiled=True)
+    arrived_own = seq_all_to_all(outbound)
     arrived_other = lax.ppermute(arrived_own, "tc", swap)
     arrived = jnp.concatenate([arrived_own, arrived_other], axis=2)
     gate_val = jnp.einsum("jsrd,sdf->jsrf", arrived, w_gate, preferred_element_type=jnp.float32)
@@ -274,7 +281,7 @@
     pair_sum = (result[:, :, :half].astype(jnp.float32) + sibling_part.astype(jnp.float32)).astype(
         jnp.bfloat16
     )
-    returned = lax.all_to_all(pair_sum, SUB_AXES, split_axis=0, concat_axis=0, tiled=True).reshape(
+    returned = seq_all_to_all(pair_sum).reshape(
         slot_total * half, model_width
     )
     own_route = (slot_rank // half) == core

time: 559 us -> 758 us (1.36)
  blocking collectives: 158 us -> 395 us
  waiting for transfers between devices: 253 us -> 208 us
  local copies, waits for them, and re-layouts: 42.8 us -> 50.6 us
    all_to_all x1 -> x5, blocking collectives: 145 us -> 382 us  [seq_all_to_all(): lax.all_to_all(grid, axis_name, split_axis=position, concat_axis=position...]
    all_to_all x1, waiting for transfers between devices: 92.9 us -> 46.4 us  [seq_all_to_all(): lax.all_to_all(grid, axis_name, split_axis=position, concat_axis=position...]
  transfers between devices with their start and end apart: 9 -> 9, of which waited for: 9 -> 9; matrix products, arithmetic and copies ran while one was open for 6% -> 5% of each run, Pallas kernels for 0% -> 0%
where the time goes in v6:
time: 758 us; the launch traced here: 757 us
  blocking collectives  395 us (52%)
  waiting for transfers between devices  208 us (27%)
  local copies, waits for them, and re-layouts  50.6 us (7%)
  other arithmetic  37.1 us (5%)
  matrix products  25.8 us (3%)
  starting transfers between devices  19.2 us (3%)
  between operations  14.6 us (2%)
    all_to_all x5, blocking collectives, seq_all_to_all(): lax.all_to_all(grid, axis_name, split_axis=position, concat_axis=position...  382 us
    all_gather x2, waiting for transfers between devices, per_device(): joined = lax.all_gather(joined, axis_name, axis=0, tiled=True)  116 us
    all_to_all x1, waiting for transfers between devices, seq_all_to_all(): lax.all_to_all(grid, axis_name, split_axis=position, concat_axis=position...  46.4 us
    ppermute x2, waiting for transfers between devices, tp_sum(): lax.ppermute(pair, 'tz', swap).astype(jnp.float32)  29.5 us
    another operation x6, other arithmetic  19.3 us
  transfers between devices with their start and end apart: 9, of which 9 were waited for; matrix products, arithmetic and copies ran while one was open for 5% of the time, Pallas kernels for 0%

profile of v6, /device:TPU:1, one launch (start us, length us, event | category | flops | bytes accessed | tf_op | source)
XLA Modules:
  0.0 757.3 jit_solution(10101769902277235291)
XLA Ops:
  7.3 1.2 convert_reduce_fusion
  8.5 0.7 fusion.44
  9.1 0.7 convert_element_type.129
  9.8 1.2 fusion.9
  11.0 5.7 fusion.32
  16.7 0.2 multiply_cosine_fusion
  16.9 1.5 fusion.39
  18.6 1.5 convolution_convert_fusion.1
  20.1 12.8 %all_gather.9 = bf16[1024,256]{1,0:T(8,128)(2,1)} all-gather(bf16[256,256]{1,0:T(8,128)(2,1)S(1)} %pad_maximum_fusion), channel_id=1, replica_groups=mesh['sy'=4,'sz'=4,'sx'=4,'tz'=2,'tc'=2] {'sx'}, dimensions={0}, use_global_device_ids=true | all-gather | bytes 655360 | tf_op jit(solution)/shard_map/all_gather | solution.py:221
  33.0 54.5 %all-gather.3.cloned.1.call-done = bf16[4096,256]{1,0:T(8,128)(2,1)} async-done(((bf16[1024,256]{1,0:T(8,128)(2,1)}), bf16[4096,256]{1,0:T(8,128)(2,1)}) %all-gather.3.cloned.1.call-update) | async-done | bytes 2097168 | tf_op jit(solution)/shard_map/all_gather | solution.py:221
  87.5 0.9 slice.38
  88.5 0.4 fusion.41
  89.0 0.2 copy.88
  89.4 0.5 slice.39
  89.9 0.8 copy.91.qseg_ref
  90.9 18.0 %reduce-window.6 = s32[2,32,8,128]{3,2,1,0:T(8,128)S(1)} reduce-window(s32[2,32,8,128]{3,2,1,0:T(8,128)S(1)} %fusion.24, s32[]{:T(128)} %constant.93.clone.1), window={size=1x1x1x128 pad=0_0x0_0x0_0x127_0}, to_apply=%region_3.4 | reduce-window | flops 8323072 | bytes 524292 | tf_op jit(solution)/shard_map/reduce-window
  109.4 1.2 fusion.33
  110.6 1.2 pad_add_fusion.bounds_ref
  111.8 0.7 iota_add_fusion.qidx_ref
  112.5 0.7 broadcast_select_fusion.q_ref
  113.2 61.8 %all-gather.5.cloned.1.call-done.k_ref.v_ref = bf16[16384,256]{1,0:T(8,128)(2,1)} async-done(((bf16[4096,256]{1,0:T(8,128)(2,1)}), bf16[16384,256]{1,0:T(8,128)(2,1)}) %all-gather.5.cloned.1.call-update) | async-done | bytes 8388624 | tf_op jit(solution)/shard_map/all_gather | solution.py:221
  175.0 7.1 shard_map.140
  182.1 1.1 convert.27
  183.4 0.3 convolution_convert_fusion
  183.7 0.8 collective-permute-start
  185.4 0.7 collective-permute-done
  186.1 0.2 add_convert_fusion.2
  186.3 5.5 collective-permute-start.1
  191.9 8.1 %scatter_custom_fusion = s32[4096]{0:T(1024)S(1)} fusion(s32[2048]{0:T(1024)S(1)} %bitcast.149, s32[2048]{0:T(1024)S(1)} %reshape.276, s32[]{:T(128)} %constant.92.clone.1), kind=kCustom, calls=%fused_computation.76 | custom fusion | bytes 16388 | tf_op jit(solution)/shard_map/scatter | solution.py:262
  200.2 3.3 collective-permute-done.1
  203.6 0.3 fusion.13
  203.9 0.2 fusion.15
  204.2 9.7 %gather_fusion = bf16[2048,1024]{1,0:T(8,128)(2,1)} fusion(bf16[257,1024]{1,0:T(8,128)(2,1)S(1)} %concatenate.27, s32[2048]{0:T(1024)S(1)} %broadcast_clamp_fusion.1), kind=kCustom, calls=%fused_computation | custom fusion | bytes 8396800 | tf_op jit(solution)/shard_map/gather | solution.py:271
  213.9 2.6 copy.103
  216.5 50.9 %all_to_all.30 = bf16[4,4,4,1,32,1024]{5,4,1,0,3,2:T(8,128)(2,1)S(1)} all-to-all(bf16[4,4,4,1,32,1024]{5,4,1,0,3,2:T(8,128)(2,1)S(1)} %copy.103), channel_id=1, replica_groups=mesh['sy'=4,'sz'=4,'sx'=4,'tz'=2,'tc'=2] {'sx'}, dimensions={2} | all-to-all | bytes 8388608 | tf_op jit(solution)/shard_map/all_to_all | solution.py:160
  267.4 0.8 copy.104
  268.2 114.3 %all_to_all.31 = bf16[4,4,4,1,32,1024]{5,4,2,0,3,1:T(8,128)(2,1)S(1)} all-to-all(bf16[4,4,4,1,32,1024]{5,4,2,0,3,1:T(8,128)(2,1)S(1)} %copy.104), channel_id=1, replica_groups=mesh['sy'=4,'sz'=4,'sx'=4,'tz'=2,'tc'=2] {'sz'}, dimensions={1} | all-to-all | bytes 8388608 | tf_op jit(solution)/shard_map/all_to_all | solution.py:160
  382.5 0.8 copy.105
  383.3 71.1 %all_to_all.32 = bf16[4,4,4,1,32,1024]{5,4,2,1,3,0:T(8,128)(2,1)S(1)} all-to-all(bf16[4,4,4,1,32,1024]{5,4,2,1,3,0:T(8,128)(2,1)S(1)} %copy.105), channel_id=1, replica_groups=mesh['sy'=4,'sz'=4,'sx'=4,'tz'=2,'tc'=2] {'sy'}, dimensions={0} | all-to-all | bytes 8388608 | tf_op jit(solution)/shard_map/all_to_all | solution.py:160
  454.5 3.3 collective-permute-start.2
  457.8 6.8 collective-permute-done.2
  464.5 2.0 copy-done.8
  466.5 3.6 fusion.1
  470.1 12.6 %convert_bitcast_fusion = bf16[64,1,64,1024]{3,2,0,1:T(8,128)(2,1)} fusion(bf16[64,1,32,1024]{3,2,0,1:T(8,128)(2,1)} %copy-done.8, bf16[64,1,32,1024]{3,2,0,1:T(8,128)(2,1)} %bitcast.135, f32[64,64,128]{2,1,0:T(8,128)} %fusion.1, bf16[1,128,1024]{2,1,0:T(8,128)(2,1)S(1)} %copy-done.11, bf16[1,1024,128]{2,1,0:T(8,128)(2,1)S(1)} %copy-done.12), kind=kOutput, calls=%fused_computation.5 | convolution fusion | flops 2171600896 | bytes 19398656 | tf_op jit(solution)/shard_map/jsrf,sfd->jsrd/dot_general | solution.py:278
  482.7 2.8 slice.72
  485.5 0.5 collective-permute-start.3
  486.0 6.8 collective-permute-done.3
  492.8 2.5 add_convert_fusion
  495.3 0.5 copy.106
  495.8 51.1 %all_to_all.33 = bf16[4,4,4,1,32,1024]{5,4,1,0,3,2:T(8,128)(2,1)S(1)} all-to-all(bf16[4,4,4,1,32,1024]{5,4,1,0,3,2:T(8,128)(2,1)S(1)} %copy.106), channel_id=1, replica_groups=mesh['sy'=4,'sz'=4,'sx'=4,'tz'=2,'tc'=2] {'sx'}, dimensions={2} | all-to-all | bytes 8388608 | tf_op jit(solution)/shard_map/all_to_all | solution.py:160
  546.9 0.8 copy.107
  547.7 94.7 %all_to_all.34 = bf16[4,4,4,1,32,1024]{5,4,2,0,3,1:T(8,128)(2,1)S(1)} all-to-all(bf16[4,4,4,1,32,1024]{5,4,2,0,3,1:T(8,128)(2,1)S(1)} %copy.107), channel_id=1, replica_groups=mesh['sy'=4,'sz'=4,'sx'=4,'tz'=2,'tc'=2] {'sz'}, dimensions={1} | all-to-all | bytes 8388608 | tf_op jit(solution)/shard_map/all_to_all | solution.py:160
  642.4 2.4 copy.108
  644.8 5.2 all-to-all-start.5
  650.4 46.4 %all-to-all-done.5 = bf16[4,4,4,1,32,1024]{5,4,2,1,3,0:T(8,128)(2,1)} async-done(((bf16[4,4,4,1,32,1024]{5,4,2,1,3,0:T(8,128)(2,1)}), bf16[4,4,4,1,32,1024]{5,4,2,1,3,0:T(8,128)(2,1)}, u32[]{:S(2)}, u32[]{:S(2)}) %all-to-all-start.5) | async-done | bytes 4194336 | tf_op jit(solution)/shard_map/all_to_all | solution.py:160
  696.8 13.7 %gather_fusion.1 = bf16[2048,1024]{1,0:T(8,128)(2,1)} fusion(bf16[2048,1024]{1,0:T(8,128)(2,1)} %bitcast.53, s32[2048]{0:T(1024)S(1)} %broadcast_clamp_fusion), kind=kCustom, calls=%fused_computation.1 | custom fusion | bytes 8396800 | tf_op jit(solution)/shard_map/gather | solution.py:290
  710.5 5.8 fusion.2
  716.6 2.9 collective-permute-start.4
  719.5 1.5 collective-permute-done.4
  721.0 0.3 add_convert_fusion.1
  721.3 0.9 collective-permute-start.5
  722.4 0.8 copy.112
  723.2 26.2 %collective-permute-done.5 = bf16[256,1024]{1,0:T(8,128)(2,1)S(1)} collective-permute-done((bf16[256,1024]{1,0:T(8,128)(2,1)S(1)}, bf16[256,1024]{1,0:T(8,128)(2,1)S(1)}, u32[]{:S(2)}, u32[]{:S(2)}) %collective-permute-start.5) | collective-permute-done | bytes 524320 | tf_op jit(solution)/shard_map/ppermute | solution.py:168
  749.4 1.1 fusion.16
  (80 shorter events, 3.3 us)
Async XLA Ops:
  7.2 176.2 %copy-start = (bf16[256,1024]{1,0:T(8,128)(2,1)S(1)}, bf16[256,1024]{1,0:T(8,128)(2,1)}, u32[]{:S(2)}) copy-start(bf16[256,1024]{1,0:T(8,128)(2,1)} %param.22) | copy-start | bytes 1572868
  7.2 81.3 %copy-start.4 = (bf16[256,1024]{1,0:T(8,128)(2,1)S(1)}, bf16[256,1024]{1,0:T(8,128)(2,1)}, u32[]{:S(2)}) copy-start(bf16[256,1024]{1,0:T(8,128)(2,1)} %param.13) | copy-start | bytes 1572868
  7.2 81.3 %copy-start.9 = (bf16[1024,256]{1,0:T(8,128)(2,1)S(1)}, bf16[1024,256]{1,0:T(8,128)(2,1)}, u32[]{:S(2)}) copy-start(bf16[1024,256]{1,0:T(8,128)(2,1)} %param.19) | copy-start | bytes 1572868
  7.2 80.3 %all-gather.3.cloned.1.call-start = ((), (), s32[]{:S(2)}) async-start(), calls=%async_computation.6 | async-start | bytes 2621440 | tf_op jit(solution)/shard_map/all_gather | solution.py:221
  18.5 72.2 %copy-start.5 = (s32[256,8]{0,1:T(8,128)S(1)}, s32[256,8]{0,1:T(8,128)}, u32[]{:S(2)}) copy-start(s32[256,8]{0,1:T(8,128)} %param.15) | copy-start | bytes 24580
  32.9 142.1 %all-gather.5.cloned.1.call-start = ((), (), s32[]{:S(2)}) async-start(), calls=%async_computation.7 | async-start | bytes 10485760 | tf_op jit(solution)/shard_map/all_gather | solution.py:221
  182.1 9.7 %copy-start.7 = (bf16[1024]{0:T(1024)(128)(2,1)S(1)}, bf16[1024]{0:T(1024)(128)(2,1)}, u32[]{:S(2)}) copy-start(bf16[1024]{0:T(1024)(128)(2,1)} %param.18) | copy-start | bytes 6148
  183.7 2.4 collective-permute-start
  186.3 17.3 %collective-permute-start.1 = (bf16[256,1024]{1,0:T(8,128)(2,1)S(1)}, bf16[256,1024]{1,0:T(8,128)(2,1)S(1)}, u32[]{:S(2)}, u32[]{:S(2)}) collective-permute-start(bf16[256,1024]{1,0:T(8,128)(2,1)S(1)} %add_convert_fusion.2), channel_id=1, source_target_pairs={{0,2},{2,0},{1,3},{3,1},{4,6},{6,4},{5,7},{7,5},{8,10},{10,8},{9,1... | collective-permute-start | bytes 1572872 | tf_op jit(solution)/shard_map/ppermute | solution.py:168
  383.3 83.2 %copy-start.10 = (bf16[1,1024,128]{2,1,0:T(8,128)(2,1)S(1)}, bf16[1,1024,128]{2,1,0:T(8,128)(2,1)}, u32[]{:S(2)}) copy-start(bf16[1,1024,128]{2,1,0:T(8,128)(2,1)} %param.23) | copy-start | bytes 786436
  454.5 10.1 %copy-start.3 = (bf16[4,4,4,1,32,1024]{5,4,2,1,3,0:T(8,128)(2,1)}, bf16[4,4,4,1,32,1024]{5,4,2,1,3,0:T(8,128)(2,1)S(1)}, u32[]{:S(2)}) copy-start(bf16[4,4,4,1,32,1024]{5,4,2,1,3,0:T(8,128)(2,1)S(1)} %all_to_all.32) | copy-start | bytes 12582916
  454.5 15.6 %copy-start.11 = (bf16[1,128,1024]{2,1,0:T(8,128)(2,1)S(1)}, bf16[1,128,1024]{2,1,0:T(8,128)(2,1)}, u32[]{:S(2)}) copy-start(bf16[1,128,1024]{2,1,0:T(8,128)(2,1)} %param.25) | copy-start | bytes 786436
  454.5 15.6 %copy-start.12 = (bf16[1,1024,128]{2,1,0:T(8,128)(2,1)S(1)}, bf16[1,1024,128]{2,1,0:T(8,128)(2,1)}, u32[]{:S(2)}) copy-start(bf16[1,1024,128]{2,1,0:T(8,128)(2,1)} %param.24) | copy-start | bytes 786436
  454.5 10.1 %collective-permute-start.2 = (bf16[64,1,32,1024]{3,2,0,1:T(8,128)(2,1)S(1)}, bf16[64,1,32,1024]{3,2,0,1:T(8,128)(2,1)S(1)}, u32[]{:S(2)}, u32[]{:S(2)}) collective-permute-start(bf16[64,1,32,1024]{3,2,0,1:T(8,128)(2,1)S(1)} %bitcast.133), channel_id=1, source_target_pairs={{0,1},{1,0},{2,3},{3,2},{4,5},{5,4},{6,7},{7,6},{8,9},{9,8},{10,11... | collective-permute-start | bytes 12582920 | tf_op jit(solution)/shard_map/ppermute | solution.py:273
  464.5 2.0 copy-start.8
  482.7 10.1 %copy-start.2 = (bf16[64,1,64,1024]{3,2,0,1:T(8,128)(2,1)S(1)}, bf16[64,1,64,1024]{3,2,0,1:T(8,128)(2,1)}, u32[]{:S(2)}) copy-start(bf16[64,1,64,1024]{3,2,0,1:T(8,128)(2,1)} %convert_bitcast_fusion) | copy-start | bytes 25165828
  485.5 7.2 collective-permute-start.3
  644.8 5.4 copy-start.6
  644.8 52.0 %all-to-all-start.5 = ((bf16[4,4,4,1,32,1024]{5,4,2,1,3,0:T(8,128)(2,1)}), bf16[4,4,4,1,32,1024]{5,4,2,1,3,0:T(8,128)(2,1)}, u32[]{:S(2)}, u32[]{:S(2)}) async-start(bf16[4,4,4,1,32,1024]{5,4,2,1,3,0:T(8,128)(2,1)} %copy.108), calls=%async_computation.5 | async-start | bytes 8388608 | tf_op jit(solution)/shard_map/all_to_all | solution.py:160
  710.5 39.9 %copy-start.1 = (bf16[256,1024]{1,0:T(8,128)(2,1)S(1)}, bf16[256,1024]{1,0:T(8,128)(2,1)}, u32[]{:S(2)}) copy-start(bf16[256,1024]{1,0:T(8,128)(2,1)} %param.22) | copy-start | bytes 1572868
  716.6 4.4 collective-permute-start.4
  721.3 28.0 %collective-permute-start.5 = (bf16[256,1024]{1,0:T(8,128)(2,1)S(1)}, bf16[256,1024]{1,0:T(8,128)(2,1)S(1)}, u32[]{:S(2)}, u32[]{:S(2)}) collective-permute-start(bf16[256,1024]{1,0:T(8,128)(2,1)S(1)} %add_convert_fusion.1), channel_id=1, source_target_pairs={{0,2},{2,0},{1,3},{3,1},{4,6},{6,4},{5,7},{7,5},{8,10},{10,8},{9,1... | collective-permute-start | bytes 1572872 | tf_op jit(solution)/shard_map/ppermute | solution.py:168
Sparse Core Ops, SparseCore 0:
  33.0 54.4 all-gather.2
  89.3 85.6 all-gather.4

commit v7 on v5

--- a/solution.py
+++ b/solution.py
@@ -246,22 +246,16 @@
     before = jnp.cumsum(onehot, axis=1) - onehot
     slot_rank = jnp.sum(before * onehot, axis=2).reshape(tokens, route_count)
     target = slot_of * capacity + slot_rank
-    token_ids = jnp.broadcast_to(
-        jnp.arange(tokens, dtype=jnp.int32)[:, None], (tokens, route_count)
-    )
-    source = (
-        jnp.full((slot_total * capacity,), tokens, jnp.int32)
-        .at[target.reshape(-1)]
-        .set(token_ids.reshape(-1))
-    )
     half = capacity // 2
     core = lax.axis_index("tc")
     swap = [(0, 1), (1, 0)]
-    own_source = lax.dynamic_slice_in_dim(
-        source.reshape(seq_count, slots_dev, capacity), core * half, half, axis=2
-    )
-    padded_rows = jnp.concatenate([normed_moe, jnp.zeros((1, normed_moe.shape[1]), jnp.bfloat16)])
-    outbound = padded_rows[own_source]
+    own_route = (slot_rank // half) == core
+    local_target = jnp.where(own_route, slot_of * half + slot_rank - core * half, -1)
+    row_ids = jnp.arange(slot_total * half, dtype=jnp.int32)
+    picks = local_target[None, :, :] == row_ids[:, None, None]
+    dispatch = jnp.any(picks, axis=2).astype(jnp.bfloat16)
+    outbound = jnp.dot(dispatch, normed_moe, preferred_element_type=jnp.float32).astype(jnp.bfloat16)
+    outbound = outbound.reshape(seq_count, slots_dev, half, model_width)
     arrived_own = lax.all_to_all(outbound, SUB_AXES, split_axis=0, concat_axis=0, tiled=True)
     arrived_other = lax.ppermute(arrived_own, "tc", swap)
     arrived = jnp.concatenate([arrived_own, arrived_other], axis=2)
@@ -277,16 +271,11 @@
     returned = lax.all_to_all(pair_sum, SUB_AXES, split_axis=0, concat_axis=0, tiled=True).reshape(
         slot_total * half, model_width
     )
-    own_route = (slot_rank // half) == core
-    local_target = jnp.where(own_route, slot_of * half + slot_rank - core * half, 0)
-    own_gates = jnp.where(own_route, gates, 0.0)
-    picked = returned[local_target]
-    combined = jnp.einsum(
-        "tk,tkd->td",
-        own_gates,
-        picked,
-        preferred_element_type=jnp.float32,
-        precision=lax.Precision.HIGHEST,
+    weighting = jnp.sum(
+        jnp.where(local_target[:, :, None] == row_ids[None, None, :], gates[:, :, None], 0.0), axis=1
+    )
+    combined = jnp.dot(
+        weighting, returned, preferred_element_type=jnp.float32, precision=lax.Precision.HIGHEST
     )
     expert_sum = tp_sum(combined.astype(jnp.bfloat16))
     hidden_out = (residual.astype(jnp.float32) + expert_sum).astype(jnp.bfloat16)

time: 559 us -> 556 us (level)
  local copies, waits for them, and re-layouts: 42.8 us -> 10.5 us
  other arithmetic: 38.9 us -> 62.9 us
  waiting for transfers between devices: 253 us -> 262 us
  blocking collectives: 158 us -> 150 us
    gather x2 -> x0, local copies, waits for them, and re-layouts: 23.4 us -> none  [the longest x1 13.7 us: per_device(): picked = returned[local_target]]
    reduce_or x0 -> x1, other arithmetic: none -> 18.7 us  [per_device(): dispatch = jnp.any(picks, axis=2).astype(jnp.bfloat16)]
    all_gather x2, waiting for transfers between devices: 116 us -> 135 us  [per_device(): joined = lax.all_gather(joined, axis_name, axis=0, tiled=True)]
    all_to_all x1, blocking collectives: 145 us -> 137 us  [per_device(): lax.all_to_all(outbound, SUB_AXES, split_axis=0, concat_axis=0, tiled=True)]
    scatter x1 -> x0, local copies, waits for them, and re-layouts: 8.06 us -> none  [per_device(): source = jnp.full((slot_total * capacity,), tokens, jnp.int32).at[target....]
  transfers between devices with their start and end apart: 9 -> 9, of which waited for: 9 -> 7; matrix products, arithmetic and copies ran while one was open for 6% -> 9% of each run, Pallas kernels for 0% -> 0%
where the time goes in v7:
time: 556 us; the launch traced here: 553 us
  waiting for transfers between devices  262 us (47%)
  blocking collectives  150 us (27%)
  other arithmetic  62.9 us (11%)
  matrix products  27.1 us (5%)
  starting transfers between devices  19 us (3%)
  between operations  14.5 us (3%)
  local copies, waits for them, and re-layouts  10.5 us (2%)
  Pallas kernels  7.05 us (1%)
    all_to_all x1, blocking collectives, per_device(): lax.all_to_all(outbound, SUB_AXES, split_axis=0, concat_axis=0, tiled=True)  137 us
    all_gather x2, waiting for transfers between devices, per_device(): joined = lax.all_gather(joined, axis_name, axis=0, tiled=True)  135 us
    all_to_all x1, waiting for transfers between devices, per_device(): lax.all_to_all(pair_sum, SUB_AXES, split_axis=0, concat_axis=0, tiled=True)  87.5 us
    ppermute x2, waiting for transfers between devices, tp_sum(): lax.ppermute(pair, 'tz', swap).astype(jnp.float32)  25.1 us
    another operation x6, other arithmetic  19.3 us
    reduce_or x1, other arithmetic, per_device(): dispatch = jnp.any(picks, axis=2).astype(jnp.bfloat16)  18.7 us
    all_gather x1, blocking collectives, per_device(): joined = lax.all_gather(joined, axis_name, axis=0, tiled=True)  12.8 us
    dot_general x1, matrix products, per_device(): jnp.einsum('jsrf,sfd->jsrd', activated, w_down, preferred_element_type=jn...  12.7 us
  transfers between devices with their start and end apart: 9, of which 7 were waited for; matrix products, arithmetic and copies ran while one was open for 9% of the time, Pallas kernels for 0%

profile of v7, /device:TPU:1, one launch (start us, length us, event | category | flops | bytes accessed | tf_op | source)
XLA Modules:
  0.0 553.5 jit_solution(16791971855514193472)
XLA Ops:
  7.3 1.2 convert_reduce_fusion
  8.5 0.7 fusion.45
  9.1 0.7 convert_element_type.133
  9.8 1.2 fusion.9
  11.1 5.8 %fusion.33 = (f32[256]{0:T(256)S(1)}, s32[256]{0:T(256)S(1)}) fusion(s32[]{:T(128)} %bitcast.4, s32[]{:T(128)} %bitcast.5, s32[]{:T(128)} %bitcast.6, s32[]{:T(128)} %bitcast.7, s32[]{:T(128)} %bitcast.8, s32[]{:T(128)} %bitcast.9, s32[]{:T(128)} %bitcast.10, s32[]{:T(128)} %bitcast.11, s32[]{:T(128)S(6)} %mul.163, s32[16384]{0:T(1024)} %param.14, ...), kind=kLoop, calls=%fused_computation.94 | loop fusion | flops 5120 | bytes 3112 | tf_op jit(solution)/shard_map/convert_element_type | solution.py:32
  16.9 0.2 multiply_cosine_fusion
  17.1 1.5 fusion.40
  18.6 0.1 copy.84
  18.7 1.5 convolution_convert_fusion.3
  20.2 12.8 %all_gather.9 = bf16[1024,256]{1,0:T(8,128)(2,1)} all-gather(bf16[256,256]{1,0:T(8,128)(2,1)S(1)} %pad_maximum_fusion), channel_id=1, replica_groups=mesh['sy'=4,'sz'=4,'sx'=4,'tz'=2,'tc'=2] {'sx'}, dimensions={0}, use_global_device_ids=true | all-gather | bytes 655360 | tf_op jit(solution)/shard_map/all_gather | solution.py:214
  33.1 54.5 %all-gather.3.cloned.1.call-done = bf16[4096,256]{1,0:T(8,128)(2,1)} async-done(((bf16[1024,256]{1,0:T(8,128)(2,1)}), bf16[4096,256]{1,0:T(8,128)(2,1)}) %all-gather.3.cloned.1.call-update) | async-done | bytes 2097168 | tf_op jit(solution)/shard_map/all_gather | solution.py:214
  87.7 0.9 slice.38
  88.6 0.5 fusion.42
  89.2 0.2 copy.82
  89.4 0.1 broadcast_in_dim.39
  89.5 0.5 slice.39
  90.0 0.8 copy.85.qseg_ref
  90.8 0.1 copy.87
  91.0 0.1 eq.69
  91.1 1.3 fusion.34
  92.4 1.2 pad_add_fusion.bounds_ref
  93.6 0.7 iota_add_fusion.qidx_ref
  94.3 0.7 broadcast_select_fusion.q_ref
  95.0 80.0 %all-gather.5.cloned.1.call-done.k_ref.v_ref = bf16[16384,256]{1,0:T(8,128)(2,1)} async-done(((bf16[4096,256]{1,0:T(8,128)(2,1)}), bf16[16384,256]{1,0:T(8,128)(2,1)}) %all-gather.5.cloned.1.call-update) | async-done | bytes 8388624 | tf_op jit(solution)/shard_map/all_gather | solution.py:214
  175.1 7.1 %shard_map.140 = f32[4,256,128]{2,1,0:T(8,128)} custom-call(s32[2]{0:T(128)} %pad_add_fusion.bounds_ref, bf16[2,2,256,128]{3,2,1,0:T(8,128)(2,1)} %broadcast_select_fusion.q_ref, bf16[16384,256]{1,0:T(8,128)(2,1)} %all-gather.5.cloned.1.call-done.k_ref.v_ref, bf16[16384,256]{1,0:T(8,128)(2,1)} %all-gather.5.cloned.1.call-done.k_ref.v_ref, ...), custom_call_target="tpu_custom_call" | custom-call | tf_op jit(solution)/shard_map/pallas_call | solution.py:139
  182.1 1.1 convert.27
  183.2 0.1 copy.86
  183.4 0.3 convolution_convert_fusion.2
  183.7 0.9 collective-permute-start
  184.7 0.1 eq.65
  184.8 18.0 %reduce-window.6 = s32[2,32,8,128]{3,2,1,0:T(8,128)S(1)} reduce-window(s32[2,32,8,128]{3,2,1,0:T(8,128)S(1)} %fusion.27, s32[]{:T(128)} %constant.85.clone.1), window={size=1x1x1x128 pad=0_0x0_0x0_0x127_0}, to_apply=%region_3.4 | reduce-window | flops 8323072 | bytes 524292 | tf_op jit(solution)/shard_map/reduce-window
  202.8 0.1 slice.65
  202.9 0.2 copy.89
  203.2 0.1 broadcast_add_fusion
  203.5 0.1 reshape.191
  203.7 0.2 add_convert_fusion.2
  203.9 5.7 %collective-permute-start.1 = (bf16[256,1024]{1,0:T(8,128)(2,1)S(1)}, bf16[256,1024]{1,0:T(8,128)(2,1)S(1)}, u32[]{:S(2)}, u32[]{:S(2)}) collective-permute-start(bf16[256,1024]{1,0:T(8,128)(2,1)S(1)} %add_convert_fusion.2), channel_id=1, source_target_pairs={{0,2},{2,0},{1,3},{3,1},{4,6},{6,4},{5,7},{7,5},{8,10},{10,8},{9,1... | collective-permute-start | bytes 1572872 | tf_op jit(solution)/shard_map/ppermute | solution.py:161
  209.7 18.7 %fusion = pred[2048,256]{1,0:T(8,128)(4,1)S(1)} fusion(s32[256,8]{0,1:T(8,128)S(1)} %subtract_select_fusion), kind=kLoop, calls=%fused_computation.3 | loop fusion | flops 7864320 | bytes 532480 | tf_op jit(solution)/shard_map/reduce_or | solution.py:256
  228.4 0.3 fusion.13
  228.7 1.4 convolution_convert_fusion
  230.1 137.4 %all_to_all.10 = bf16[64,1,32,1024]{3,2,1,0:T(8,128)(2,1)S(1)} all-to-all(bf16[64,1,32,1024]{3,2,1,0:T(8,128)(2,1)S(1)} %bitcast.124), channel_id=1, replica_groups=mesh['sy'=4,'sz'=4,'sx'=4,'tz'=2,'tc'=2] {'sy','sz','sx'}, dimensions={0} | all-to-all | bytes 8388608 | tf_op jit(solution)/shard_map/all_to_all | solution.py:259
  367.5 2.4 collective-permute-start.2
  369.9 6.8 %collective-permute-done.2 = bf16[64,1,32,1024]{3,2,0,1:T(8,128)(2,1)S(1)} collective-permute-done((bf16[64,1,32,1024]{3,2,0,1:T(8,128)(2,1)S(1)}, bf16[64,1,32,1024]{3,2,0,1:T(8,128)(2,1)S(1)}, u32[]{:S(2)}, u32[]{:S(2)}) %collective-permute-start.2) | collective-permute-done | bytes 4194336 | tf_op jit(solution)/shard_map/ppermute | solution.py:260
  376.7 2.0 copy-done.8
  378.7 3.6 fusion.2
  382.3 12.7 %convert_bitcast_fusion = bf16[64,1,64,1024]{3,2,0,1:T(8,128)(2,1)} fusion(bf16[64,1,32,1024]{3,2,0,1:T(8,128)(2,1)} %copy-done.8, bf16[64,1,32,1024]{3,2,0,1:T(8,128)(2,1)} %bitcast.127, f32[64,64,128]{2,1,0:T(8,128)} %fusion.2, bf16[1,128,1024]{2,1,0:T(8,128)(2,1)S(1)} %copy-done.11, bf16[1,1024,128]{2,1,0:T(8,128)(2,1)S(1)} %copy-done.12), kind=kOutput, calls=%fused_computation.6 | convolution fusion | flops 2171600896 | bytes 19398656 | tf_op jit(solution)/shard_map/jsrf,sfd->jsrd/dot_general | solution.py:265
  394.9 2.9 slice.68
  397.8 0.5 collective-permute-start.3
  398.3 6.8 %collective-permute-done.3 = bf16[64,1,32,1024]{3,2,0,1:T(8,128)(2,1)S(1)} collective-permute-done((bf16[64,1,32,1024]{3,2,0,1:T(8,128)(2,1)S(1)}, bf16[64,1,32,1024]{3,2,0,1:T(8,128)(2,1)S(1)}, u32[]{:S(2)}, u32[]{:S(2)}) %collective-permute-start.3) | collective-permute-done | bytes 4194336 | tf_op jit(solution)/shard_map/ppermute | solution.py:267
  405.1 4.3 fusion.3
  409.4 6.1 %all-to-all-start.1 = ((bf16[64,1,32,1024]{3,2,1,0:T(8,128)(2,1)}), bf16[64,1,32,1024]{3,2,1,0:T(8,128)(2,1)}, u32[]{:S(2)}, u32[]{:S(2)}) async-start(bf16[64,1,32,1024]{3,2,1,0:T(8,128)(2,1)} %fusion.3), calls=%async_computation.1 | async-start | bytes 8388608 | tf_op jit(solution)/shard_map/all_to_all | solution.py:271
  415.4 0.1 copy.96
  415.6 0.1 copy.97
  415.7 5.5 select_reduce_fusion
  421.2 87.5 %all-to-all-done.1 = bf16[64,1,32,1024]{3,2,1,0:T(8,128)(2,1)} async-done(((bf16[64,1,32,1024]{3,2,1,0:T(8,128)(2,1)}), bf16[64,1,32,1024]{3,2,1,0:T(8,128)(2,1)}, u32[]{:S(2)}, u32[]{:S(2)}) %all-to-all-start.1) | async-done | bytes 4194336 | tf_op jit(solution)/shard_map/all_to_all | solution.py:271
  508.8 5.7 %convolution_convert_fusion.1 = bf16[256,1024]{1,0:T(8,128)(2,1)S(1)} fusion(f32[256,2048]{1,0:T(8,128)S(1)} %select_reduce_fusion, bf16[2048,1024]{1,0:T(8,128)(2,1)} %bitcast.53), kind=kOutput, calls=%fused_computation.25 | convolution fusion | flops 6442713088 | bytes 6815744 | tf_op jit(solution)/shard_map/dot_general | solution.py:277
  514.5 2.4 collective-permute-start.4
  516.9 1.5 collective-permute-done.4
  518.4 0.2 add_convert_fusion.1
  518.6 0.9 collective-permute-start.5
  519.5 0.1 copy.102
  519.7 0.8 copy.103
  520.5 25.1 %collective-permute-done.5 = bf16[256,1024]{1,0:T(8,128)(2,1)S(1)} collective-permute-done((bf16[256,1024]{1,0:T(8,128)(2,1)S(1)}, bf16[256,1024]{1,0:T(8,128)(2,1)S(1)}, u32[]{:S(2)}, u32[]{:S(2)}) %collective-permute-start.5) | collective-permute-done | bytes 524320 | tf_op jit(solution)/shard_map/ppermute | solution.py:161
  545.6 1.1 fusion.16
  (55 shorter events, 0.8 us)
Async XLA Ops:
  7.2 176.2 %copy-start = (bf16[256,1024]{1,0:T(8,128)(2,1)S(1)}, bf16[256,1024]{1,0:T(8,128)(2,1)}, u32[]{:S(2)}) copy-start(bf16[256,1024]{1,0:T(8,128)(2,1)} %param.22) | copy-start | bytes 1572868
  7.2 81.4 %copy-start.4 = (bf16[256,1024]{1,0:T(8,128)(2,1)S(1)}, bf16[256,1024]{1,0:T(8,128)(2,1)}, u32[]{:S(2)}) copy-start(bf16[256,1024]{1,0:T(8,128)(2,1)} %param.13) | copy-start | bytes 1572868
  7.2 81.4 %copy-start.9 = (bf16[1024,256]{1,0:T(8,128)(2,1)S(1)}, bf16[1024,256]{1,0:T(8,128)(2,1)}, u32[]{:S(2)}) copy-start(bf16[1024,256]{1,0:T(8,128)(2,1)} %param.19) | copy-start | bytes 1572868
  7.2 80.4 %all-gather.3.cloned.1.call-start = ((), (), s32[]{:S(2)}) async-start(), calls=%async_computation.2 | async-start | bytes 2621440 | tf_op jit(solution)/shard_map/all_gather | solution.py:214
  18.6 72.2 %copy-start.5 = (s32[256,8]{0,1:T(8,128)S(1)}, s32[256,8]{0,1:T(8,128)}, u32[]{:S(2)}) copy-start(s32[256,8]{0,1:T(8,128)} %param.15) | copy-start | bytes 24580
  33.1 142.0 %all-gather.5.cloned.1.call-start = ((), (), s32[]{:S(2)}) async-start(), calls=%async_computation.3 | async-start | bytes 10485760 | tf_op jit(solution)/shard_map/all_gather | solution.py:214
  182.1 21.6 %copy-start.7 = (bf16[1024]{0:T(1024)(128)(2,1)S(1)}, bf16[1024]{0:T(1024)(128)(2,1)}, u32[]{:S(2)}) copy-start(bf16[1024]{0:T(1024)(128)(2,1)} %param.18) | copy-start | bytes 6148
  183.7 20.0 %collective-permute-start = (bf16[256,1024]{1,0:T(8,128)(2,1)S(1)}, bf16[256,1024]{1,0:T(8,128)(2,1)S(1)}, u32[]{:S(2)}, u32[]{:S(2)}) collective-permute-start(bf16[256,1024]{1,0:T(8,128)(2,1)S(1)} %convolution_convert_fusion.2), channel_id=1, source_target_pairs={{0,1},{1,0},{2,3},{3,2},{4,5},{5,4},{6,7},{7,6},{8,9},{9,8},{10,11... | collective-permute-start | bytes 1572872 | tf_op jit(solution)/shard_map/ppermute | solution.py:159
  203.9 24.4 %collective-permute-start.1 = (bf16[256,1024]{1,0:T(8,128)(2,1)S(1)}, bf16[256,1024]{1,0:T(8,128)(2,1)S(1)}, u32[]{:S(2)}, u32[]{:S(2)}) collective-permute-start(bf16[256,1024]{1,0:T(8,128)(2,1)S(1)} %add_convert_fusion.2), channel_id=1, source_target_pairs={{0,2},{2,0},{1,3},{3,1},{4,6},{6,4},{5,7},{7,5},{8,10},{10,8},{9,1... | collective-permute-start | bytes 1572872 | tf_op jit(solution)/shard_map/ppermute | solution.py:161
  230.1 148.6 %copy-start.10 = (bf16[1,1024,128]{2,1,0:T(8,128)(2,1)S(1)}, bf16[1,1024,128]{2,1,0:T(8,128)(2,1)}, u32[]{:S(2)}) copy-start(bf16[1,1024,128]{2,1,0:T(8,128)(2,1)} %param.23) | copy-start | bytes 786436
  367.5 9.2 %copy-start.3 = (bf16[64,1,32,1024]{3,2,1,0:T(8,128)(2,1)}, bf16[64,1,32,1024]{3,2,1,0:T(8,128)(2,1)S(1)}, u32[]{:S(2)}) copy-start(bf16[64,1,32,1024]{3,2,1,0:T(8,128)(2,1)S(1)} %all_to_all.10) | copy-start | bytes 12582916
  367.5 14.8 %copy-start.11 = (bf16[1,128,1024]{2,1,0:T(8,128)(2,1)S(1)}, bf16[1,128,1024]{2,1,0:T(8,128)(2,1)}, u32[]{:S(2)}) copy-start(bf16[1,128,1024]{2,1,0:T(8,128)(2,1)} %param.25) | copy-start | bytes 786436
  367.5 14.8 %copy-start.12 = (bf16[1,1024,128]{2,1,0:T(8,128)(2,1)S(1)}, bf16[1,1024,128]{2,1,0:T(8,128)(2,1)}, u32[]{:S(2)}) copy-start(bf16[1,1024,128]{2,1,0:T(8,128)(2,1)} %param.24) | copy-start | bytes 786436
  367.5 9.2 %collective-permute-start.2 = (bf16[64,1,32,1024]{3,2,0,1:T(8,128)(2,1)S(1)}, bf16[64,1,32,1024]{3,2,0,1:T(8,128)(2,1)S(1)}, u32[]{:S(2)}, u32[]{:S(2)}) collective-permute-start(bf16[64,1,32,1024]{3,2,0,1:T(8,128)(2,1)S(1)} %bitcast.125), channel_id=1, source_target_pairs={{0,1},{1,0},{2,3},{3,2},{4,5},{5,4},{6,7},{7,6},{8,9},{9,8},{10,11... | collective-permute-start | bytes 12582920 | tf_op jit(solution)/shard_map/ppermute | solution.py:260
  376.7 2.0 copy-start.8
  394.9 10.1 %copy-start.2 = (bf16[64,1,64,1024]{3,2,0,1:T(8,128)(2,1)S(1)}, bf16[64,1,64,1024]{3,2,0,1:T(8,128)(2,1)}, u32[]{:S(2)}) copy-start(bf16[64,1,64,1024]{3,2,0,1:T(8,128)(2,1)} %convert_bitcast_fusion) | copy-start | bytes 25165828
  397.8 7.2 %collective-permute-start.3 = (bf16[64,1,32,1024]{3,2,0,1:T(8,128)(2,1)S(1)}, bf16[64,1,32,1024]{3,2,0,1:T(8,128)(2,1)S(1)}, u32[]{:S(2)}, u32[]{:S(2)}) collective-permute-start(bf16[64,1,32,1024]{3,2,0,1:T(8,128)(2,1)S(1)} %slice.68), channel_id=1, source_target_pairs={{0,1},{1,0},{2,3},{3,2},{4,5},{5,4},{6,7},{7,6},{8,9},{9,8},{10,11... | collective-permute-start | bytes 12582920 | tf_op jit(solution)/shard_map/ppermute | solution.py:267
  409.4 6.2 %copy-start.6 = (f32[256,8]{0,1:T(8,128)S(1)}, f32[256,8]{0,1:T(8,128)}, u32[]{:S(2)}) copy-start(f32[256,8]{0,1:T(8,128)} %param.16) | copy-start | bytes 24580
  409.4 99.4 %all-to-all-start.1 = ((bf16[64,1,32,1024]{3,2,1,0:T(8,128)(2,1)}), bf16[64,1,32,1024]{3,2,1,0:T(8,128)(2,1)}, u32[]{:S(2)}, u32[]{:S(2)}) async-start(bf16[64,1,32,1024]{3,2,1,0:T(8,128)(2,1)} %fusion.3), calls=%async_computation.1 | async-start | bytes 8388608 | tf_op jit(solution)/shard_map/all_to_all | solution.py:271
  508.8 37.9 %copy-start.1 = (bf16[256,1024]{1,0:T(8,128)(2,1)S(1)}, bf16[256,1024]{1,0:T(8,128)(2,1)}, u32[]{:S(2)}) copy-start(bf16[256,1024]{1,0:T(8,128)(2,1)} %param.22) | copy-start | bytes 1572868
  514.5 4.0 collective-permute-start.4
  518.6 26.9 %collective-permute-start.5 = (bf16[256,1024]{1,0:T(8,128)(2,1)S(1)}, bf16[256,1024]{1,0:T(8,128)(2,1)S(1)}, u32[]{:S(2)}, u32[]{:S(2)}) collective-permute-start(bf16[256,1024]{1,0:T(8,128)(2,1)S(1)} %add_convert_fusion.1), channel_id=1, source_target_pairs={{0,2},{2,0},{1,3},{3,1},{4,6},{6,4},{5,7},{7,5},{8,10},{10,8},{9,1... | collective-permute-start | bytes 1572872 | tf_op jit(solution)/shard_map/ppermute | solution.py:161
Sparse Core Ops, SparseCore 0:
  33.2 54.4 all-gather.2
  89.4 85.5 all-gather.4

commit v8 on v7

--- a/solution.py
+++ b/solution.py
@@ -218,18 +218,6 @@
     first_chunk = jnp.sum((chunk_ends < lowest_seg).astype(jnp.int32))
     last_chunk = last_query // KEY_CHUNK
 
-    attended = chunk_attention(
-        queries, joined, segment_ids, own_segs, query_index, first_chunk, last_chunk
-    )
-    attended = (
-        attended.transpose(2, 0, 1, 3)
-        .reshape(tokens, query_heads * HEAD_DIM)
-    )
-    attended = attended.astype(jnp.bfloat16)
-    partial_out = jnp.dot(attended, w_out, preferred_element_type=jnp.float32)
-    attn_mixed = tp_sum(partial_out.astype(jnp.bfloat16))
-    residual = (hidden.astype(jnp.float32) + attn_mixed).astype(jnp.bfloat16)
-    normed_moe = normalize(residual, norm_moe).astype(jnp.bfloat16)
     route_count = routes.shape[1]
     slots_dev = w_gate.shape[0]
     seq_count = lax.axis_size(SUB_AXES)
@@ -242,18 +230,36 @@
     flat_expert = routes.reshape(copies, block_rows * route_count)
     onehot = (
         flat_expert[:, :, None] == jnp.arange(EXPERTS, dtype=jnp.int32)[None, None, :]
-    ).astype(jnp.int32)
-    before = jnp.cumsum(onehot, axis=1) - onehot
-    slot_rank = jnp.sum(before * onehot, axis=2).reshape(tokens, route_count)
-    target = slot_of * capacity + slot_rank
+    ).astype(jnp.bfloat16)
+    flat_rows = block_rows * route_count
+    strictly_before = (
+        jnp.arange(flat_rows, dtype=jnp.int32)[None, :] < jnp.arange(flat_rows, dtype=jnp.int32)[:, None]
+    ).astype(jnp.bfloat16)
+    before = jnp.einsum("ij,cje->cie", strictly_before, onehot, preferred_element_type=jnp.float32)
+    slot_rank = (
+        jnp.sum(before * onehot.astype(jnp.float32), axis=2).astype(jnp.int32).reshape(tokens, route_count)
+    )
     half = capacity // 2
     core = lax.axis_index("tc")
     swap = [(0, 1), (1, 0)]
     own_route = (slot_rank // half) == core
     local_target = jnp.where(own_route, slot_of * half + slot_rank - core * half, -1)
     row_ids = jnp.arange(slot_total * half, dtype=jnp.int32)
-    picks = local_target[None, :, :] == row_ids[:, None, None]
-    dispatch = jnp.any(picks, axis=2).astype(jnp.bfloat16)
+    picks = local_target.T[:, None, :] == row_ids[None, :, None]
+    dispatch = jnp.any(picks, axis=0).astype(jnp.bfloat16)
+    joined, local_target, dispatch = lax.optimization_barrier((joined, local_target, dispatch))
+    attended = chunk_attention(
+        queries, joined, segment_ids, own_segs, query_index, first_chunk, last_chunk
+    )
+    attended = (
+        attended.transpose(2, 0, 1, 3)
+        .reshape(tokens, query_heads * HEAD_DIM)
+    )
+    attended = attended.astype(jnp.bfloat16)
+    partial_out = jnp.dot(attended, w_out, preferred_element_type=jnp.float32)
+    attn_mixed = tp_sum(partial_out.astype(jnp.bfloat16))
+    residual = (hidden.astype(jnp.float32) + attn_mixed).astype(jnp.bfloat16)
+    normed_moe = normalize(residual, norm_moe).astype(jnp.bfloat16)
     outbound = jnp.dot(dispatch, normed_moe, preferred_element_type=jnp.float32).astype(jnp.bfloat16)
     outbound = outbound.reshape(seq_count, slots_dev, half, model_width)
     arrived_own = lax.all_to_all(outbound, SUB_AXES, split_axis=0, concat_axis=0, tiled=True)
@@ -272,7 +278,8 @@
         slot_total * half, model_width
     )
     weighting = jnp.sum(
-        jnp.where(local_target[:, :, None] == row_ids[None, None, :], gates[:, :, None], 0.0), axis=1
+        jnp.where(local_target.T[:, :, None] == row_ids[None, None, :], gates.T[:, :, None], 0.0),
+        axis=0,
     )
     combined = jnp.dot(
         weighting, returned, preferred_element_type=jnp.float32, precision=lax.Precision.HIGHEST

time: 556 us -> 538 us (0.968)
  other arithmetic: 62.9 us -> 27.4 us
  waiting for transfers between devices: 262 us -> 274 us
  blocking collectives: 150 us -> 156 us
    another operation x6 -> x3, other arithmetic: 19.3 us -> 1.15 us
    reduce_or x1, other arithmetic: 18.7 us -> 3.02 us  [per_device(): dispatch = jnp.any(picks, axis=0).astype(jnp.bfloat16)]
    ppermute x2, waiting for transfers between devices: 25.1 us -> 36.9 us  [tp_sum(): lax.ppermute(pair, 'tz', swap).astype(jnp.float32)]
    all_to_all x1, blocking collectives: 137 us -> 143 us  [per_device(): lax.all_to_all(outbound, SUB_AXES, split_axis=0, concat_axis=0, tiled=True)]
  transfers between devices with their start and end apart: 9 -> 9, of which waited for: 7 -> 9; matrix products, arithmetic and copies ran while one was open for 9% -> 3% of each run, Pallas kernels for 0% -> 0%
where the time goes in v8:
time: 538 us; the launch traced here: 535 us
  waiting for transfers between devices  274 us (51%)
  blocking collectives  156 us (29%)
  matrix products  28.2 us (5%)
  other arithmetic  27.4 us (5%)
  starting transfers between devices  19 us (4%)
  between operations  14.4 us (3%)
  local copies, waits for them, and re-layouts  9.7 us (2%)
  Pallas kernels  7.04 us (1%)
    all_to_all x1, blocking collectives, per_device(): lax.all_to_all(outbound, SUB_AXES, split_axis=0, concat_axis=0, tiled=True)  143 us
    all_gather x2, waiting for transfers between devices, per_device(): joined = lax.all_gather(joined, axis_name, axis=0, tiled=True)  131 us
    all_to_all x1, waiting for transfers between devices, per_device(): lax.all_to_all(pair_sum, SUB_AXES, split_axis=0, concat_axis=0, tiled=True)  89.5 us
    ppermute x2, waiting for transfers between devices, tp_sum(): lax.ppermute(pair, 'tz', swap).astype(jnp.float32)  36.9 us
    all_gather x1, blocking collectives, per_device(): joined = lax.all_gather(joined, axis_name, axis=0, tiled=True)  12.9 us
    dot_general x1, matrix products, per_device(): jnp.einsum('jsrf,sfd->jsrd', activated, w_down, preferred_element_type=jn...  12.6 us
  transfers between devices with their start and end apart: 9, of which 9 were waited for; matrix products, arithmetic and copies ran while one was open for 3% of the time, Pallas kernels for 0%

profile of v8, /device:TPU:1, one launch (start us, length us, event | category | flops | bytes accessed | tf_op | source)
XLA Modules:
  0.0 535.4 jit_solution(4173430039977135953)
XLA Ops:
  7.3 1.1 convert_reduce_fusion
  8.4 0.7 fusion.56
  9.0 0.7 convert_element_type.142
  9.7 1.2 fusion.21
  10.9 5.7 %fusion.44 = (f32[256]{0:T(256)S(1)}, s32[256]{0:T(256)S(1)}) fusion(s32[]{:T(128)} %bitcast.4, s32[]{:T(128)} %bitcast.5, s32[]{:T(128)} %bitcast.6, s32[]{:T(128)} %bitcast.7, s32[]{:T(128)} %bitcast.8, s32[]{:T(128)} %bitcast.9, s32[]{:T(128)} %bitcast.10, s32[]{:T(128)} %bitcast.11, s32[]{:T(128)S(6)} %mul.163, s32[16384]{0:T(1024)} %param.14, ...), kind=kLoop, calls=%fused_computation.96 | loop fusion | flops 5120 | bytes 3112 | tf_op jit(solution)/shard_map/convert_element_type | solution.py:32
  16.6 0.2 multiply_cosine_fusion
  16.8 1.5 fusion.51
  18.4 0.1 copy.74
  18.5 1.5 convolution_convert_fusion.3
  20.0 12.9 %all_gather.9 = bf16[1024,256]{1,0:T(8,128)(2,1)} all-gather(bf16[256,256]{1,0:T(8,128)(2,1)S(1)} %pad_maximum_fusion), channel_id=1, replica_groups=mesh['sy'=4,'sz'=4,'sx'=4,'tz'=2,'tc'=2] {'sx'}, dimensions={0}, use_global_device_ids=true | all-gather | bytes 655360 | tf_op jit(solution)/shard_map/all_gather | solution.py:214
  32.9 0.0 all-gather.5.cloned.1.call-start
  33.0 54.5 %all-gather.3.cloned.1.call-done = bf16[4096,256]{1,0:T(8,128)(2,1)} async-done(((bf16[1024,256]{1,0:T(8,128)(2,1)}), bf16[4096,256]{1,0:T(8,128)(2,1)}) %all-gather.3.cloned.1.call-update) | async-done | bytes 2097168 | tf_op jit(solution)/shard_map/all_gather | solution.py:214
  87.5 0.9 slice.32
  88.5 0.1 copy.75
  88.6 0.1 eq.55
  88.7 0.6 fusion.18
  89.4 0.1 convert_element_type.151
  89.5 0.1 copy.76
  89.6 3.0 fusion
  92.6 0.2 convert_element_type.152
  92.8 0.5 fusion.53
  93.4 0.2 copy.72
  93.6 0.1 broadcast_in_dim.38
  93.7 0.1 broadcast_in_dim.39
  93.7 0.5 slice.33
  94.3 0.8 copy.81.qseg_ref
  95.1 1.2 fusion.45
  96.3 1.2 pad_add_fusion.bounds_ref
  97.5 0.7 iota_add_fusion.qidx_ref
  98.2 0.7 broadcast_select_fusion.q_ref
  98.9 76.0 %all-gather.5.cloned.1.call-done.k_ref.v_ref = bf16[16384,256]{1,0:T(8,128)(2,1)} async-done(((bf16[4096,256]{1,0:T(8,128)(2,1)}), bf16[16384,256]{1,0:T(8,128)(2,1)}) %all-gather.5.cloned.1.call-update) | async-done | bytes 8388624 | tf_op jit(solution)/shard_map/all_gather | solution.py:214
  174.9 7.0 %shard_map.140 = f32[4,256,128]{2,1,0:T(8,128)} custom-call(s32[2]{0:T(128)} %pad_add_fusion.bounds_ref, bf16[2,2,256,128]{3,2,1,0:T(8,128)(2,1)} %broadcast_select_fusion.q_ref, bf16[16384,256]{1,0:T(8,128)(2,1)} %all-gather.5.cloned.1.call-done.k_ref.v_ref, bf16[16384,256]{1,0:T(8,128)(2,1)} %all-gather.5.cloned.1.call-done.k_ref.v_ref, ...), custom_call_target="tpu_custom_call" | custom-call | tf_op jit(solution)/shard_map/pallas_call | solution.py:139
  182.0 1.1 convert.27
  183.1 0.1 copy.82
  183.3 0.3 convolution_convert_fusion.2
  183.6 0.9 collective-permute-start
  184.5 1.5 collective-permute-done
  186.1 0.2 add_convert_fusion.2
  186.3 5.7 %collective-permute-start.1 = (bf16[256,1024]{1,0:T(8,128)(2,1)S(1)}, bf16[256,1024]{1,0:T(8,128)(2,1)S(1)}, u32[]{:S(2)}, u32[]{:S(2)}) collective-permute-start(bf16[256,1024]{1,0:T(8,128)(2,1)S(1)} %add_convert_fusion.2), channel_id=1, source_target_pairs={{0,2},{2,0},{1,3},{3,1},{4,6},{6,4},{5,7},{7,5},{8,10},{10,8},{9,1... | collective-permute-start | bytes 1572872 | tf_op jit(solution)/shard_map/ppermute | solution.py:161
  192.0 11.8 %collective-permute-done.1 = bf16[256,1024]{1,0:T(8,128)(2,1)S(1)} collective-permute-done((bf16[256,1024]{1,0:T(8,128)(2,1)S(1)}, bf16[256,1024]{1,0:T(8,128)(2,1)S(1)}, u32[]{:S(2)}, u32[]{:S(2)}) %collective-permute-start.1) | collective-permute-done | bytes 524320 | tf_op jit(solution)/shard_map/ppermute | solution.py:161
  203.8 0.3 fusion.25
  204.2 1.4 convolution_convert_fusion
  205.6 143.2 %all_to_all.10 = bf16[64,1,32,1024]{3,2,1,0:T(8,128)(2,1)S(1)} all-to-all(bf16[64,1,32,1024]{3,2,1,0:T(8,128)(2,1)S(1)} %bitcast.133), channel_id=1, replica_groups=mesh['sy'=4,'sz'=4,'sx'=4,'tz'=2,'tc'=2] {'sy','sz','sx'}, dimensions={0} | all-to-all | bytes 8388608 | tf_op jit(solution)/shard_map/all_to_all | solution.py:265
  348.8 2.4 collective-permute-start.2
  351.2 6.8 %collective-permute-done.2 = bf16[64,1,32,1024]{3,2,0,1:T(8,128)(2,1)S(1)} collective-permute-done((bf16[64,1,32,1024]{3,2,0,1:T(8,128)(2,1)S(1)}, bf16[64,1,32,1024]{3,2,0,1:T(8,128)(2,1)S(1)}, u32[]{:S(2)}, u32[]{:S(2)}) %collective-permute-start.2) | collective-permute-done | bytes 4194336 | tf_op jit(solution)/shard_map/ppermute | solution.py:266
  358.0 2.0 copy-done.7
  359.9 3.6 fusion.2
  363.5 12.6 %convert_bitcast_fusion = bf16[64,1,64,1024]{3,2,0,1:T(8,128)(2,1)} fusion(bf16[64,1,32,1024]{3,2,0,1:T(8,128)(2,1)} %copy-done.7, bf16[64,1,32,1024]{3,2,0,1:T(8,128)(2,1)} %bitcast.136, f32[64,64,128]{2,1,0:T(8,128)} %fusion.2, bf16[1,128,1024]{2,1,0:T(8,128)(2,1)S(1)} %copy-done.10, bf16[1,1024,128]{2,1,0:T(8,128)(2,1)S(1)} %copy-done.11), kind=kOutput, calls=%fused_computation.6 | convolution fusion | flops 2171600896 | bytes 19398656 | tf_op jit(solution)/shard_map/jsrf,sfd->jsrd/dot_general | solution.py:271
  376.1 2.9 slice.58
  379.0 0.5 collective-permute-start.3
  379.5 6.8 %collective-permute-done.3 = bf16[64,1,32,1024]{3,2,0,1:T(8,128)(2,1)S(1)} collective-permute-done((bf16[64,1,32,1024]{3,2,0,1:T(8,128)(2,1)S(1)}, bf16[64,1,32,1024]{3,2,0,1:T(8,128)(2,1)S(1)}, u32[]{:S(2)}, u32[]{:S(2)}) %collective-permute-start.3) | collective-permute-done | bytes 4194336 | tf_op jit(solution)/shard_map/ppermute | solution.py:273
  386.3 4.3 fusion.3
  390.6 6.0 %all-to-all-start.1 = ((bf16[64,1,32,1024]{3,2,1,0:T(8,128)(2,1)}), bf16[64,1,32,1024]{3,2,1,0:T(8,128)(2,1)}, u32[]{:S(2)}, u32[]{:S(2)}) async-start(bf16[64,1,32,1024]{3,2,1,0:T(8,128)(2,1)} %fusion.3), calls=%async_computation.1 | async-start | bytes 8388608 | tf_op jit(solution)/shard_map/all_to_all | solution.py:277
  396.6 4.1 select_reduce_fusion
  400.7 89.5 %all-to-all-done.1 = bf16[64,1,32,1024]{3,2,1,0:T(8,128)(2,1)} async-done(((bf16[64,1,32,1024]{3,2,1,0:T(8,128)(2,1)}), bf16[64,1,32,1024]{3,2,1,0:T(8,128)(2,1)}, u32[]{:S(2)}, u32[]{:S(2)}) %all-to-all-start.1) | async-done | bytes 4194336 | tf_op jit(solution)/shard_map/all_to_all | solution.py:277
  490.2 6.3 %convolution_convert_fusion.1 = bf16[256,1024]{1,0:T(8,128)(2,1)S(1)} fusion(f32[256,2048]{1,0:T(8,128)} %select_reduce_fusion, bf16[2048,1024]{1,0:T(8,128)(2,1)} %bitcast.56), kind=kOutput, calls=%fused_computation.28 | convolution fusion | flops 6442713088 | bytes 6815744 | tf_op jit(solution)/shard_map/dot_general | solution.py:284
  496.4 2.4 collective-permute-start.4
  498.9 1.5 collective-permute-done.4
  500.4 0.2 add_convert_fusion.1
  500.6 0.9 collective-permute-start.5
  501.5 0.1 copy.87
  501.7 0.8 copy.88
  502.5 25.1 %collective-permute-done.5 = bf16[256,1024]{1,0:T(8,128)(2,1)S(1)} collective-permute-done((bf16[256,1024]{1,0:T(8,128)(2,1)S(1)}, bf16[256,1024]{1,0:T(8,128)(2,1)S(1)}, u32[]{:S(2)}, u32[]{:S(2)}) %collective-permute-start.5) | collective-permute-done | bytes 524320 | tf_op jit(solution)/shard_map/ppermute | solution.py:161
  527.5 1.1 fusion.28
  (43 shorter events, 0.4 us)
Async XLA Ops:
  7.2 176.1 %copy-start = (bf16[256,1024]{1,0:T(8,128)(2,1)S(1)}, bf16[256,1024]{1,0:T(8,128)(2,1)}, u32[]{:S(2)}) copy-start(bf16[256,1024]{1,0:T(8,128)(2,1)} %param.22) | copy-start | bytes 1572868
  7.2 81.3 %copy-start.4 = (s32[256,8]{0,1:T(8,128)S(1)}, s32[256,8]{0,1:T(8,128)}, u32[]{:S(2)}) copy-start(s32[256,8]{0,1:T(8,128)} %param.15) | copy-start | bytes 24580
  7.2 80.3 %all-gather.3.cloned.1.call-start = ((), (), s32[]{:S(2)}) async-start(), calls=%async_computation.2 | async-start | bytes 2621440 | tf_op jit(solution)/shard_map/all_gather | solution.py:214
  20.0 72.9 %copy-start.3 = (bf16[256,1024]{1,0:T(8,128)(2,1)S(1)}, bf16[256,1024]{1,0:T(8,128)(2,1)}, u32[]{:S(2)}) copy-start(bf16[256,1024]{1,0:T(8,128)(2,1)} %param.13) | copy-start | bytes 1572868
  20.0 72.9 %copy-start.8 = (bf16[1024,256]{1,0:T(8,128)(2,1)S(1)}, bf16[1024,256]{1,0:T(8,128)(2,1)}, u32[]{:S(2)}) copy-start(bf16[1024,256]{1,0:T(8,128)(2,1)} %param.19) | copy-start | bytes 1572868
  32.9 142.0 %all-gather.5.cloned.1.call-start = ((), (), s32[]{:S(2)}) async-start(), calls=%async_computation.3 | async-start | bytes 10485760 | tf_op jit(solution)/shard_map/all_gather | solution.py:214
  182.0 10.0 %copy-start.6 = (bf16[1024]{0:T(1024)(128)(2,1)S(1)}, bf16[1024]{0:T(1024)(128)(2,1)}, u32[]{:S(2)}) copy-start(bf16[1024]{0:T(1024)(128)(2,1)} %param.18) | copy-start | bytes 6148
  183.6 2.5 collective-permute-start
  186.3 17.6 %collective-permute-start.1 = (bf16[256,1024]{1,0:T(8,128)(2,1)S(1)}, bf16[256,1024]{1,0:T(8,128)(2,1)S(1)}, u32[]{:S(2)}, u32[]{:S(2)}) collective-permute-start(bf16[256,1024]{1,0:T(8,128)(2,1)S(1)} %add_convert_fusion.2), channel_id=1, source_target_pairs={{0,2},{2,0},{1,3},{3,1},{4,6},{6,4},{5,7},{7,5},{8,10},{10,8},{9,1... | collective-permute-start | bytes 1572872 | tf_op jit(solution)/shard_map/ppermute | solution.py:161
  205.6 154.4 %copy-start.9 = (bf16[1,1024,128]{2,1,0:T(8,128)(2,1)S(1)}, bf16[1,1024,128]{2,1,0:T(8,128)(2,1)}, u32[]{:S(2)}) copy-start(bf16[1,1024,128]{2,1,0:T(8,128)(2,1)} %param.23) | copy-start | bytes 786436
  348.8 9.2 %copy-start.2 = (bf16[64,1,32,1024]{3,2,1,0:T(8,128)(2,1)}, bf16[64,1,32,1024]{3,2,1,0:T(8,128)(2,1)S(1)}, u32[]{:S(2)}) copy-start(bf16[64,1,32,1024]{3,2,1,0:T(8,128)(2,1)S(1)} %all_to_all.10) | copy-start | bytes 12582916
  348.8 14.7 %copy-start.10 = (bf16[1,128,1024]{2,1,0:T(8,128)(2,1)S(1)}, bf16[1,128,1024]{2,1,0:T(8,128)(2,1)}, u32[]{:S(2)}) copy-start(bf16[1,128,1024]{2,1,0:T(8,128)(2,1)} %param.25) | copy-start | bytes 786436
  348.8 14.7 %copy-start.11 = (bf16[1,1024,128]{2,1,0:T(8,128)(2,1)S(1)}, bf16[1,1024,128]{2,1,0:T(8,128)(2,1)}, u32[]{:S(2)}) copy-start(bf16[1,1024,128]{2,1,0:T(8,128)(2,1)} %param.24) | copy-start | bytes 786436
  348.8 9.2 %collective-permute-start.2 = (bf16[64,1,32,1024]{3,2,0,1:T(8,128)(2,1)S(1)}, bf16[64,1,32,1024]{3,2,0,1:T(8,128)(2,1)S(1)}, u32[]{:S(2)}, u32[]{:S(2)}) collective-permute-start(bf16[64,1,32,1024]{3,2,0,1:T(8,128)(2,1)S(1)} %bitcast.134), channel_id=1, source_target_pairs={{0,1},{1,0},{2,3},{3,2},{4,5},{5,4},{6,7},{7,6},{8,9},{9,8},{10,11... | collective-permute-start | bytes 12582920 | tf_op jit(solution)/shard_map/ppermute | solution.py:266
  358.0 2.0 copy-start.7
  376.1 10.1 %copy-start.1 = (bf16[64,1,64,1024]{3,2,0,1:T(8,128)(2,1)S(1)}, bf16[64,1,64,1024]{3,2,0,1:T(8,128)(2,1)}, u32[]{:S(2)}) copy-start(bf16[64,1,64,1024]{3,2,0,1:T(8,128)(2,1)} %convert_bitcast_fusion) | copy-start | bytes 25165828
  379.0 7.3 %collective-permute-start.3 = (bf16[64,1,32,1024]{3,2,0,1:T(8,128)(2,1)S(1)}, bf16[64,1,32,1024]{3,2,0,1:T(8,128)(2,1)S(1)}, u32[]{:S(2)}, u32[]{:S(2)}) collective-permute-start(bf16[64,1,32,1024]{3,2,0,1:T(8,128)(2,1)S(1)} %slice.58), channel_id=1, source_target_pairs={{0,1},{1,0},{2,3},{3,2},{4,5},{5,4},{6,7},{7,6},{8,9},{9,8},{10,11... | collective-permute-start | bytes 12582920 | tf_op jit(solution)/shard_map/ppermute | solution.py:273
  390.6 6.0 %copy-start.5 = (f32[256,8]{0,1:T(8,128)S(1)}, f32[256,8]{0,1:T(8,128)}, u32[]{:S(2)}) copy-start(f32[256,8]{0,1:T(8,128)} %param.16) | copy-start | bytes 24580
  390.6 99.6 %all-to-all-start.1 = ((bf16[64,1,32,1024]{3,2,1,0:T(8,128)(2,1)}), bf16[64,1,32,1024]{3,2,1,0:T(8,128)(2,1)}, u32[]{:S(2)}, u32[]{:S(2)}) async-start(bf16[64,1,32,1024]{3,2,1,0:T(8,128)(2,1)} %fusion.3), calls=%async_computation.1 | async-start | bytes 8388608 | tf_op jit(solution)/shard_map/all_to_all | solution.py:277
  496.4 4.0 collective-permute-start.4
  500.6 26.9 %collective-permute-start.5 = (bf16[256,1024]{1,0:T(8,128)(2,1)S(1)}, bf16[256,1024]{1,0:T(8,128)(2,1)S(1)}, u32[]{:S(2)}, u32[]{:S(2)}) collective-permute-start(bf16[256,1024]{1,0:T(8,128)(2,1)S(1)} %add_convert_fusion.1), channel_id=1, source_target_pairs={{0,2},{2,0},{1,3},{3,1},{4,6},{6,4},{5,7},{7,5},{8,10},{10,8},{9,1... | collective-permute-start | bytes 1572872 | tf_op jit(solution)/shard_map/ppermute | solution.py:161
Sparse Core Ops, SparseCore 0:
  33.1 54.4 all-gather.2
  89.3 85.5 all-gather.4

commit v9 on v8

--- a/solution.py
+++ b/solution.py
@@ -264,14 +264,16 @@
     outbound = outbound.reshape(seq_count, slots_dev, half, model_width)
     arrived_own = lax.all_to_all(outbound, SUB_AXES, split_axis=0, concat_axis=0, tiled=True)
     arrived_other = lax.ppermute(arrived_own, "tc", swap)
-    arrived = jnp.concatenate([arrived_own, arrived_other], axis=2)
-    gate_val = jnp.einsum("jsrd,sdf->jsrf", arrived, w_gate, preferred_element_type=jnp.float32)
-    up_val = jnp.einsum("jsrd,sdf->jsrf", arrived, w_up, preferred_element_type=jnp.float32)
-    activated = (jax.nn.silu(gate_val) * up_val).astype(jnp.bfloat16)
-    group_part = jnp.einsum("jsrf,sfd->jsrd", activated, w_down, preferred_element_type=jnp.float32)
-    result = group_part.astype(jnp.bfloat16)
-    sibling_part = lax.ppermute(result[:, :, half:], "tc", swap)
-    pair_sum = (result[:, :, :half].astype(jnp.float32) + sibling_part.astype(jnp.float32)).astype(
+    def expert_rows(arrived):
+        gate_val = jnp.einsum("jsrd,sdf->jsrf", arrived, w_gate, preferred_element_type=jnp.float32)
+        up_val = jnp.einsum("jsrd,sdf->jsrf", arrived, w_up, preferred_element_type=jnp.float32)
+        activated = (jax.nn.silu(gate_val) * up_val).astype(jnp.bfloat16)
+        group_part = jnp.einsum("jsrf,sfd->jsrd", activated, w_down, preferred_element_type=jnp.float32)
+        return group_part.astype(jnp.bfloat16)
+
+    sibling_part = lax.ppermute(expert_rows(arrived_other), "tc", swap)
+    own_part = expert_rows(arrived_own)
+    pair_sum = (own_part.astype(jnp.float32) + sibling_part.astype(jnp.float32)).astype(
         jnp.bfloat16
     )
     returned = lax.all_to_all(pair_sum, SUB_AXES, split_axis=0, concat_axis=0, tiled=True).reshape(

time: 538 us -> 535 us (level)
  matrix products: 28.2 us -> 35.5 us
    dot_general x2 -> x4, matrix products: 16.2 us -> 22.5 us  [the longest x2 17.8 us: expert_rows(): jnp.einsum('jsrf,sfd->jsrd', activated, w_down, preferred_element_type=jn...]
  transfers between devices with their start and end apart: 9 -> 9, of which waited for: 9 -> 9; matrix products, arithmetic and copies ran while one was open for 3% -> 4% of each run, Pallas kernels for 0% -> 0%
where the time goes in v9:
time: 535 us; the launch traced here: 533 us
  waiting for transfers between devices  270 us (50%)
  blocking collectives  156 us (29%)
  matrix products  35.5 us (7%)
  other arithmetic  23.1 us (4%)
  starting transfers between devices  18.7 us (3%)
  between operations  14.4 us (3%)
  local copies, waits for them, and re-layouts  8.75 us (2%)
  Pallas kernels  7.05 us (1%)
    all_to_all x1, blocking collectives, per_device(): lax.all_to_all(outbound, SUB_AXES, split_axis=0, concat_axis=0, tiled=True)  143 us
    all_gather x2, waiting for transfers between devices, per_device(): joined = lax.all_gather(joined, axis_name, axis=0, tiled=True)  130 us
    all_to_all x1, waiting for transfers between devices, per_device(): lax.all_to_all(pair_sum, SUB_AXES, split_axis=0, concat_axis=0, tiled=True)  89.5 us
    ppermute x2, waiting for transfers between devices, tp_sum(): lax.ppermute(pair, 'tz', swap).astype(jnp.float32)  36.9 us
    dot_general x2, matrix products, expert_rows(): jnp.einsum('jsrf,sfd->jsrd', activated, w_down, preferred_element_type=jn...  17.8 us
    all_gather x1, blocking collectives, per_device(): joined = lax.all_gather(joined, axis_name, axis=0, tiled=True)  12.9 us
  transfers between devices with their start and end apart: 9, of which 9 were waited for; matrix products, arithmetic and copies ran while one was open for 4% of the time, Pallas kernels for 0%

profile of v9, /device:TPU:1, one launch (start us, length us, event | category | flops | bytes accessed | tf_op | source)
XLA Modules:
  0.0 533.2 jit_solution(6317930992444327332)
XLA Ops:
  7.3 1.1 convert_reduce_fusion
  8.4 0.7 fusion.93
  9.0 0.7 convert_element_type.160
  9.7 1.2 fusion.46
  10.9 5.8 %fusion.83 = (f32[256]{0:T(256)S(1)}, s32[256]{0:T(256)S(1)}) fusion(s32[]{:T(128)} %bitcast.4, s32[]{:T(128)} %bitcast.5, s32[]{:T(128)} %bitcast.6, s32[]{:T(128)} %bitcast.7, s32[]{:T(128)} %bitcast.8, s32[]{:T(128)} %bitcast.9, s32[]{:T(128)} %bitcast.10, s32[]{:T(128)} %bitcast.11, s32[]{:T(128)S(6)} %mul.169, s32[16384]{0:T(1024)} %param.14, ...), kind=kLoop, calls=%fused_computation.111 | loop fusion | flops 5120 | bytes 3112 | tf_op jit(solution)/shard_map/convert_element_type | solution.py:32
  16.7 0.2 multiply_cosine_fusion
  16.9 1.5 fusion.88
  18.5 0.1 copy.72
  18.6 1.5 convolution_convert_fusion.3
  20.1 12.9 %all_gather.9 = bf16[1024,256]{1,0:T(8,128)(2,1)} all-gather(bf16[256,256]{1,0:T(8,128)(2,1)S(1)} %pad_maximum_fusion), channel_id=1, replica_groups=mesh['sy'=4,'sz'=4,'sx'=4,'tz'=2,'tc'=2] {'sx'}, dimensions={0}, use_global_device_ids=true | all-gather | bytes 655360 | tf_op jit(solution)/shard_map/all_gather | solution.py:214
  33.1 54.5 %all-gather.3.cloned.1.call-done = bf16[4096,256]{1,0:T(8,128)(2,1)} async-done(((bf16[1024,256]{1,0:T(8,128)(2,1)}), bf16[4096,256]{1,0:T(8,128)(2,1)}) %all-gather.3.cloned.1.call-update) | async-done | bytes 2097168 | tf_op jit(solution)/shard_map/all_gather | solution.py:214
  87.6 0.9 slice.26
  88.6 0.1 copy.73
  88.7 0.1 eq.55
  88.8 0.6 fusion.41
  89.4 0.1 convert_element_type.169
  89.5 0.1 copy.74
  89.6 3.0 fusion
  92.7 0.2 convert_element_type.170
  92.9 1.5 fusion.90
  94.5 0.2 copy.70
  94.7 0.1 broadcast_in_dim.38
  94.8 0.1 broadcast_in_dim.39
  94.8 0.5 slice.27
  95.3 0.8 copy.79.qseg_ref
  96.1 1.2 fusion.84
  97.3 1.2 pad_add_fusion.bounds_ref
  98.5 0.7 iota_add_fusion.qidx_ref
  99.2 0.7 broadcast_select_fusion.q_ref
  99.9 75.1 %all-gather.5.cloned.1.call-done.k_ref.v_ref = bf16[16384,256]{1,0:T(8,128)(2,1)} async-done(((bf16[4096,256]{1,0:T(8,128)(2,1)}), bf16[16384,256]{1,0:T(8,128)(2,1)}) %all-gather.5.cloned.1.call-update) | async-done | bytes 8388624 | tf_op jit(solution)/shard_map/all_gather | solution.py:214
  175.0 7.0 %shard_map.140 = f32[4,256,128]{2,1,0:T(8,128)} custom-call(s32[2]{0:T(128)} %pad_add_fusion.bounds_ref, bf16[2,2,256,128]{3,2,1,0:T(8,128)(2,1)} %broadcast_select_fusion.q_ref, bf16[16384,256]{1,0:T(8,128)(2,1)} %all-gather.5.cloned.1.call-done.k_ref.v_ref, bf16[16384,256]{1,0:T(8,128)(2,1)} %all-gather.5.cloned.1.call-done.k_ref.v_ref, ...), custom_call_target="tpu_custom_call" | custom-call | tf_op jit(solution)/shard_map/pallas_call | solution.py:139
  182.1 1.1 convert.30
  183.2 0.1 copy.80
  183.4 0.3 convolution_convert_fusion.2
  183.7 0.9 collective-permute-start
  184.6 1.5 collective-permute-done
  186.2 0.2 add_convert_fusion.1
  186.4 5.7 %collective-permute-start.1 = (bf16[256,1024]{1,0:T(8,128)(2,1)S(1)}, bf16[256,1024]{1,0:T(8,128)(2,1)S(1)}, u32[]{:S(2)}, u32[]{:S(2)}) collective-permute-start(bf16[256,1024]{1,0:T(8,128)(2,1)S(1)} %add_convert_fusion.1), channel_id=1, source_target_pairs={{0,2},{2,0},{1,3},{3,1},{4,6},{6,4},{5,7},{7,5},{8,10},{10,8},{9,1... | collective-permute-start | bytes 1572872 | tf_op jit(solution)/shard_map/ppermute | solution.py:161
  192.1 11.8 %collective-permute-done.1 = bf16[256,1024]{1,0:T(8,128)(2,1)S(1)} collective-permute-done((bf16[256,1024]{1,0:T(8,128)(2,1)S(1)}, bf16[256,1024]{1,0:T(8,128)(2,1)S(1)}, u32[]{:S(2)}, u32[]{:S(2)}) %collective-permute-start.1) | collective-permute-done | bytes 524320 | tf_op jit(solution)/shard_map/ppermute | solution.py:161
  203.9 0.3 fusion.50
  204.2 1.4 convolution_convert_fusion
  205.6 143.2 %all_to_all.10 = bf16[64,1,32,1024]{3,2,1,0:T(8,128)(2,1)S(1)} all-to-all(bf16[64,1,32,1024]{3,2,1,0:T(8,128)(2,1)S(1)} %bitcast.172), channel_id=1, replica_groups=mesh['sy'=4,'sz'=4,'sx'=4,'tz'=2,'tc'=2] {'sy','sz','sx'}, dimensions={0} | all-to-all | bytes 8388608 | tf_op jit(solution)/shard_map/all_to_all | solution.py:265
  348.9 1.9 copy-done.1
  350.8 2.4 collective-permute-start.2
  353.2 6.8 %collective-permute-done.2 = bf16[64,1,32,1024]{3,2,0,1:T(8,128)(2,1)S(1)} collective-permute-done((bf16[64,1,32,1024]{3,2,0,1:T(8,128)(2,1)S(1)}, bf16[64,1,32,1024]{3,2,0,1:T(8,128)(2,1)S(1)}, u32[]{:S(2)}, u32[]{:S(2)}) %collective-permute-start.2) | collective-permute-done | bytes 4194336 | tf_op jit(solution)/shard_map/ppermute | solution.py:266
  360.0 2.0 copy-done.2
  362.0 1.3 fusion.20
  363.3 8.2 %convert_bitcast_fusion = bf16[64,1,32,1024]{3,2,0,1:T(8,128)(2,1)} fusion(f32[64,1,32,128]{3,2,0,1:T(8,128)S(1)} %fusion.20, bf16[64,1,32,1024]{3,2,0,1:T(8,128)(2,1)} %copy-done.2, bf16[1,128,1024]{2,1,0:T(8,128)(2,1)S(1)} %copy-done.5, bf16[1,1024,128]{2,1,0:T(8,128)(2,1)S(1)} %copy-done.6), kind=kOutput, calls=%fused_computation.15 | convolution fusion | flops 1077411840 | bytes 9961472 | tf_op jit(solution)/shard_map/jsrf,sfd->jsrd/dot_general | solution.py:271
  371.5 0.4 collective-permute-start.3
  371.9 3.4 fusion.14
  375.3 3.7 collective-permute-done.3
  379.0 9.5 %fusion.2 = bf16[64,1,32,1024]{3,2,1,0:T(8,128)(2,1)} fusion(bf16[64,1,32,1024]{3,2,0,1:T(8,128)(2,1)} %collective-permute-done.3, bf16[64,1,32,1024]{3,2,1,0:T(8,128)(2,1)} %copy-done.1, f32[64,1,32,128]{3,2,0,1:T(8,128)S(1)} %fusion.14, bf16[1,128,1024]{2,1,0:T(8,128)(2,1)S(1)} %copy-done.5, bf16[1,1024,128]{2,1,0:T(8,128)(2,1)S(1)} %copy-done.6), kind=kOutput, calls=%fused_computation.6 | convolution fusion | flops 1085800448 | bytes 14155776 | tf_op jit(solution)/shard_map/jsrf,sfd->jsrd/dot_general | solution.py:271
  388.5 5.8 %all-to-all-start.1 = ((bf16[64,1,32,1024]{3,2,1,0:T(8,128)(2,1)}), bf16[64,1,32,1024]{3,2,1,0:T(8,128)(2,1)}, u32[]{:S(2)}, u32[]{:S(2)}) async-start(bf16[64,1,32,1024]{3,2,1,0:T(8,128)(2,1)} %fusion.2), calls=%async_computation.1 | async-start | bytes 8388608 | tf_op jit(solution)/shard_map/all_to_all | solution.py:279
  394.4 4.1 select_reduce_fusion
  398.4 89.5 %all-to-all-done.1 = bf16[64,1,32,1024]{3,2,1,0:T(8,128)(2,1)} async-done(((bf16[64,1,32,1024]{3,2,1,0:T(8,128)(2,1)}), bf16[64,1,32,1024]{3,2,1,0:T(8,128)(2,1)}, u32[]{:S(2)}, u32[]{:S(2)}) %all-to-all-start.1) | async-done | bytes 4194336 | tf_op jit(solution)/shard_map/all_to_all | solution.py:279
  487.9 6.3 %convolution_convert_fusion.1 = bf16[256,1024]{1,0:T(8,128)(2,1)S(1)} fusion(f32[256,2048]{1,0:T(8,128)} %select_reduce_fusion, bf16[2048,1024]{1,0:T(8,128)(2,1)} %bitcast.66), kind=kOutput, calls=%fused_computation.31 | convolution fusion | flops 6442713088 | bytes 6815744 | tf_op jit(solution)/shard_map/dot_general | solution.py:286
  494.2 2.4 collective-permute-start.4
  496.6 1.5 collective-permute-done.4
  498.2 0.2 add_convert_fusion
  498.4 0.9 collective-permute-start.5
  499.3 0.1 copy.84
  499.4 0.8 copy.85
  500.2 25.1 %collective-permute-done.5 = bf16[256,1024]{1,0:T(8,128)(2,1)S(1)} collective-permute-done((bf16[256,1024]{1,0:T(8,128)(2,1)S(1)}, bf16[256,1024]{1,0:T(8,128)(2,1)S(1)}, u32[]{:S(2)}, u32[]{:S(2)}) %collective-permute-start.5) | collective-permute-done | bytes 524320 | tf_op jit(solution)/shard_map/ppermute | solution.py:161
  525.3 1.1 fusion.53
  (39 shorter events, 0.4 us)
Async XLA Ops:
  7.2 176.2 %copy-start = (bf16[256,1024]{1,0:T(8,128)(2,1)S(1)}, bf16[256,1024]{1,0:T(8,128)(2,1)}, u32[]{:S(2)}) copy-start(bf16[256,1024]{1,0:T(8,128)(2,1)} %param.22) | copy-start | bytes 1572868
  7.2 81.4 %copy-start.7 = (s32[256,8]{0,1:T(8,128)S(1)}, s32[256,8]{0,1:T(8,128)}, u32[]{:S(2)}) copy-start(s32[256,8]{0,1:T(8,128)} %param.15) | copy-start | bytes 24580
  7.2 80.4 %all-gather.3.cloned.1.call-start = ((), (), s32[]{:S(2)}) async-start(), calls=%async_computation.2 | async-start | bytes 2621440 | tf_op jit(solution)/shard_map/all_gather | solution.py:214
  20.0 72.9 %copy-start.3 = (bf16[256,1024]{1,0:T(8,128)(2,1)S(1)}, bf16[256,1024]{1,0:T(8,128)(2,1)}, u32[]{:S(2)}) copy-start(bf16[256,1024]{1,0:T(8,128)(2,1)} %param.13) | copy-start | bytes 1572868
  33.0 142.0 %all-gather.5.cloned.1.call-start = ((), (), s32[]{:S(2)}) async-start(), calls=%async_computation.3 | async-start | bytes 10485760 | tf_op jit(solution)/shard_map/all_gather | solution.py:214
  182.1 10.0 %copy-start.9 = (bf16[1024]{0:T(1024)(128)(2,1)S(1)}, bf16[1024]{0:T(1024)(128)(2,1)}, u32[]{:S(2)}) copy-start(bf16[1024]{0:T(1024)(128)(2,1)} %param.18) | copy-start | bytes 6148
  183.7 2.5 collective-permute-start
  186.4 17.5 %collective-permute-start.1 = (bf16[256,1024]{1,0:T(8,128)(2,1)S(1)}, bf16[256,1024]{1,0:T(8,128)(2,1)S(1)}, u32[]{:S(2)}, u32[]{:S(2)}) collective-permute-start(bf16[256,1024]{1,0:T(8,128)(2,1)S(1)} %add_convert_fusion.1), channel_id=1, source_target_pairs={{0,2},{2,0},{1,3},{3,1},{4,6},{6,4},{5,7},{7,5},{8,10},{10,8},{9,1... | collective-permute-start | bytes 1572872 | tf_op jit(solution)/shard_map/ppermute | solution.py:161
  205.6 156.3 %copy-start.4 = (bf16[1,1024,128]{2,1,0:T(8,128)(2,1)S(1)}, bf16[1,1024,128]{2,1,0:T(8,128)(2,1)}, u32[]{:S(2)}) copy-start(bf16[1,1024,128]{2,1,0:T(8,128)(2,1)} %param.23) | copy-start | bytes 786436
  348.8 1.9 copy-start.1
  348.8 14.4 %copy-start.5 = (bf16[1,128,1024]{2,1,0:T(8,128)(2,1)S(1)}, bf16[1,128,1024]{2,1,0:T(8,128)(2,1)}, u32[]{:S(2)}) copy-start(bf16[1,128,1024]{2,1,0:T(8,128)(2,1)} %param.25) | copy-start | bytes 786436
  348.8 14.4 %copy-start.6 = (bf16[1,1024,128]{2,1,0:T(8,128)(2,1)S(1)}, bf16[1,1024,128]{2,1,0:T(8,128)(2,1)}, u32[]{:S(2)}) copy-start(bf16[1,1024,128]{2,1,0:T(8,128)(2,1)} %param.24) | copy-start | bytes 786436
  350.8 9.2 %collective-permute-start.2 = (bf16[64,1,32,1024]{3,2,0,1:T(8,128)(2,1)S(1)}, bf16[64,1,32,1024]{3,2,0,1:T(8,128)(2,1)S(1)}, u32[]{:S(2)}, u32[]{:S(2)}) collective-permute-start(bf16[64,1,32,1024]{3,2,0,1:T(8,128)(2,1)S(1)} %bitcast.173), channel_id=1, source_target_pairs={{0,1},{1,0},{2,3},{3,2},{4,5},{5,4},{6,7},{7,6},{8,9},{9,8},{10,11... | collective-permute-start | bytes 12582920 | tf_op jit(solution)/shard_map/ppermute | solution.py:266
  360.0 2.0 copy-start.2
  371.5 7.5 %collective-permute-start.3 = (bf16[64,1,32,1024]{3,2,0,1:T(8,128)(2,1)}, bf16[64,1,32,1024]{3,2,0,1:T(8,128)(2,1)}, u32[]{:S(2)}, u32[]{:S(2)}) collective-permute-start(bf16[64,1,32,1024]{3,2,0,1:T(8,128)(2,1)} %convert_bitcast_fusion), channel_id=1, source_target_pairs={{0,1},{1,0},{2,3},{3,2},{4,5},{5,4},{6,7},{7,6},{8,9},{9,8},{10,11... | collective-permute-start | bytes 12582920 | tf_op jit(solution)/shard_map/ppermute | solution.py:274
  388.5 5.8 %copy-start.8 = (f32[256,8]{0,1:T(8,128)S(1)}, f32[256,8]{0,1:T(8,128)}, u32[]{:S(2)}) copy-start(f32[256,8]{0,1:T(8,128)} %param.16) | copy-start | bytes 24580
  388.5 99.4 %all-to-all-start.1 = ((bf16[64,1,32,1024]{3,2,1,0:T(8,128)(2,1)}), bf16[64,1,32,1024]{3,2,1,0:T(8,128)(2,1)}, u32[]{:S(2)}, u32[]{:S(2)}) async-start(bf16[64,1,32,1024]{3,2,1,0:T(8,128)(2,1)} %fusion.2), calls=%async_computation.1 | async-start | bytes 8388608 | tf_op jit(solution)/shard_map/all_to_all | solution.py:279
  494.2 4.0 collective-permute-start.4
  498.4 26.9 %collective-permute-start.5 = (bf16[256,1024]{1,0:T(8,128)(2,1)S(1)}, bf16[256,1024]{1,0:T(8,128)(2,1)S(1)}, u32[]{:S(2)}, u32[]{:S(2)}) collective-permute-start(bf16[256,1024]{1,0:T(8,128)(2,1)S(1)} %add_convert_fusion), channel_id=1, source_target_pairs={{0,2},{2,0},{1,3},{3,1},{4,6},{6,4},{5,7},{7,5},{8,10},{10,8},{9,1... | collective-permute-start | bytes 1572872 | tf_op jit(solution)/shard_map/ppermute | solution.py:161
Sparse Core Ops, SparseCore 0:
  33.1 54.4 all-gather.2
  89.4 85.5 all-gather.4

commit v10 on v9

--- a/solution.py
+++ b/solution.py
@@ -156,9 +156,20 @@
 
 def tp_sum(partial):
     swap = [(0, 1), (1, 0)]
-    pair = partial.astype(jnp.float32) + lax.ppermute(partial, "tc", swap).astype(jnp.float32)
+    core = lax.axis_index("tc")
+    rows, width = partial.shape
+    halves = partial.reshape(rows, 2, width // 2)
+    mine = lax.dynamic_index_in_dim(halves, core, axis=1, keepdims=False)
+    theirs = lax.dynamic_index_in_dim(halves, 1 - core, axis=1, keepdims=False)
+    pair = mine.astype(jnp.float32) + lax.ppermute(theirs, "tc", swap).astype(jnp.float32)
     pair = pair.astype(jnp.bfloat16)
-    return pair.astype(jnp.float32) + lax.ppermute(pair, "tz", swap).astype(jnp.float32)
+    summed = pair.astype(jnp.float32) + lax.ppermute(pair, "tz", swap).astype(jnp.float32)
+    other = lax.ppermute(summed, "tc", swap)
+    return jnp.where(
+        core == 0,
+        jnp.concatenate([summed, other], axis=1),
+        jnp.concatenate([other, summed], axis=1),
+    )
 
 
 def per_device(

time: 535 us -> 523 us (0.978)
  waiting for transfers between devices: 270 us -> 255 us
    ppermute x2, waiting for transfers between devices: 36.9 us -> 20.9 us  [tp_sum(): lax.ppermute(pair, 'tz', swap).astype(jnp.float32)]
  transfers between devices with their start and end apart: 9 -> 11, of which waited for: 9 -> 11; matrix products, arithmetic and copies ran while one was open for 4% -> 4% of each run, Pallas kernels for 0% -> 0%
where the time goes in v10:
time: 523 us
  waiting for transfers between devices  255 us (49%)
  blocking collectives  153 us (29%)
  matrix products  35.5 us (7%)
  other arithmetic  24.4 us (5%)
  starting transfers between devices  22.3 us (4%)
  between operations  14.5 us (3%)
  local copies, waits for them, and re-layouts  11.8 us (2%)
  Pallas kernels  7.04 us (1%)
    all_to_all x1, blocking collectives, per_device(): lax.all_to_all(outbound, SUB_AXES, split_axis=0, concat_axis=0, tiled=True)  140 us
    all_gather x2, waiting for transfers between devices, per_device(): joined = lax.all_gather(joined, axis_name, axis=0, tiled=True)  129 us
    all_to_all x1, waiting for transfers between devices, per_device(): lax.all_to_all(pair_sum, SUB_AXES, split_axis=0, concat_axis=0, tiled=True)  89.5 us
    ppermute x2, waiting for transfers between devices, tp_sum(): lax.ppermute(pair, 'tz', swap).astype(jnp.float32)  20.9 us
    dot_general x2, matrix products, expert_rows(): jnp.einsum('jsrf,sfd->jsrd', activated, w_down, preferred_element_type=jn...  17.8 us
    all_gather x1, blocking collectives, per_device(): joined = lax.all_gather(joined, axis_name, axis=0, tiled=True)  12.9 us
  transfers between devices with their start and end apart: 11, of which 11 were waited for; matrix products, arithmetic and copies ran while one was open for 4% of the time, Pallas kernels for 0%

profile of v10, /device:TPU:1, one launch (start us, length us, event | category | flops | bytes accessed | tf_op | source)
XLA Modules:
  0.0 523.4 jit_solution(13852499713302712868)
XLA Ops:
  7.3 1.1 convert_reduce_fusion
  8.4 0.7 fusion.95
  9.0 0.7 convert_element_type.166
  9.7 1.2 fusion.46
  11.0 5.9 %fusion.85 = (f32[256]{0:T(256)S(1)}, s32[256]{0:T(256)S(1)}) fusion(s32[]{:T(128)} %bitcast.4, s32[]{:T(128)} %bitcast.5, s32[]{:T(128)} %bitcast.6, s32[]{:T(128)} %bitcast.7, s32[]{:T(128)} %bitcast.8, s32[]{:T(128)} %bitcast.9, s32[]{:T(128)} %bitcast.10, s32[]{:T(128)} %bitcast.11, s32[]{:T(128)S(6)} %mul.169, s32[16384]{0:T(1024)} %param.14, ...), kind=kLoop, calls=%fused_computation.121 | loop fusion | flops 5120 | bytes 3112 | tf_op jit(solution)/shard_map/convert_element_type | solution.py:32
  16.8 0.2 multiply_cosine_fusion
  17.0 1.5 fusion.90
  18.7 1.5 convolution_convert_fusion.3
  20.2 12.9 %all_gather.9 = bf16[1024,256]{1,0:T(8,128)(2,1)} all-gather(bf16[256,256]{1,0:T(8,128)(2,1)S(1)} %pad_maximum_fusion), channel_id=1, replica_groups=mesh['sy'=4,'sz'=4,'sx'=4,'tz'=2,'tc'=2] {'sx'}, dimensions={0}, use_global_device_ids=true | all-gather | bytes 655360 | tf_op jit(solution)/shard_map/all_gather | solution.py:225
  33.2 54.5 %all-gather.3.cloned.1.call-done = bf16[4096,256]{1,0:T(8,128)(2,1)} async-done(((bf16[1024,256]{1,0:T(8,128)(2,1)}), bf16[4096,256]{1,0:T(8,128)(2,1)}) %all-gather.3.cloned.1.call-update) | async-done | bytes 2097168 | tf_op jit(solution)/shard_map/all_gather | solution.py:225
  87.7 0.9 slice.26
  88.7 0.1 copy.87
  88.8 0.1 eq.60
  88.9 0.6 fusion.41
  89.8 3.0 fusion
  92.8 0.2 convert_element_type.176
  93.0 1.5 fusion.92
  94.6 0.2 copy.84
  95.0 0.5 slice.27
  95.5 0.8 copy.93.qseg_ref
  96.3 1.3 fusion.86
  97.6 1.2 pad_add_fusion.bounds_ref
  98.8 0.7 iota_add_fusion.qidx_ref
  99.5 0.7 broadcast_select_fusion.q_ref
  100.2 74.9 %all-gather.5.cloned.1.call-done.k_ref.v_ref = bf16[16384,256]{1,0:T(8,128)(2,1)} async-done(((bf16[4096,256]{1,0:T(8,128)(2,1)}), bf16[16384,256]{1,0:T(8,128)(2,1)}) %all-gather.5.cloned.1.call-update) | async-done | bytes 8388624 | tf_op jit(solution)/shard_map/all_gather | solution.py:225
  175.1 7.0 %shard_map.140 = f32[4,256,128]{2,1,0:T(8,128)} custom-call(s32[2]{0:T(128)} %pad_add_fusion.bounds_ref, bf16[2,2,256,128]{3,2,1,0:T(8,128)(2,1)} %broadcast_select_fusion.q_ref, bf16[16384,256]{1,0:T(8,128)(2,1)} %all-gather.5.cloned.1.call-done.k_ref.v_ref, bf16[16384,256]{1,0:T(8,128)(2,1)} %all-gather.5.cloned.1.call-done.k_ref.v_ref, ...), custom_call_target="tpu_custom_call" | custom-call | tf_op jit(solution)/shard_map/pallas_call | solution.py:139
  182.2 1.1 convert.32
  183.3 0.1 copy.94
  183.5 0.3 convolution_convert_fusion.2
  183.8 0.4 reshape.205
  184.2 1.1 constant_dynamic-slice_fusion.3
  185.3 1.1 collective-permute-start
  186.4 1.2 collective-permute-done
  187.7 5.5 %collective-permute-start.1 = (bf16[256,512]{1,0:T(8,128)(2,1)S(1)}, bf16[256,512]{1,0:T(8,128)(2,1)S(1)}, u32[]{:S(2)}, u32[]{:S(2)}) collective-permute-start(bf16[256,512]{1,0:T(8,128)(2,1)S(1)} %fusion.61), channel_id=1, source_target_pairs={{0,2},{2,0},{1,3},{3,1},{4,6},{6,4},{5,7},{7,5},{8,10},{10,8},{9,1... | collective-permute-start | bytes 786440 | tf_op jit(solution)/shard_map/ppermute | solution.py:166
  193.2 6.1 %collective-permute-done.1 = bf16[256,512]{1,0:T(8,128)(2,1)S(1)} collective-permute-done((bf16[256,512]{1,0:T(8,128)(2,1)S(1)}, bf16[256,512]{1,0:T(8,128)(2,1)S(1)}, u32[]{:S(2)}, u32[]{:S(2)}) %collective-permute-start.1) | collective-permute-done | bytes 262176 | tf_op jit(solution)/shard_map/ppermute | solution.py:166
  199.4 1.2 collective-permute-start.2
  200.7 1.7 collective-permute-done.2
  202.3 1.5 fusion.50
  203.8 1.4 convolution_convert_fusion
  205.2 140.0 %all_to_all.10 = bf16[64,1,32,1024]{3,2,1,0:T(8,128)(2,1)S(1)} all-to-all(bf16[64,1,32,1024]{3,2,1,0:T(8,128)(2,1)S(1)} %bitcast.188), channel_id=1, replica_groups=mesh['sy'=4,'sz'=4,'sx'=4,'tz'=2,'tc'=2] {'sy','sz','sx'}, dimensions={0} | all-to-all | bytes 8388608 | tf_op jit(solution)/shard_map/all_to_all | solution.py:276
  345.2 1.9 copy-done.1
  347.2 2.4 collective-permute-start.3
  349.6 6.8 %collective-permute-done.3 = bf16[64,1,32,1024]{3,2,0,1:T(8,128)(2,1)S(1)} collective-permute-done((bf16[64,1,32,1024]{3,2,0,1:T(8,128)(2,1)S(1)}, bf16[64,1,32,1024]{3,2,0,1:T(8,128)(2,1)S(1)}, u32[]{:S(2)}, u32[]{:S(2)}) %collective-permute-start.3) | collective-permute-done | bytes 4194336 | tf_op jit(solution)/shard_map/ppermute | solution.py:277
  356.4 2.0 copy-done.2
  358.3 1.3 fusion.20
  359.6 8.2 %convert_bitcast_fusion = bf16[64,1,32,1024]{3,2,0,1:T(8,128)(2,1)} fusion(f32[64,1,32,128]{3,2,0,1:T(8,128)S(1)} %fusion.20, bf16[64,1,32,1024]{3,2,0,1:T(8,128)(2,1)} %copy-done.2, bf16[1,128,1024]{2,1,0:T(8,128)(2,1)S(1)} %copy-done.5, bf16[1,1024,128]{2,1,0:T(8,128)(2,1)S(1)} %copy-done.6), kind=kOutput, calls=%fused_computation.15 | convolution fusion | flops 1077411840 | bytes 9961472 | tf_op jit(solution)/shard_map/jsrf,sfd->jsrd/dot_general | solution.py:282
  367.9 0.4 collective-permute-start.4
  368.2 3.4 fusion.14
  371.7 3.7 collective-permute-done.4
  375.4 9.5 %fusion.2 = bf16[64,1,32,1024]{3,2,1,0:T(8,128)(2,1)} fusion(bf16[64,1,32,1024]{3,2,0,1:T(8,128)(2,1)} %collective-permute-done.4, bf16[64,1,32,1024]{3,2,1,0:T(8,128)(2,1)} %copy-done.1, f32[64,1,32,128]{3,2,0,1:T(8,128)S(1)} %fusion.14, bf16[1,128,1024]{2,1,0:T(8,128)(2,1)S(1)} %copy-done.5, bf16[1,1024,128]{2,1,0:T(8,128)(2,1)S(1)} %copy-done.6), kind=kOutput, calls=%fused_computation.6 | convolution fusion | flops 1085800448 | bytes 14155776 | tf_op jit(solution)/shard_map/jsrf,sfd->jsrd/dot_general | solution.py:282
  384.9 5.8 %all-to-all-start.1 = ((bf16[64,1,32,1024]{3,2,1,0:T(8,128)(2,1)}), bf16[64,1,32,1024]{3,2,1,0:T(8,128)(2,1)}, u32[]{:S(2)}, u32[]{:S(2)}) async-start(bf16[64,1,32,1024]{3,2,1,0:T(8,128)(2,1)} %fusion.2), calls=%async_computation.1 | async-start | bytes 8388608 | tf_op jit(solution)/shard_map/all_to_all | solution.py:290
  390.7 4.1 select_reduce_fusion
  394.8 89.5 %all-to-all-done.1 = bf16[64,1,32,1024]{3,2,1,0:T(8,128)(2,1)} async-done(((bf16[64,1,32,1024]{3,2,1,0:T(8,128)(2,1)}), bf16[64,1,32,1024]{3,2,1,0:T(8,128)(2,1)}, u32[]{:S(2)}, u32[]{:S(2)}) %all-to-all-start.1) | async-done | bytes 4194336 | tf_op jit(solution)/shard_map/all_to_all | solution.py:290
  484.3 6.3 %convolution_convert_fusion.1 = bf16[256,1024]{1,0:T(8,128)(2,1)S(1)} fusion(f32[256,2048]{1,0:T(8,128)} %select_reduce_fusion, bf16[2048,1024]{1,0:T(8,128)(2,1)} %bitcast.68), kind=kOutput, calls=%fused_computation.31 | convolution fusion | flops 6442713088 | bytes 6815744 | tf_op jit(solution)/shard_map/dot_general | solution.py:297
  490.6 0.4 reshape.215
  490.9 1.1 constant_dynamic-slice_fusion.1
  492.1 2.4 collective-permute-start.5
  494.5 1.2 collective-permute-done.5
  495.8 2.7 collective-permute-start.6
  498.5 14.8 %collective-permute-done.6 = bf16[256,512]{1,0:T(8,128)(2,1)S(1)} collective-permute-done((bf16[256,512]{1,0:T(8,128)(2,1)S(1)}, bf16[256,512]{1,0:T(8,128)(2,1)S(1)}, u32[]{:S(2)}, u32[]{:S(2)}) %collective-permute-start.6) | collective-permute-done | bytes 262176 | tf_op jit(solution)/shard_map/ppermute | solution.py:166
  513.4 0.6 collective-permute-start.7
  514.1 0.8 copy.103
  514.9 0.6 collective-permute-done.7
  515.5 1.0 fusion.53
  (51 shorter events, 1.3 us)
Async XLA Ops:
  7.2 176.3 %copy-start = (bf16[256,1024]{1,0:T(8,128)(2,1)S(1)}, bf16[256,1024]{1,0:T(8,128)(2,1)}, u32[]{:S(2)}) copy-start(bf16[256,1024]{1,0:T(8,128)(2,1)} %param.22) | copy-start | bytes 1572868
  7.2 81.5 %copy-start.7 = (s32[256,8]{0,1:T(8,128)S(1)}, s32[256,8]{0,1:T(8,128)}, u32[]{:S(2)}) copy-start(s32[256,8]{0,1:T(8,128)} %param.15) | copy-start | bytes 24580
  7.2 80.5 %all-gather.3.cloned.1.call-start = ((), (), s32[]{:S(2)}) async-start(), calls=%async_computation.2 | async-start | bytes 2621440 | tf_op jit(solution)/shard_map/all_gather | solution.py:225
  20.2 72.9 %copy-start.3 = (bf16[256,1024]{1,0:T(8,128)(2,1)S(1)}, bf16[256,1024]{1,0:T(8,128)(2,1)}, u32[]{:S(2)}) copy-start(bf16[256,1024]{1,0:T(8,128)(2,1)} %param.13) | copy-start | bytes 1572868
  33.1 142.0 %all-gather.5.cloned.1.call-start = ((), (), s32[]{:S(2)}) async-start(), calls=%async_computation.3 | async-start | bytes 10485760 | tf_op jit(solution)/shard_map/all_gather | solution.py:225
  183.3 17.4 %copy-start.9 = (bf16[1024]{0:T(1024)(128)(2,1)S(1)}, bf16[1024]{0:T(1024)(128)(2,1)}, u32[]{:S(2)}) copy-start(bf16[1024]{0:T(1024)(128)(2,1)} %param.18) | copy-start | bytes 6148
  185.3 2.3 collective-permute-start
  187.7 11.7 %collective-permute-start.1 = (bf16[256,512]{1,0:T(8,128)(2,1)S(1)}, bf16[256,512]{1,0:T(8,128)(2,1)S(1)}, u32[]{:S(2)}, u32[]{:S(2)}) collective-permute-start(bf16[256,512]{1,0:T(8,128)(2,1)S(1)} %fusion.61), channel_id=1, source_target_pairs={{0,2},{2,0},{1,3},{3,1},{4,6},{6,4},{5,7},{7,5},{8,10},{10,8},{9,1... | collective-permute-start | bytes 786440 | tf_op jit(solution)/shard_map/ppermute | solution.py:166
  199.4 2.9 collective-permute-start.2
  205.2 153.2 %copy-start.4 = (bf16[1,1024,128]{2,1,0:T(8,128)(2,1)S(1)}, bf16[1,1024,128]{2,1,0:T(8,128)(2,1)}, u32[]{:S(2)}) copy-start(bf16[1,1024,128]{2,1,0:T(8,128)(2,1)} %param.23) | copy-start | bytes 786436
  345.2 1.9 copy-start.1
  345.2 14.4 %copy-start.5 = (bf16[1,128,1024]{2,1,0:T(8,128)(2,1)S(1)}, bf16[1,128,1024]{2,1,0:T(8,128)(2,1)}, u32[]{:S(2)}) copy-start(bf16[1,128,1024]{2,1,0:T(8,128)(2,1)} %param.25) | copy-start | bytes 786436
  345.2 14.4 %copy-start.6 = (bf16[1,1024,128]{2,1,0:T(8,128)(2,1)S(1)}, bf16[1,1024,128]{2,1,0:T(8,128)(2,1)}, u32[]{:S(2)}) copy-start(bf16[1,1024,128]{2,1,0:T(8,128)(2,1)} %param.24) | copy-start | bytes 786436
  347.2 9.2 %collective-permute-start.3 = (bf16[64,1,32,1024]{3,2,0,1:T(8,128)(2,1)S(1)}, bf16[64,1,32,1024]{3,2,0,1:T(8,128)(2,1)S(1)}, u32[]{:S(2)}, u32[]{:S(2)}) collective-permute-start(bf16[64,1,32,1024]{3,2,0,1:T(8,128)(2,1)S(1)} %bitcast.189), channel_id=1, source_target_pairs={{0,1},{1,0},{2,3},{3,2},{4,5},{5,4},{6,7},{7,6},{8,9},{9,8},{10,11... | collective-permute-start | bytes 12582920 | tf_op jit(solution)/shard_map/ppermute | solution.py:277
  356.4 2.0 copy-start.2
  367.9 7.5 %collective-permute-start.4 = (bf16[64,1,32,1024]{3,2,0,1:T(8,128)(2,1)}, bf16[64,1,32,1024]{3,2,0,1:T(8,128)(2,1)}, u32[]{:S(2)}, u32[]{:S(2)}) collective-permute-start(bf16[64,1,32,1024]{3,2,0,1:T(8,128)(2,1)} %convert_bitcast_fusion), channel_id=1, source_target_pairs={{0,1},{1,0},{2,3},{3,2},{4,5},{5,4},{6,7},{7,6},{8,9},{9,8},{10,11... | collective-permute-start | bytes 12582920 | tf_op jit(solution)/shard_map/ppermute | solution.py:285
  384.9 5.8 %copy-start.8 = (f32[256,8]{0,1:T(8,128)S(1)}, f32[256,8]{0,1:T(8,128)}, u32[]{:S(2)}) copy-start(f32[256,8]{0,1:T(8,128)} %param.16) | copy-start | bytes 24580
  384.9 99.4 %all-to-all-start.1 = ((bf16[64,1,32,1024]{3,2,1,0:T(8,128)(2,1)}), bf16[64,1,32,1024]{3,2,1,0:T(8,128)(2,1)}, u32[]{:S(2)}, u32[]{:S(2)}) async-start(bf16[64,1,32,1024]{3,2,1,0:T(8,128)(2,1)} %fusion.2), calls=%async_computation.1 | async-start | bytes 8388608 | tf_op jit(solution)/shard_map/all_to_all | solution.py:290
  492.1 3.6 collective-permute-start.5
  495.8 17.6 %collective-permute-start.6 = (bf16[256,512]{1,0:T(8,128)(2,1)S(1)}, bf16[256,512]{1,0:T(8,128)(2,1)S(1)}, u32[]{:S(2)}, u32[]{:S(2)}) collective-permute-start(bf16[256,512]{1,0:T(8,128)(2,1)S(1)} %fusion.60), channel_id=1, source_target_pairs={{0,2},{2,0},{1,3},{3,1},{4,6},{6,4},{5,7},{7,5},{8,10},{10,8},{9,1... | collective-permute-start | bytes 786440 | tf_op jit(solution)/shard_map/ppermute | solution.py:166
  513.4 2.1 collective-permute-start.7
Sparse Core Ops, SparseCore 0:
  33.3 54.4 all-gather.2
  89.5 85.5 all-gather.4

commit v11 on v10

--- a/solution.py
+++ b/solution.py
@@ -221,8 +221,14 @@
     key_rot = rotary(key_raw, positions).astype(jnp.bfloat16)
     kv_width = kv_heads * HEAD_DIM
     joined = jnp.concatenate([key_rot.reshape(tokens, kv_width), value_proj], axis=1)
-    for axis_name in SUB_AXES[::-1]:
-        joined = lax.all_gather(joined, axis_name, axis=0, tiled=True)
+    for axis_name in ("sx", "sz"):
+        coordinate = lax.axis_index(axis_name)
+        shifted = [joined] + [
+            lax.ppermute(joined, axis_name, [(j, (j + k) % 4) for j in range(4)]) for k in (1, 2, 3)
+        ]
+        order = (coordinate - jnp.arange(4, dtype=jnp.int32)) % 4
+        joined = jnp.take(jnp.stack(shifted), order, axis=0).reshape(-1, joined.shape[1])
+    joined = lax.all_gather(joined, "sy", axis=0, tiled=True)
     last_query = first_row + tokens - 1
     lowest_seg = own_segs[0]
     chunk_ends = segment_ids[KEY_CHUNK - 1 :: KEY_CHUNK]

time: 523 us -> 526 us (level); the launches traced: 523 us -> 520 us
  blocking collectives: 153 us -> 140 us
  starting transfers between devices: 22.3 us -> 32.3 us
  waiting for transfers between devices: 255 us -> 248 us
    all_gather x2 -> x1, waiting for transfers between devices: 129 us -> 84.4 us  [per_device(): joined = lax.all_gather(joined, 'sy', axis=0, tiled=True)]
    ppermute x0 -> x6, waiting for transfers between devices: none -> 37.9 us  [per_device(): lax.ppermute(joined, axis_name, [(j, (j + k) % 4) for j in range(4)])]
    all_gather x1 -> x0, blocking collectives: 12.9 us -> none  [per_device(): joined = lax.all_gather(joined, axis_name, axis=0, tiled=True)]
    ppermute x0 -> x6, starting transfers between devices: none -> 11.3 us  [per_device(): lax.ppermute(joined, axis_name, [(j, (j + k) % 4) for j in range(4)])]
  transfers between devices with their start and end apart: 11 -> 16, of which waited for: 11 -> 13; matrix products, arithmetic and copies ran while one was open for 4% -> 4% of each run, Pallas kernels for 0% -> 0%
where the time goes in v11:
time: 526 us; the launch traced here: 520 us
  waiting for transfers between devices  248 us (47%)
  blocking collectives  140 us (27%)
  matrix products  35.6 us (7%)
  starting transfers between devices  32.3 us (6%)
  other arithmetic  27.2 us (5%)
  local copies, waits for them, and re-layouts  14.9 us (3%)
  between operations  14.9 us (3%)
  Pallas kernels  7.05 us (1%)
    all_to_all x1, blocking collectives, per_device(): lax.all_to_all(outbound, SUB_AXES, split_axis=0, concat_axis=0, tiled=True)  140 us
    all_to_all x1, waiting for transfers between devices, per_device(): lax.all_to_all(pair_sum, SUB_AXES, split_axis=0, concat_axis=0, tiled=True)  89.5 us
    all_gather x1, waiting for transfers between devices, per_device(): joined = lax.all_gather(joined, 'sy', axis=0, tiled=True)  84.4 us
    ppermute x6, waiting for transfers between devices, per_device(): lax.ppermute(joined, axis_name, [(j, (j + k) % 4) for j in range(4)])  37.9 us
    ppermute x2, waiting for transfers between devices, tp_sum(): lax.ppermute(pair, 'tz', swap).astype(jnp.float32)  20.9 us
    dot_general x2, matrix products, expert_rows(): jnp.einsum('jsrf,sfd->jsrd', activated, w_down, preferred_element_type=jn...  17.8 us
    ppermute x6, starting transfers between devices, per_device(): lax.ppermute(joined, axis_name, [(j, (j + k) % 4) for j in range(4)])  11.3 us
  transfers between devices with their start and end apart: 16, of which 13 were waited for; matrix products, arithmetic and copies ran while one was open for 4% of the time, Pallas kernels for 0%

profile of v11, /device:TPU:1, one launch (start us, length us, event | category | flops | bytes accessed | tf_op | source)
XLA Modules:
  0.0 519.9 jit_solution(6234789544912720420)
XLA Ops:
  7.3 1.1 convert_reduce_fusion
  8.4 0.7 fusion.102
  9.1 0.7 convert_element_type.166
  9.8 1.2 fusion.46
  11.0 1.5 fusion.97
  12.5 1.5 convolution_convert_fusion.3
  14.0 5.8 %fusion.85 = (f32[256]{0:T(256)S(1)}, s32[256]{0:T(256)S(1)}) fusion(s32[]{:T(128)} %bitcast.4, s32[]{:T(128)} %bitcast.5, s32[]{:T(128)} %bitcast.6, s32[]{:T(128)} %bitcast.7, s32[]{:T(128)} %bitcast.8, s32[]{:T(128)} %bitcast.9, s32[]{:T(128)} %bitcast.10, s32[]{:T(128)} %bitcast.11, s32[]{:T(128)S(6)} %mul.169, s32[16384]{0:T(1024)} %param.14, ...), kind=kLoop, calls=%fused_computation.150 | loop fusion | flops 5120 | bytes 3112 | tf_op jit(solution)/shard_map/convert_element_type | solution.py:32
  20.1 2.1 collective-permute-start
  22.2 2.5 collective-permute-start.1
  24.6 1.2 collective-permute-start.2
  25.9 4.4 collective-permute-done.1
  31.4 1.7 collective-permute-start.3
  33.2 3.0 collective-permute-start.4
  36.2 0.9 collective-permute-start.5
  37.4 9.4 %collective-permute-done.3 = bf16[1024,256]{1,0:T(8,128)(2,1)S(1)} collective-permute-done((bf16[1024,256]{1,0:T(8,128)(2,1)S(1)}, bf16[1024,256]{1,0:T(8,128)(2,1)S(1)}, u32[]{:S(2)}, u32[]{:S(2)}) %collective-permute-start.3) | collective-permute-done | bytes 524320 | tf_op jit(solution)/shard_map/ppermute | solution.py:227
  46.7 24.0 %collective-permute-done.4 = bf16[1024,256]{1,0:T(8,128)(2,1)S(1)} collective-permute-done((bf16[1024,256]{1,0:T(8,128)(2,1)S(1)}, bf16[1024,256]{1,0:T(8,128)(2,1)S(1)}, u32[]{:S(2)}, u32[]{:S(2)}) %collective-permute-start.4) | collective-permute-done | bytes 524320 | tf_op jit(solution)/shard_map/ppermute | solution.py:227
  70.8 1.6 pad_maximum_fusion
  72.4 2.3 gather_fusion.1
  74.7 1.9 bitcast_select_fusion
  76.6 1.0 slice.26
  77.8 0.6 fusion.41
  78.7 3.0 fusion
  81.9 1.5 fusion.99
  83.9 0.6 slice.27
  84.5 0.8 copy.84.qseg_ref
  85.3 1.3 fusion.86
  86.6 1.2 pad_add_fusion.bounds_ref
  87.8 0.7 iota_add_fusion.qidx_ref
  88.5 0.7 broadcast_select_fusion.q_ref
  89.2 84.4 %all-gather.2.cloned.1.call-done.k_ref.v_ref = bf16[16384,256]{1,0:T(8,128)(2,1)} async-done(((bf16[4096,256]{1,0:T(8,128)(2,1)}), bf16[16384,256]{1,0:T(8,128)(2,1)}) %all-gather.2.cloned.1.call-update) | async-done | bytes 8388624 | tf_op jit(solution)/shard_map/all_gather | solution.py:231
  173.6 7.0 %shard_map.140 = f32[4,256,128]{2,1,0:T(8,128)} custom-call(s32[2]{0:T(128)} %pad_add_fusion.bounds_ref, bf16[2,2,256,128]{3,2,1,0:T(8,128)(2,1)} %broadcast_select_fusion.q_ref, bf16[16384,256]{1,0:T(8,128)(2,1)} %all-gather.2.cloned.1.call-done.k_ref.v_ref, bf16[16384,256]{1,0:T(8,128)(2,1)} %all-gather.2.cloned.1.call-done.k_ref.v_ref, ...), custom_call_target="tpu_custom_call" | custom-call | tf_op jit(solution)/shard_map/pallas_call | solution.py:139
  180.7 1.1 convert.32
  182.7 1.1 constant_dynamic-slice_fusion.3
  183.8 0.9 collective-permute-start.6
  184.8 1.2 collective-permute-done.6
  186.0 5.8 %collective-permute-start.7 = (bf16[256,512]{1,0:T(8,128)(2,1)S(1)}, bf16[256,512]{1,0:T(8,128)(2,1)S(1)}, u32[]{:S(2)}, u32[]{:S(2)}) collective-permute-start(bf16[256,512]{1,0:T(8,128)(2,1)S(1)} %fusion.61), channel_id=1, source_target_pairs={{0,2},{2,0},{1,3},{3,1},{4,6},{6,4},{5,7},{7,5},{8,10},{10,8},{9,1... | collective-permute-start | bytes 786440 | tf_op jit(solution)/shard_map/ppermute | solution.py:166
  191.8 6.1 %collective-permute-done.7 = bf16[256,512]{1,0:T(8,128)(2,1)S(1)} collective-permute-done((bf16[256,512]{1,0:T(8,128)(2,1)S(1)}, bf16[256,512]{1,0:T(8,128)(2,1)S(1)}, u32[]{:S(2)}, u32[]{:S(2)}) %collective-permute-start.7) | collective-permute-done | bytes 262176 | tf_op jit(solution)/shard_map/ppermute | solution.py:166
  198.0 1.2 collective-permute-start.8
  199.2 1.5 collective-permute-done.8
  201.0 1.4 convolution_convert_fusion
  202.4 140.0 %all_to_all.10 = bf16[64,1,32,1024]{3,2,1,0:T(8,128)(2,1)S(1)} all-to-all(bf16[64,1,32,1024]{3,2,1,0:T(8,128)(2,1)S(1)} %bitcast.211), channel_id=1, replica_groups=mesh['sy'=4,'sz'=4,'sx'=4,'tz'=2,'tc'=2] {'sy','sz','sx'}, dimensions={0} | all-to-all | bytes 8388608 | tf_op jit(solution)/shard_map/all_to_all | solution.py:282
  342.4 1.9 copy-done.2
  344.4 2.4 collective-permute-start.9
  346.8 6.8 %collective-permute-done.9 = bf16[64,1,32,1024]{3,2,0,1:T(8,128)(2,1)S(1)} collective-permute-done((bf16[64,1,32,1024]{3,2,0,1:T(8,128)(2,1)S(1)}, bf16[64,1,32,1024]{3,2,0,1:T(8,128)(2,1)S(1)}, u32[]{:S(2)}, u32[]{:S(2)}) %collective-permute-start.9) | collective-permute-done | bytes 4194336 | tf_op jit(solution)/shard_map/ppermute | solution.py:283
  353.6 2.0 copy-done.3
  355.6 1.3 fusion.20
  356.9 8.3 %convert_bitcast_fusion = bf16[64,1,32,1024]{3,2,0,1:T(8,128)(2,1)} fusion(f32[64,1,32,128]{3,2,0,1:T(8,128)S(1)} %fusion.20, bf16[64,1,32,1024]{3,2,0,1:T(8,128)(2,1)} %copy-done.3, bf16[1,128,1024]{2,1,0:T(8,128)(2,1)S(1)} %copy-done.6, bf16[1,1024,128]{2,1,0:T(8,128)(2,1)S(1)} %copy-done.7), kind=kOutput, calls=%fused_computation.17 | convolution fusion | flops 1077411840 | bytes 9961472 | tf_op jit(solution)/shard_map/jsrf,sfd->jsrd/dot_general | solution.py:288
  365.1 0.6 collective-permute-start.10
  365.7 3.4 fusion.14
  369.1 3.7 collective-permute-done.10
  372.8 9.5 %fusion.2 = bf16[64,1,32,1024]{3,2,1,0:T(8,128)(2,1)} fusion(bf16[64,1,32,1024]{3,2,0,1:T(8,128)(2,1)} %collective-permute-done.10, bf16[64,1,32,1024]{3,2,1,0:T(8,128)(2,1)} %copy-done.2, f32[64,1,32,128]{3,2,0,1:T(8,128)S(1)} %fusion.14, bf16[1,128,1024]{2,1,0:T(8,128)(2,1)S(1)} %copy-done.6, bf16[1,1024,128]{2,1,0:T(8,128)(2,1)S(1)} %copy-done.7), kind=kOutput, calls=%fused_computation.8 | convolution fusion | flops 1085800448 | bytes 14155776 | tf_op jit(solution)/shard_map/jsrf,sfd->jsrd/dot_general | solution.py:288
  382.4 5.8 %all-to-all-start.1 = ((bf16[64,1,32,1024]{3,2,1,0:T(8,128)(2,1)}), bf16[64,1,32,1024]{3,2,1,0:T(8,128)(2,1)}, u32[]{:S(2)}, u32[]{:S(2)}) async-start(bf16[64,1,32,1024]{3,2,1,0:T(8,128)(2,1)} %fusion.2), calls=%async_computation.1 | async-start | bytes 8388608 | tf_op jit(solution)/shard_map/all_to_all | solution.py:296
  388.2 4.1 select_reduce_fusion
  392.3 89.5 %all-to-all-done.1 = bf16[64,1,32,1024]{3,2,1,0:T(8,128)(2,1)} async-done(((bf16[64,1,32,1024]{3,2,1,0:T(8,128)(2,1)}), bf16[64,1,32,1024]{3,2,1,0:T(8,128)(2,1)}, u32[]{:S(2)}, u32[]{:S(2)}) %all-to-all-start.1) | async-done | bytes 4194336 | tf_op jit(solution)/shard_map/all_to_all | solution.py:296
  481.7 6.3 %convolution_convert_fusion.1 = bf16[256,1024]{1,0:T(8,128)(2,1)S(1)} fusion(f32[256,2048]{1,0:T(8,128)} %select_reduce_fusion, bf16[2048,1024]{1,0:T(8,128)(2,1)} %bitcast.80), kind=kOutput, calls=%fused_computation.35 | convolution fusion | flops 6442713088 | bytes 6815744 | tf_op jit(solution)/shard_map/dot_general | solution.py:303
  488.5 1.1 constant_dynamic-slice_fusion.1
  489.6 2.4 collective-permute-start.11
  492.0 1.2 collective-permute-done.11
  493.3 1.2 collective-permute-start.12
  494.5 14.8 %collective-permute-done.12 = bf16[256,512]{1,0:T(8,128)(2,1)S(1)} collective-permute-done((bf16[256,512]{1,0:T(8,128)(2,1)S(1)}, bf16[256,512]{1,0:T(8,128)(2,1)S(1)}, u32[]{:S(2)}, u32[]{:S(2)}) %collective-permute-start.12) | collective-permute-done | bytes 262176 | tf_op jit(solution)/shard_map/ppermute | solution.py:166
  509.4 0.6 collective-permute-start.13
  510.0 0.8 copy.93
  510.8 0.7 collective-permute-done.13
  511.5 1.0 fusion.53
  (77 shorter events, 4.8 us)
Async XLA Ops:
  7.2 174.8 %copy-start = (bf16[256,1024]{1,0:T(8,128)(2,1)S(1)}, bf16[256,1024]{1,0:T(8,128)(2,1)}, u32[]{:S(2)}) copy-start(bf16[256,1024]{1,0:T(8,128)(2,1)} %param.22) | copy-start | bytes 1572868
  7.2 166.5 %all-gather.2.cloned.1.call-start = ((), (), s32[]{:S(2)}) async-start(), calls=%async_computation.2 | async-start | bytes 10485760 | tf_op jit(solution)/shard_map/all_gather | solution.py:231
  20.1 5.8 %collective-permute-start = (bf16[256,256]{0,1:T(8,128)(2,1)S(1)}, bf16[256,256]{0,1:T(8,128)(2,1)S(1)}, u32[]{:S(2)}, u32[]{:S(2)}) collective-permute-start(bf16[256,256]{0,1:T(8,128)(2,1)S(1)} %get-tuple-element.33), channel_id=1, source_target_pairs={{0,4},{4,8},{8,12},{12,0},{1,5},{5,9},{9,13},{13,1},{2,6},{6,10},{... | collective-permute-start | bytes 393224 | tf_op jit(solution)/shard_map/ppermute | solution.py:227
  22.2 8.2 %collective-permute-start.1 = (bf16[256,256]{0,1:T(8,128)(2,1)S(1)}, bf16[256,256]{0,1:T(8,128)(2,1)S(1)}, u32[]{:S(2)}, u32[]{:S(2)}) collective-permute-start(bf16[256,256]{0,1:T(8,128)(2,1)S(1)} %get-tuple-element.33), channel_id=1, source_target_pairs={{0,8},{4,12},{8,0},{12,4},{1,9},{5,13},{9,1},{13,5},{2,10},{6,14},... | collective-permute-start | bytes 393224 | tf_op jit(solution)/shard_map/ppermute | solution.py:227
  24.6 5.7 %collective-permute-start.2 = (bf16[256,256]{0,1:T(8,128)(2,1)S(1)}, bf16[256,256]{0,1:T(8,128)(2,1)S(1)}, u32[]{:S(2)}, u32[]{:S(2)}) collective-permute-start(bf16[256,256]{0,1:T(8,128)(2,1)S(1)} %get-tuple-element.33), channel_id=1, source_target_pairs={{0,12},{4,0},{8,4},{12,8},{1,13},{5,1},{9,5},{13,9},{2,14},{6,2},{... | collective-permute-start | bytes 393224 | tf_op jit(solution)/shard_map/ppermute | solution.py:227
  31.4 15.3 %collective-permute-start.3 = (bf16[1024,256]{1,0:T(8,128)(2,1)S(1)}, bf16[1024,256]{1,0:T(8,128)(2,1)S(1)}, u32[]{:S(2)}, u32[]{:S(2)}) collective-permute-start(bf16[1024,256]{1,0:T(8,128)(2,1)S(1)} %bitcast_select_fusion.1), channel_id=1, source_target_pairs={{0,16},{16,32},{32,48},{48,0},{1,17},{17,33},{33,49},{49,1},{2,18}... | collective-permute-start | bytes 1572872 | tf_op jit(solution)/shard_map/ppermute | solution.py:227
  33.2 37.6 %collective-permute-start.4 = (bf16[1024,256]{1,0:T(8,128)(2,1)S(1)}, bf16[1024,256]{1,0:T(8,128)(2,1)S(1)}, u32[]{:S(2)}, u32[]{:S(2)}) collective-permute-start(bf16[1024,256]{1,0:T(8,128)(2,1)S(1)} %bitcast_select_fusion.1), channel_id=1, source_target_pairs={{0,32},{16,48},{32,0},{48,16},{1,33},{17,49},{33,1},{49,17},{2,34}... | collective-permute-start | bytes 1572872 | tf_op jit(solution)/shard_map/ppermute | solution.py:227
  36.2 34.6 %collective-permute-start.5 = (bf16[1024,256]{1,0:T(8,128)(2,1)S(1)}, bf16[1024,256]{1,0:T(8,128)(2,1)S(1)}, u32[]{:S(2)}, u32[]{:S(2)}) collective-permute-start(bf16[1024,256]{1,0:T(8,128)(2,1)S(1)} %bitcast_select_fusion.1), channel_id=1, source_target_pairs={{0,48},{16,0},{32,16},{48,32},{1,49},{17,1},{33,17},{49,33},{2,50}... | collective-permute-start | bytes 1572872 | tf_op jit(solution)/shard_map/ppermute | solution.py:227
  74.6 2.9 copy-start.8
  76.6 5.4 %copy-start.4 = (bf16[256,1024]{1,0:T(8,128)(2,1)S(1)}, bf16[256,1024]{1,0:T(8,128)(2,1)}, u32[]{:S(2)}) copy-start(bf16[256,1024]{1,0:T(8,128)(2,1)} %param.13) | copy-start | bytes 1572868
  181.8 17.4 %copy-start.10 = (bf16[1024]{0:T(1024)(128)(2,1)S(1)}, bf16[1024]{0:T(1024)(128)(2,1)}, u32[]{:S(2)}) copy-start(bf16[1024]{0:T(1024)(128)(2,1)} %param.18) | copy-start | bytes 6148
  183.8 2.1 collective-permute-start.6
  186.0 11.9 %collective-permute-start.7 = (bf16[256,512]{1,0:T(8,128)(2,1)S(1)}, bf16[256,512]{1,0:T(8,128)(2,1)S(1)}, u32[]{:S(2)}, u32[]{:S(2)}) collective-permute-start(bf16[256,512]{1,0:T(8,128)(2,1)S(1)} %fusion.61), channel_id=1, source_target_pairs={{0,2},{2,0},{1,3},{3,1},{4,6},{6,4},{5,7},{7,5},{8,10},{10,8},{9,1... | collective-permute-start | bytes 786440 | tf_op jit(solution)/shard_map/ppermute | solution.py:166
  198.0 2.8 collective-permute-start.8
  202.4 153.2 %copy-start.5 = (bf16[1,1024,128]{2,1,0:T(8,128)(2,1)S(1)}, bf16[1,1024,128]{2,1,0:T(8,128)(2,1)}, u32[]{:S(2)}) copy-start(bf16[1,1024,128]{2,1,0:T(8,128)(2,1)} %param.23) | copy-start | bytes 786436
  342.4 1.9 copy-start.2
  342.4 14.4 %copy-start.6 = (bf16[1,128,1024]{2,1,0:T(8,128)(2,1)S(1)}, bf16[1,128,1024]{2,1,0:T(8,128)(2,1)}, u32[]{:S(2)}) copy-start(bf16[1,128,1024]{2,1,0:T(8,128)(2,1)} %param.25) | copy-start | bytes 786436
  342.4 14.4 %copy-start.7 = (bf16[1,1024,128]{2,1,0:T(8,128)(2,1)S(1)}, bf16[1,1024,128]{2,1,0:T(8,128)(2,1)}, u32[]{:S(2)}) copy-start(bf16[1,1024,128]{2,1,0:T(8,128)(2,1)} %param.24) | copy-start | bytes 786436
  344.4 9.2 %collective-permute-start.9 = (bf16[64,1,32,1024]{3,2,0,1:T(8,128)(2,1)S(1)}, bf16[64,1,32,1024]{3,2,0,1:T(8,128)(2,1)S(1)}, u32[]{:S(2)}, u32[]{:S(2)}) collective-permute-start(bf16[64,1,32,1024]{3,2,0,1:T(8,128)(2,1)S(1)} %bitcast.212), channel_id=1, source_target_pairs={{0,1},{1,0},{2,3},{3,2},{4,5},{5,4},{6,7},{7,6},{8,9},{9,8},{10,11... | collective-permute-start | bytes 12582920 | tf_op jit(solution)/shard_map/ppermute | solution.py:283
  353.6 2.0 copy-start.3
  365.1 7.7 %collective-permute-start.10 = (bf16[64,1,32,1024]{3,2,0,1:T(8,128)(2,1)}, bf16[64,1,32,1024]{3,2,0,1:T(8,128)(2,1)}, u32[]{:S(2)}, u32[]{:S(2)}) collective-permute-start(bf16[64,1,32,1024]{3,2,0,1:T(8,128)(2,1)} %convert_bitcast_fusion), channel_id=1, source_target_pairs={{0,1},{1,0},{2,3},{3,2},{4,5},{5,4},{6,7},{7,6},{8,9},{9,8},{10,11... | collective-permute-start | bytes 12582920 | tf_op jit(solution)/shard_map/ppermute | solution.py:291
  382.4 5.8 %copy-start.9 = (f32[256,8]{0,1:T(8,128)S(1)}, f32[256,8]{0,1:T(8,128)}, u32[]{:S(2)}) copy-start(f32[256,8]{0,1:T(8,128)} %param.16) | copy-start | bytes 24580
  382.4 99.4 %all-to-all-start.1 = ((bf16[64,1,32,1024]{3,2,1,0:T(8,128)(2,1)}), bf16[64,1,32,1024]{3,2,1,0:T(8,128)(2,1)}, u32[]{:S(2)}, u32[]{:S(2)}) async-start(bf16[64,1,32,1024]{3,2,1,0:T(8,128)(2,1)} %fusion.2), calls=%async_computation.1 | async-start | bytes 8388608 | tf_op jit(solution)/shard_map/all_to_all | solution.py:296
  481.7 30.8 %copy-start.1 = (bf16[256,1024]{1,0:T(8,128)(2,1)S(1)}, bf16[256,1024]{1,0:T(8,128)(2,1)}, u32[]{:S(2)}) copy-start(bf16[256,1024]{1,0:T(8,128)(2,1)} %param.22) | copy-start | bytes 1572868
  489.6 3.6 collective-permute-start.11
  493.3 16.0 %collective-permute-start.12 = (bf16[256,512]{1,0:T(8,128)(2,1)S(1)}, bf16[256,512]{1,0:T(8,128)(2,1)S(1)}, u32[]{:S(2)}, u32[]{:S(2)}) collective-permute-start(bf16[256,512]{1,0:T(8,128)(2,1)S(1)} %fusion.60), channel_id=1, source_target_pairs={{0,2},{2,0},{1,3},{3,1},{4,6},{6,4},{5,7},{7,5},{8,10},{10,8},{9,1... | collective-permute-start | bytes 786440 | tf_op jit(solution)/shard_map/ppermute | solution.py:166
  509.4 2.1 collective-permute-start.13
Sparse Core Ops, SparseCore 0:
  76.7 96.8 all-gather.1

commit v12 on v10

--- a/solution.py
+++ b/solution.py
@@ -45,7 +45,6 @@
 
 def attention_kernel(bounds_ref, q_ref, k_ref, v_ref, kseg_ref, qseg_ref, qidx_ref, o_ref, m_sc, l_sc, acc_sc):
     step = pl.program_id(0)
-    kv_heads, group_size = q_ref.shape[0], q_ref.shape[1]
 
     @pl.when(step == 0)
     def _():
@@ -61,28 +60,30 @@
         allowed = (qseg_ref[...] == kseg_ref[0]) & (qidx_ref[...] >= key_index)
         key_rows = k_ref[...]
         value_rows = v_ref[...]
-        for head in range(kv_heads):
-            for member in range(group_size):
-                slot = head * group_size + member
-                scores = (
-                    lax.dot_general(
-                        q_ref[head, member],
-                        key_rows,
-                        (((1,), (1,)), ((), ())),
-                        preferred_element_type=jnp.float32,
-                    )
-                    * SCORE_SCALE
+
+        def one_slot(slot, carry):
+            scores = (
+                lax.dot_general(
+                    q_ref[slot],
+                    key_rows,
+                    (((1,), (1,)), ((), ())),
+                    preferred_element_type=jnp.float32,
                 )
-                masked = jnp.where(allowed, scores, -1e30)
-                running_max = m_sc[slot]
-                new_max = jnp.maximum(running_max, jnp.max(masked, axis=-1, keepdims=True))
-                weights = jnp.where(allowed, jnp.exp(masked - new_max), 0.0)
-                factor = jnp.exp(running_max - new_max)
-                l_sc[slot] = l_sc[slot] * factor + jnp.sum(weights, axis=-1, keepdims=True)
-                acc_sc[slot] = acc_sc[slot] * factor + jnp.dot(
-                    weights.astype(jnp.bfloat16), value_rows, preferred_element_type=jnp.float32
-                )
-                m_sc[slot] = new_max
+                * SCORE_SCALE
+            )
+            masked = jnp.where(allowed, scores, -1e30)
+            running_max = m_sc[slot]
+            new_max = jnp.maximum(running_max, jnp.max(masked, axis=-1, keepdims=True))
+            weights = jnp.where(allowed, jnp.exp(masked - new_max), 0.0)
+            factor = jnp.exp(running_max - new_max)
+            l_sc[slot] = l_sc[slot] * factor + jnp.sum(weights, axis=-1, keepdims=True)
+            acc_sc[slot] = acc_sc[slot] * factor + jnp.dot(
+                weights.astype(jnp.bfloat16), value_rows, preferred_element_type=jnp.float32
+            )
+            m_sc[slot] = new_max
+            return carry
+
+        lax.fori_loop(0, q_ref.shape[0], one_slot, 0)
 
     @pl.when(step == pl.num_programs(0) - 1)
     def _():
@@ -122,7 +123,7 @@
         num_scalar_prefetch=1,
         grid=(chunks,),
         in_specs=[
-            pl.BlockSpec((kv_heads, group_size, tokens, kv_width), whole),
+            pl.BlockSpec((kv_heads * group_size, tokens, kv_width), whole3),
             pl.BlockSpec((KEY_CHUNK, kv_width), key_map),
             pl.BlockSpec((KEY_CHUNK, kv_width), value_map),
             pl.BlockSpec((1, 1, KEY_CHUNK), seg_map),
@@ -143,7 +144,7 @@
         compiler_params=pltpu.CompilerParams(dimension_semantics=("arbitrary",)),
     )(
         bounds,
-        padded_queries,
+        padded_queries.reshape(kv_heads * group_size, tokens, kv_width),
         joined,
         joined,
         segment_ids.reshape(chunks, 1, KEY_CHUNK),

time: 523 us -> 534 us (1.021)
  blocking collectives: 153 us -> 164 us
    all_to_all x1, blocking collectives: 140 us -> 151 us  [per_device(): lax.all_to_all(outbound, SUB_AXES, split_axis=0, concat_axis=0, tiled=True)]
where the time goes in v12:
time: 534 us; the launch traced here: 535 us
  waiting for transfers between devices  255 us (48%)
  blocking collectives  164 us (31%)
  matrix products  35.5 us (7%)
  other arithmetic  24.4 us (5%)
  starting transfers between devices  22.3 us (4%)
  between operations  14.5 us (3%)
  local copies, waits for them, and re-layouts  11.8 us (2%)
  Pallas kernels  7.92 us (1%)
    all_to_all x1, blocking collectives, per_device(): lax.all_to_all(outbound, SUB_AXES, split_axis=0, concat_axis=0, tiled=True)  151 us
    all_gather x2, waiting for transfers between devices, per_device(): joined = lax.all_gather(joined, axis_name, axis=0, tiled=True)  129 us
    all_to_all x1, waiting for transfers between devices, per_device(): lax.all_to_all(pair_sum, SUB_AXES, split_axis=0, concat_axis=0, tiled=True)  89.5 us
    ppermute x2, waiting for transfers between devices, tp_sum(): lax.ppermute(pair, 'tz', swap).astype(jnp.float32)  20.9 us
    dot_general x2, matrix products, expert_rows(): jnp.einsum('jsrf,sfd->jsrd', activated, w_down, preferred_element_type=jn...  17.8 us
    all_gather x1, blocking collectives, per_device(): joined = lax.all_gather(joined, axis_name, axis=0, tiled=True)  12.9 us
  transfers between devices with their start and end apart: 11, of which 11 were waited for; matrix products, arithmetic and copies ran while one was open for 4% of the time, Pallas kernels for 0%

profile of v12, /device:TPU:1, one launch (start us, length us, event | category | flops | bytes accessed | tf_op | source)
XLA Modules:
  0.0 534.9 jit_solution(13960723865794862496)
XLA Ops:
  7.3 1.1 convert_reduce_fusion
  8.4 0.7 fusion.95
  9.0 0.7 convert_element_type.166
  9.7 1.2 fusion.46
  11.0 5.9 %fusion.85 = (f32[256]{0:T(256)S(1)}, s32[256]{0:T(256)S(1)}) fusion(s32[]{:T(128)} %bitcast.4, s32[]{:T(128)} %bitcast.5, s32[]{:T(128)} %bitcast.6, s32[]{:T(128)} %bitcast.7, s32[]{:T(128)} %bitcast.8, s32[]{:T(128)} %bitcast.9, s32[]{:T(128)} %bitcast.10, s32[]{:T(128)} %bitcast.11, s32[]{:T(128)S(6)} %mul.169, s32[16384]{0:T(1024)} %param.14, ...), kind=kLoop, calls=%fused_computation.121 | loop fusion | flops 5120 | bytes 3112 | tf_op jit(solution)/shard_map/convert_element_type | solution.py:32
  16.8 0.2 multiply_cosine_fusion
  17.0 1.5 fusion.90
  18.7 1.5 convolution_convert_fusion.3
  20.2 12.9 %all_gather.9 = bf16[1024,256]{1,0:T(8,128)(2,1)} all-gather(bf16[256,256]{1,0:T(8,128)(2,1)S(1)} %pad_maximum_fusion), channel_id=1, replica_groups=mesh['sy'=4,'sz'=4,'sx'=4,'tz'=2,'tc'=2] {'sx'}, dimensions={0}, use_global_device_ids=true | all-gather | bytes 655360 | tf_op jit(solution)/shard_map/all_gather | solution.py:226
  33.2 54.5 %all-gather.3.cloned.1.call-done = bf16[4096,256]{1,0:T(8,128)(2,1)} async-done(((bf16[1024,256]{1,0:T(8,128)(2,1)}), bf16[4096,256]{1,0:T(8,128)(2,1)}) %all-gather.3.cloned.1.call-update) | async-done | bytes 2097168 | tf_op jit(solution)/shard_map/all_gather | solution.py:226
  87.7 0.9 slice.26
  88.7 0.1 copy.87
  88.8 0.1 eq.60
  88.9 0.6 fusion.41
  89.8 3.0 fusion
  92.8 0.2 convert_element_type.176
  93.0 1.5 fusion.92
  94.6 0.2 copy.84
  95.0 0.5 slice.27
  95.5 0.8 copy.93.qseg_ref
  96.3 1.3 fusion.86
  97.6 1.2 pad_add_fusion.bounds_ref
  98.8 0.7 iota_add_fusion.qidx_ref
  99.5 0.7 broadcast_select_fusion.q_ref
  100.2 74.9 %all-gather.5.cloned.1.call-done.k_ref.v_ref = bf16[16384,256]{1,0:T(8,128)(2,1)} async-done(((bf16[4096,256]{1,0:T(8,128)(2,1)}), bf16[16384,256]{1,0:T(8,128)(2,1)}) %all-gather.5.cloned.1.call-update) | async-done | bytes 8388624 | tf_op jit(solution)/shard_map/all_gather | solution.py:226
  175.1 7.9 %shard_map.140 = f32[4,256,128]{2,1,0:T(8,128)} custom-call(s32[2]{0:T(128)} %pad_add_fusion.bounds_ref, bf16[4,256,128]{2,1,0:T(8,128)(2,1)} %broadcast_select_fusion.q_ref, bf16[16384,256]{1,0:T(8,128)(2,1)} %all-gather.5.cloned.1.call-done.k_ref.v_ref, bf16[16384,256]{1,0:T(8,128)(2,1)} %all-gather.5.cloned.1.call-done.k_ref.v_ref, ...), custom_call_target="tpu_custom_call" | custom-call | tf_op jit(solution)/shard_map/pallas_call | solution.py:140
  183.1 1.1 convert.32
  184.1 0.1 copy.94
  184.3 0.3 convolution_convert_fusion.2
  184.7 0.4 reshape.204
  185.1 1.1 constant_dynamic-slice_fusion.3
  186.2 0.9 collective-permute-start
  187.1 1.2 collective-permute-done
  188.4 5.5 %collective-permute-start.1 = (bf16[256,512]{1,0:T(8,128)(2,1)S(1)}, bf16[256,512]{1,0:T(8,128)(2,1)S(1)}, u32[]{:S(2)}, u32[]{:S(2)}) collective-permute-start(bf16[256,512]{1,0:T(8,128)(2,1)S(1)} %fusion.61), channel_id=1, source_target_pairs={{0,2},{2,0},{1,3},{3,1},{4,6},{6,4},{5,7},{7,5},{8,10},{10,8},{9,1... | collective-permute-start | bytes 786440 | tf_op jit(solution)/shard_map/ppermute | solution.py:167
  193.9 6.1 %collective-permute-done.1 = bf16[256,512]{1,0:T(8,128)(2,1)S(1)} collective-permute-done((bf16[256,512]{1,0:T(8,128)(2,1)S(1)}, bf16[256,512]{1,0:T(8,128)(2,1)S(1)}, u32[]{:S(2)}, u32[]{:S(2)}) %collective-permute-start.1) | collective-permute-done | bytes 262176 | tf_op jit(solution)/shard_map/ppermute | solution.py:167
  200.1 1.5 collective-permute-start.2
  201.6 1.7 collective-permute-done.2
  203.3 1.5 fusion.50
  204.8 1.4 convolution_convert_fusion
  206.2 150.6 %all_to_all.10 = bf16[64,1,32,1024]{3,2,1,0:T(8,128)(2,1)S(1)} all-to-all(bf16[64,1,32,1024]{3,2,1,0:T(8,128)(2,1)S(1)} %bitcast.188), channel_id=1, replica_groups=mesh['sy'=4,'sz'=4,'sx'=4,'tz'=2,'tc'=2] {'sy','sz','sx'}, dimensions={0} | all-to-all | bytes 8388608 | tf_op jit(solution)/shard_map/all_to_all | solution.py:277
  356.8 1.9 copy-done.1
  358.7 2.4 collective-permute-start.3
  361.2 6.8 %collective-permute-done.3 = bf16[64,1,32,1024]{3,2,0,1:T(8,128)(2,1)S(1)} collective-permute-done((bf16[64,1,32,1024]{3,2,0,1:T(8,128)(2,1)S(1)}, bf16[64,1,32,1024]{3,2,0,1:T(8,128)(2,1)S(1)}, u32[]{:S(2)}, u32[]{:S(2)}) %collective-permute-start.3) | collective-permute-done | bytes 4194336 | tf_op jit(solution)/shard_map/ppermute | solution.py:278
  367.9 2.0 copy-done.2
  369.9 1.3 fusion.20
  371.2 8.2 %convert_bitcast_fusion = bf16[64,1,32,1024]{3,2,0,1:T(8,128)(2,1)} fusion(f32[64,1,32,128]{3,2,0,1:T(8,128)S(1)} %fusion.20, bf16[64,1,32,1024]{3,2,0,1:T(8,128)(2,1)} %copy-done.2, bf16[1,128,1024]{2,1,0:T(8,128)(2,1)S(1)} %copy-done.5, bf16[1,1024,128]{2,1,0:T(8,128)(2,1)S(1)} %copy-done.6), kind=kOutput, calls=%fused_computation.15 | convolution fusion | flops 1077411840 | bytes 9961472 | tf_op jit(solution)/shard_map/jsrf,sfd->jsrd/dot_general | solution.py:283
  379.4 0.4 collective-permute-start.4
  379.8 3.4 fusion.14
  383.3 3.7 collective-permute-done.4
  386.9 9.5 %fusion.2 = bf16[64,1,32,1024]{3,2,1,0:T(8,128)(2,1)} fusion(bf16[64,1,32,1024]{3,2,0,1:T(8,128)(2,1)} %collective-permute-done.4, bf16[64,1,32,1024]{3,2,1,0:T(8,128)(2,1)} %copy-done.1, f32[64,1,32,128]{3,2,0,1:T(8,128)S(1)} %fusion.14, bf16[1,128,1024]{2,1,0:T(8,128)(2,1)S(1)} %copy-done.5, bf16[1,1024,128]{2,1,0:T(8,128)(2,1)S(1)} %copy-done.6), kind=kOutput, calls=%fused_computation.6 | convolution fusion | flops 1085800448 | bytes 14155776 | tf_op jit(solution)/shard_map/jsrf,sfd->jsrd/dot_general | solution.py:283
  396.5 5.8 %all-to-all-start.1 = ((bf16[64,1,32,1024]{3,2,1,0:T(8,128)(2,1)}), bf16[64,1,32,1024]{3,2,1,0:T(8,128)(2,1)}, u32[]{:S(2)}, u32[]{:S(2)}) async-start(bf16[64,1,32,1024]{3,2,1,0:T(8,128)(2,1)} %fusion.2), calls=%async_computation.1 | async-start | bytes 8388608 | tf_op jit(solution)/shard_map/all_to_all | solution.py:291
  402.3 4.1 select_reduce_fusion
  406.4 89.5 %all-to-all-done.1 = bf16[64,1,32,1024]{3,2,1,0:T(8,128)(2,1)} async-done(((bf16[64,1,32,1024]{3,2,1,0:T(8,128)(2,1)}), bf16[64,1,32,1024]{3,2,1,0:T(8,128)(2,1)}, u32[]{:S(2)}, u32[]{:S(2)}) %all-to-all-start.1) | async-done | bytes 4194336 | tf_op jit(solution)/shard_map/all_to_all | solution.py:291
  495.8 6.3 %convolution_convert_fusion.1 = bf16[256,1024]{1,0:T(8,128)(2,1)S(1)} fusion(f32[256,2048]{1,0:T(8,128)} %select_reduce_fusion, bf16[2048,1024]{1,0:T(8,128)(2,1)} %bitcast.68), kind=kOutput, calls=%fused_computation.31 | convolution fusion | flops 6442713088 | bytes 6815744 | tf_op jit(solution)/shard_map/dot_general | solution.py:298
  502.1 0.4 reshape.214
  502.5 1.1 constant_dynamic-slice_fusion.1
  503.6 2.4 collective-permute-start.5
  506.1 1.2 collective-permute-done.5
  507.3 2.7 collective-permute-start.6
  510.0 14.8 %collective-permute-done.6 = bf16[256,512]{1,0:T(8,128)(2,1)S(1)} collective-permute-done((bf16[256,512]{1,0:T(8,128)(2,1)S(1)}, bf16[256,512]{1,0:T(8,128)(2,1)S(1)}, u32[]{:S(2)}, u32[]{:S(2)}) %collective-permute-start.6) | collective-permute-done | bytes 262176 | tf_op jit(solution)/shard_map/ppermute | solution.py:167
  524.9 0.6 collective-permute-start.7
  525.6 0.8 copy.103
  526.4 0.6 collective-permute-done.7
  527.0 1.0 fusion.53
  (51 shorter events, 1.3 us)
Async XLA Ops:
  7.2 177.2 %copy-start = (bf16[256,1024]{1,0:T(8,128)(2,1)S(1)}, bf16[256,1024]{1,0:T(8,128)(2,1)}, u32[]{:S(2)}) copy-start(bf16[256,1024]{1,0:T(8,128)(2,1)} %param.22) | copy-start | bytes 1572868
  7.2 81.5 %copy-start.7 = (s32[256,8]{0,1:T(8,128)S(1)}, s32[256,8]{0,1:T(8,128)}, u32[]{:S(2)}) copy-start(s32[256,8]{0,1:T(8,128)} %param.15) | copy-start | bytes 24580
  7.2 80.5 %all-gather.3.cloned.1.call-start = ((), (), s32[]{:S(2)}) async-start(), calls=%async_computation.2 | async-start | bytes 2621440 | tf_op jit(solution)/shard_map/all_gather | solution.py:226
  20.2 72.9 %copy-start.3 = (bf16[256,1024]{1,0:T(8,128)(2,1)S(1)}, bf16[256,1024]{1,0:T(8,128)(2,1)}, u32[]{:S(2)}) copy-start(bf16[256,1024]{1,0:T(8,128)(2,1)} %param.13) | copy-start | bytes 1572868
  33.1 142.0 %all-gather.5.cloned.1.call-start = ((), (), s32[]{:S(2)}) async-start(), calls=%async_computation.3 | async-start | bytes 10485760 | tf_op jit(solution)/shard_map/all_gather | solution.py:226
  184.1 17.5 %copy-start.9 = (bf16[1024]{0:T(1024)(128)(2,1)S(1)}, bf16[1024]{0:T(1024)(128)(2,1)}, u32[]{:S(2)}) copy-start(bf16[1024]{0:T(1024)(128)(2,1)} %param.18) | copy-start | bytes 6148
  186.2 2.1 collective-permute-start
  188.4 11.7 %collective-permute-start.1 = (bf16[256,512]{1,0:T(8,128)(2,1)S(1)}, bf16[256,512]{1,0:T(8,128)(2,1)S(1)}, u32[]{:S(2)}, u32[]{:S(2)}) collective-permute-start(bf16[256,512]{1,0:T(8,128)(2,1)S(1)} %fusion.61), channel_id=1, source_target_pairs={{0,2},{2,0},{1,3},{3,1},{4,6},{6,4},{5,7},{7,5},{8,10},{10,8},{9,1... | collective-permute-start | bytes 786440 | tf_op jit(solution)/shard_map/ppermute | solution.py:167
  200.1 3.2 collective-permute-start.2
  206.1 163.8 %copy-start.4 = (bf16[1,1024,128]{2,1,0:T(8,128)(2,1)S(1)}, bf16[1,1024,128]{2,1,0:T(8,128)(2,1)}, u32[]{:S(2)}) copy-start(bf16[1,1024,128]{2,1,0:T(8,128)(2,1)} %param.23) | copy-start | bytes 786436
  356.8 1.9 copy-start.1
  356.8 14.4 %copy-start.5 = (bf16[1,128,1024]{2,1,0:T(8,128)(2,1)S(1)}, bf16[1,128,1024]{2,1,0:T(8,128)(2,1)}, u32[]{:S(2)}) copy-start(bf16[1,128,1024]{2,1,0:T(8,128)(2,1)} %param.25) | copy-start | bytes 786436
  356.8 14.4 %copy-start.6 = (bf16[1,1024,128]{2,1,0:T(8,128)(2,1)S(1)}, bf16[1,1024,128]{2,1,0:T(8,128)(2,1)}, u32[]{:S(2)}) copy-start(bf16[1,1024,128]{2,1,0:T(8,128)(2,1)} %param.24) | copy-start | bytes 786436
  358.7 9.2 %collective-permute-start.3 = (bf16[64,1,32,1024]{3,2,0,1:T(8,128)(2,1)S(1)}, bf16[64,1,32,1024]{3,2,0,1:T(8,128)(2,1)S(1)}, u32[]{:S(2)}, u32[]{:S(2)}) collective-permute-start(bf16[64,1,32,1024]{3,2,0,1:T(8,128)(2,1)S(1)} %bitcast.189), channel_id=1, source_target_pairs={{0,1},{1,0},{2,3},{3,2},{4,5},{5,4},{6,7},{7,6},{8,9},{9,8},{10,11... | collective-permute-start | bytes 12582920 | tf_op jit(solution)/shard_map/ppermute | solution.py:278
  367.9 2.0 copy-start.2
  379.4 7.5 %collective-permute-start.4 = (bf16[64,1,32,1024]{3,2,0,1:T(8,128)(2,1)}, bf16[64,1,32,1024]{3,2,0,1:T(8,128)(2,1)}, u32[]{:S(2)}, u32[]{:S(2)}) collective-permute-start(bf16[64,1,32,1024]{3,2,0,1:T(8,128)(2,1)} %convert_bitcast_fusion), channel_id=1, source_target_pairs={{0,1},{1,0},{2,3},{3,2},{4,5},{5,4},{6,7},{7,6},{8,9},{9,8},{10,11... | collective-permute-start | bytes 12582920 | tf_op jit(solution)/shard_map/ppermute | solution.py:286
  396.5 5.8 %copy-start.8 = (f32[256,8]{0,1:T(8,128)S(1)}, f32[256,8]{0,1:T(8,128)}, u32[]{:S(2)}) copy-start(f32[256,8]{0,1:T(8,128)} %param.16) | copy-start | bytes 24580
  396.5 99.4 %all-to-all-start.1 = ((bf16[64,1,32,1024]{3,2,1,0:T(8,128)(2,1)}), bf16[64,1,32,1024]{3,2,1,0:T(8,128)(2,1)}, u32[]{:S(2)}, u32[]{:S(2)}) async-start(bf16[64,1,32,1024]{3,2,1,0:T(8,128)(2,1)} %fusion.2), calls=%async_computation.1 | async-start | bytes 8388608 | tf_op jit(solution)/shard_map/all_to_all | solution.py:291
  503.6 3.6 collective-permute-start.5
  507.3 17.5 %collective-permute-start.6 = (bf16[256,512]{1,0:T(8,128)(2,1)S(1)}, bf16[256,512]{1,0:T(8,128)(2,1)S(1)}, u32[]{:S(2)}, u32[]{:S(2)}) collective-permute-start(bf16[256,512]{1,0:T(8,128)(2,1)S(1)} %fusion.60), channel_id=1, source_target_pairs={{0,2},{2,0},{1,3},{3,1},{4,6},{6,4},{5,7},{7,5},{8,10},{10,8},{9,1... | collective-permute-start | bytes 786440 | tf_op jit(solution)/shard_map/ppermute | solution.py:167
  524.9 2.1 collective-permute-start.7
Sparse Core Ops, SparseCore 0:
  33.3 54.4 all-gather.2
  89.5 85.5 all-gather.4

commit v13 on v10

--- a/solution.py
+++ b/solution.py
@@ -154,7 +154,7 @@
     return jnp.stack([out[head, :, :, head] for head in range(kv_heads)])
 
 
-def tp_sum(partial):
+def tp_sum_into(partial, base):
     swap = [(0, 1), (1, 0)]
     core = lax.axis_index("tc")
     rows, width = partial.shape
@@ -164,11 +164,13 @@
     pair = mine.astype(jnp.float32) + lax.ppermute(theirs, "tc", swap).astype(jnp.float32)
     pair = pair.astype(jnp.bfloat16)
     summed = pair.astype(jnp.float32) + lax.ppermute(pair, "tz", swap).astype(jnp.float32)
-    other = lax.ppermute(summed, "tc", swap)
+    base_half = lax.dynamic_index_in_dim(base.reshape(rows, 2, width // 2), core, axis=1, keepdims=False)
+    own_out = (base_half.astype(jnp.float32) + summed).astype(jnp.bfloat16)
+    other = lax.ppermute(own_out, "tc", swap)
     return jnp.where(
         core == 0,
-        jnp.concatenate([summed, other], axis=1),
-        jnp.concatenate([other, summed], axis=1),
+        jnp.concatenate([own_out, other], axis=1),
+        jnp.concatenate([other, own_out], axis=1),
     )
 
 
@@ -268,8 +270,7 @@
     )
     attended = attended.astype(jnp.bfloat16)
     partial_out = jnp.dot(attended, w_out, preferred_element_type=jnp.float32)
-    attn_mixed = tp_sum(partial_out.astype(jnp.bfloat16))
-    residual = (hidden.astype(jnp.float32) + attn_mixed).astype(jnp.bfloat16)
+    residual = tp_sum_into(partial_out.astype(jnp.bfloat16), hidden)
     normed_moe = normalize(residual, norm_moe).astype(jnp.bfloat16)
     outbound = jnp.dot(dispatch, normed_moe, preferred_element_type=jnp.float32).astype(jnp.bfloat16)
     outbound = outbound.reshape(seq_count, slots_dev, half, model_width)
@@ -297,8 +298,7 @@
     combined = jnp.dot(
         weighting, returned, preferred_element_type=jnp.float32, precision=lax.Precision.HIGHEST
     )
-    expert_sum = tp_sum(combined.astype(jnp.bfloat16))
-    hidden_out = (residual.astype(jnp.float32) + expert_sum).astype(jnp.bfloat16)
+    hidden_out = tp_sum_into(combined.astype(jnp.bfloat16), residual)
     return (hidden_out, kv_cache)
 
 

time: 523 us -> 537 us (1.027)
  starting transfers between devices: 22.3 us -> 35.3 us
    ppermute x1, starting transfers between devices: 0.37 us -> 10.2 us  [per_device(): sibling_part = lax.ppermute(expert_rows(arrived_other), 'tc', swap)]
where the time goes in v13:
time: 537 us; the launch traced here: 534 us
  waiting for transfers between devices  251 us (47%)
  blocking collectives  152 us (28%)
  starting transfers between devices  35.3 us (7%)
  matrix products  34.5 us (6%)
  other arithmetic  22.6 us (4%)
  local copies, waits for them, and re-layouts  16.4 us (3%)
  between operations  14.7 us (3%)
  Pallas kernels  7.04 us (1%)
    all_to_all x1, blocking collectives, per_device(): lax.all_to_all(outbound, SUB_AXES, split_axis=0, concat_axis=0, tiled=True)  139 us
    all_gather x2, waiting for transfers between devices, per_device(): joined = lax.all_gather(joined, axis_name, axis=0, tiled=True)  130 us
    all_to_all x1, waiting for transfers between devices, per_device(): lax.all_to_all(pair_sum, SUB_AXES, split_axis=0, concat_axis=0, tiled=True)  89.5 us
    ppermute x2, waiting for transfers between devices, tp_sum_into(): lax.ppermute(pair, 'tz', swap).astype(jnp.float32)  18.1 us
    dot_general x2, matrix products, expert_rows(): jnp.einsum('jsrf,sfd->jsrd', activated, w_down, preferred_element_type=jn...  17.8 us
    all_gather x1, blocking collectives, per_device(): joined = lax.all_gather(joined, axis_name, axis=0, tiled=True)  12.9 us
  transfers between devices with their start and end apart: 11, of which 11 were waited for; matrix products, arithmetic and copies ran while one was open for 4% of the time, Pallas kernels for 0%

profile of v13, /device:TPU:1, one launch (start us, length us, event | category | flops | bytes accessed | tf_op | source)
XLA Modules:
  0.0 533.7 jit_solution(7441249523997146066)
XLA Ops:
  7.3 1.1 convert_reduce_fusion
  8.4 0.7 fusion.99
  9.0 0.7 convert_element_type.178
  9.7 1.2 fusion.46
  11.0 5.8 %fusion.89 = (f32[256]{0:T(256)S(1)}, s32[256]{0:T(256)S(1)}) fusion(s32[]{:T(128)} %bitcast.6, s32[]{:T(128)} %bitcast.7, s32[]{:T(128)} %bitcast.8, s32[]{:T(128)} %bitcast.9, s32[]{:T(128)} %bitcast.10, s32[]{:T(128)} %bitcast.11, s32[]{:T(128)} %bitcast.12, s32[]{:T(128)} %bitcast.13, s32[]{:T(128)S(6)} %mul.169, s32[16384]{0:T(1024)} %param.14, ...), kind=kLoop, calls=%fused_computation.127 | loop fusion | flops 5120 | bytes 3112 | tf_op jit(solution)/shard_map/convert_element_type | solution.py:32
  17.0 1.5 fusion.95
  18.6 1.5 convolution_convert_fusion.3
  20.2 12.9 %all_gather.9 = bf16[1024,256]{1,0:T(8,128)(2,1)} all-gather(bf16[256,256]{1,0:T(8,128)(2,1)S(1)} %pad_maximum_fusion), channel_id=1, replica_groups=mesh['sy'=4,'sz'=4,'sx'=4,'tz'=2,'tc'=2] {'sx'}, dimensions={0}, use_global_device_ids=true | all-gather | bytes 655360 | tf_op jit(solution)/shard_map/all_gather | solution.py:227
  33.1 54.5 %all-gather.3.cloned.1.call-done = bf16[4096,256]{1,0:T(8,128)(2,1)} async-done(((bf16[1024,256]{1,0:T(8,128)(2,1)}), bf16[4096,256]{1,0:T(8,128)(2,1)}) %all-gather.3.cloned.1.call-update) | async-done | bytes 2097168 | tf_op jit(solution)/shard_map/all_gather | solution.py:227
  87.7 0.9 slice.26
  88.9 0.6 fusion.41
  89.7 3.0 fusion
  92.8 0.2 convert_element_type.188
  93.0 0.4 fusion.97
  93.9 0.5 slice.27
  94.4 0.8 copy.106.qseg_ref
  95.2 1.3 fusion.90
  96.6 1.3 pad_add_fusion.bounds_ref
  97.9 0.7 iota_add_fusion.qidx_ref
  98.6 0.8 broadcast_select_fusion.q_ref
  99.3 75.8 %all-gather.5.cloned.1.call-done.k_ref.v_ref = bf16[16384,256]{1,0:T(8,128)(2,1)} async-done(((bf16[4096,256]{1,0:T(8,128)(2,1)}), bf16[16384,256]{1,0:T(8,128)(2,1)}) %all-gather.5.cloned.1.call-update) | async-done | bytes 8388624 | tf_op jit(solution)/shard_map/all_gather | solution.py:227
  175.1 7.0 %shard_map.140 = f32[4,256,128]{2,1,0:T(8,128)} custom-call(s32[2]{0:T(128)} %pad_add_fusion.bounds_ref, bf16[2,2,256,128]{3,2,1,0:T(8,128)(2,1)} %broadcast_select_fusion.q_ref, bf16[16384,256]{1,0:T(8,128)(2,1)} %all-gather.5.cloned.1.call-done.k_ref.v_ref, bf16[16384,256]{1,0:T(8,128)(2,1)} %all-gather.5.cloned.1.call-done.k_ref.v_ref, ...), custom_call_target="tpu_custom_call" | custom-call | tf_op jit(solution)/shard_map/pallas_call | solution.py:139
  182.1 1.1 convert.34
  183.4 0.3 convolution_convert_fusion.2
  183.8 0.4 reshape.218
  184.1 1.9 constant_dynamic-slice_fusion.3
  186.0 1.2 copy.125
  187.2 1.2 collective-permute-start
  188.4 0.5 copy.121
  188.9 0.7 collective-permute-done
  189.7 5.5 %collective-permute-start.1 = (bf16[256,512]{0,1:T(8,128)(2,1)S(1)}, bf16[256,512]{0,1:T(8,128)(2,1)S(1)}, u32[]{:S(2)}, u32[]{:S(2)}) collective-permute-start(bf16[256,512]{0,1:T(8,128)(2,1)S(1)} %fusion.60), channel_id=1, source_target_pairs={{0,2},{2,0},{1,3},{3,1},{4,6},{6,4},{5,7},{7,5},{8,10},{10,8},{9,1... | collective-permute-start | bytes 786440 | tf_op jit(solution)/shard_map/ppermute | solution.py:166
  195.4 5.9 %collective-permute-done.1 = bf16[256,512]{0,1:T(8,128)(2,1)S(1)} collective-permute-done((bf16[256,512]{0,1:T(8,128)(2,1)S(1)}, bf16[256,512]{0,1:T(8,128)(2,1)S(1)}, u32[]{:S(2)}, u32[]{:S(2)}) %collective-permute-start.1) | collective-permute-done | bytes 262176 | tf_op jit(solution)/shard_map/ppermute | solution.py:166
  201.4 1.3 collective-permute-start.2
  202.8 1.2 collective-permute-done.2
  203.9 0.2 fusion.49
  204.2 1.4 convolution_convert_fusion
  205.6 139.1 %all_to_all.10 = bf16[64,1,32,1024]{3,2,1,0:T(8,128)(2,1)S(1)} all-to-all(bf16[64,1,32,1024]{3,2,1,0:T(8,128)(2,1)S(1)} %bitcast.193), channel_id=1, replica_groups=mesh['sy'=4,'sz'=4,'sx'=4,'tz'=2,'tc'=2] {'sy','sz','sx'}, dimensions={0} | all-to-all | bytes 8388608 | tf_op jit(solution)/shard_map/all_to_all | solution.py:277
  344.7 2.0 copy-done.1
  346.6 2.4 collective-permute-start.3
  349.1 6.8 %collective-permute-done.3 = bf16[64,1,32,1024]{3,2,0,1:T(8,128)(2,1)S(1)} collective-permute-done((bf16[64,1,32,1024]{3,2,0,1:T(8,128)(2,1)S(1)}, bf16[64,1,32,1024]{3,2,0,1:T(8,128)(2,1)S(1)}, u32[]{:S(2)}, u32[]{:S(2)}) %collective-permute-start.3) | collective-permute-done | bytes 4194336 | tf_op jit(solution)/shard_map/ppermute | solution.py:278
  355.8 2.0 copy-done.2
  357.8 1.3 fusion.20
  359.1 8.3 %convert_bitcast_fusion = bf16[64,1,32,1024]{3,2,0,1:T(8,128)(2,1)} fusion(f32[64,1,32,128]{3,2,0,1:T(8,128)S(1)} %fusion.20, bf16[64,1,32,1024]{3,2,0,1:T(8,128)(2,1)} %copy-done.2, bf16[1,128,1024]{2,1,0:T(8,128)(2,1)S(1)} %copy-done.5, bf16[1,1024,128]{2,1,0:T(8,128)(2,1)S(1)} %copy-done.6), kind=kOutput, calls=%fused_computation.15 | convolution fusion | flops 1077411840 | bytes 9961472 | tf_op jit(solution)/shard_map/jsrf,sfd->jsrd/dot_general | solution.py:283
  367.4 10.2 %collective-permute-start.4 = (bf16[64,1,32,1024]{3,2,0,1:T(8,128)(2,1)}, bf16[64,1,32,1024]{3,2,0,1:T(8,128)(2,1)}, u32[]{:S(2)}, u32[]{:S(2)}) collective-permute-start(bf16[64,1,32,1024]{3,2,0,1:T(8,128)(2,1)} %convert_bitcast_fusion), channel_id=1, source_target_pairs={{0,1},{1,0},{2,3},{3,2},{4,5},{5,4},{6,7},{7,6},{8,9},{9,8},{10,11... | collective-permute-start | bytes 12582920 | tf_op jit(solution)/shard_map/ppermute | solution.py:286
  377.6 3.4 fusion.14
  381.0 3.7 collective-permute-done.4
  384.7 9.5 %fusion.2 = bf16[64,1,32,1024]{3,2,1,0:T(8,128)(2,1)} fusion(bf16[64,1,32,1024]{3,2,0,1:T(8,128)(2,1)} %collective-permute-done.4, bf16[64,1,32,1024]{3,2,1,0:T(8,128)(2,1)} %copy-done.1, f32[64,1,32,128]{3,2,0,1:T(8,128)S(1)} %fusion.14, bf16[1,128,1024]{2,1,0:T(8,128)(2,1)S(1)} %copy-done.5, bf16[1,1024,128]{2,1,0:T(8,128)(2,1)S(1)} %copy-done.6), kind=kOutput, calls=%fused_computation.6 | convolution fusion | flops 1085800448 | bytes 14155776 | tf_op jit(solution)/shard_map/jsrf,sfd->jsrd/dot_general | solution.py:283
  394.2 5.8 %all-to-all-start.1 = ((bf16[64,1,32,1024]{3,2,1,0:T(8,128)(2,1)}), bf16[64,1,32,1024]{3,2,1,0:T(8,128)(2,1)}, u32[]{:S(2)}, u32[]{:S(2)}) async-start(bf16[64,1,32,1024]{3,2,1,0:T(8,128)(2,1)} %fusion.2), calls=%async_computation.1 | async-start | bytes 8388608 | tf_op jit(solution)/shard_map/all_to_all | solution.py:291
  400.0 4.1 select_reduce_fusion
  404.1 89.5 %all-to-all-done.1 = bf16[64,1,32,1024]{3,2,1,0:T(8,128)(2,1)} async-done(((bf16[64,1,32,1024]{3,2,1,0:T(8,128)(2,1)}), bf16[64,1,32,1024]{3,2,1,0:T(8,128)(2,1)}, u32[]{:S(2)}, u32[]{:S(2)}) %all-to-all-start.1) | async-done | bytes 4194336 | tf_op jit(solution)/shard_map/all_to_all | solution.py:291
  493.6 6.3 %convolution_convert_fusion.1 = bf16[256,1024]{1,0:T(8,128)(2,1)S(1)} fusion(f32[256,2048]{1,0:T(8,128)} %select_reduce_fusion, bf16[2048,1024]{1,0:T(8,128)(2,1)} %bitcast.73), kind=kOutput, calls=%fused_computation.29 | convolution fusion | flops 6442713088 | bytes 6815744 | tf_op jit(solution)/shard_map/dot_general | solution.py:298
  499.9 0.4 reshape.228
  500.3 1.1 constant_dynamic-slice_fusion.1
  501.4 0.5 copy.126
  501.8 2.4 collective-permute-start.5
  504.3 0.5 copy.123
  504.8 0.7 collective-permute-done.5
  505.5 4.9 collective-permute-start.6
  510.4 12.2 %collective-permute-done.6 = bf16[256,512]{0,1:T(8,128)(2,1)S(1)} collective-permute-done((bf16[256,512]{0,1:T(8,128)(2,1)S(1)}, bf16[256,512]{0,1:T(8,128)(2,1)S(1)}, u32[]{:S(2)}, u32[]{:S(2)}) %collective-permute-start.6) | collective-permute-done | bytes 262176 | tf_op jit(solution)/shard_map/ppermute | solution.py:166
  522.6 0.3 fusion.59
  522.9 1.4 collective-permute-start.7
  524.4 0.8 copy.119
  525.4 0.2 maximum_select_fusion.1
  525.6 1.0 copy.118
  (61 shorter events, 2.3 us)
Async XLA Ops:
  7.2 176.2 %copy-start = (bf16[256,1024]{1,0:T(8,128)(2,1)S(1)}, bf16[256,1024]{1,0:T(8,128)(2,1)}, u32[]{:S(2)}) copy-start(bf16[256,1024]{1,0:T(8,128)(2,1)} %param.22) | copy-start | bytes 1572868
  7.2 81.5 %copy-start.9 = (s32[256,8]{0,1:T(8,128)S(1)}, s32[256,8]{0,1:T(8,128)}, u32[]{:S(2)}) copy-start(s32[256,8]{0,1:T(8,128)} %param.15) | copy-start | bytes 24580
  7.2 80.5 %all-gather.3.cloned.1.call-start = ((), (), s32[]{:S(2)}) async-start(), calls=%async_computation.2 | async-start | bytes 2621440 | tf_op jit(solution)/shard_map/all_gather | solution.py:227
  20.1 72.6 %copy-start.7 = (bf16[256,128]{1,0:T(8,128)(2,1)}, bf16[256,128]{1,0:T(8,128)(2,1)S(1)}, u32[]{:S(2)}) copy-start(bf16[256,128]{1,0:T(8,128)(2,1)S(1)} %convolution_convert_fusion.3) | copy-start | bytes 196612
  20.1 72.9 %copy-start.3 = (bf16[256,1024]{1,0:T(8,128)(2,1)S(1)}, bf16[256,1024]{1,0:T(8,128)(2,1)}, u32[]{:S(2)}) copy-start(bf16[256,1024]{1,0:T(8,128)(2,1)} %param.13) | copy-start | bytes 1572868
  20.1 72.9 %copy-start.12 = (bf16[1024,256]{1,0:T(8,128)(2,1)S(1)}, bf16[1024,256]{1,0:T(8,128)(2,1)}, u32[]{:S(2)}) copy-start(bf16[1024,256]{1,0:T(8,128)(2,1)} %param.19) | copy-start | bytes 1572868
  33.1 142.0 %all-gather.5.cloned.1.call-start = ((), (), s32[]{:S(2)}) async-start(), calls=%async_computation.3 | async-start | bytes 10485760 | tf_op jit(solution)/shard_map/all_gather | solution.py:227
  183.4 19.3 %copy-start.11 = (bf16[1024]{0:T(1024)(128)(2,1)S(1)}, bf16[1024]{0:T(1024)(128)(2,1)}, u32[]{:S(2)}) copy-start(bf16[1024]{0:T(1024)(128)(2,1)} %param.18) | copy-start | bytes 6148
  187.2 2.4 collective-permute-start
  189.7 11.6 %collective-permute-start.1 = (bf16[256,512]{0,1:T(8,128)(2,1)S(1)}, bf16[256,512]{0,1:T(8,128)(2,1)S(1)}, u32[]{:S(2)}, u32[]{:S(2)}) collective-permute-start(bf16[256,512]{0,1:T(8,128)(2,1)S(1)} %fusion.60), channel_id=1, source_target_pairs={{0,2},{2,0},{1,3},{3,1},{4,6},{6,4},{5,7},{7,5},{8,10},{10,8},{9,1... | collective-permute-start | bytes 786440 | tf_op jit(solution)/shard_map/ppermute | solution.py:166
  201.4 2.5 collective-permute-start.2
  205.6 152.3 %copy-start.4 = (bf16[1,1024,128]{2,1,0:T(8,128)(2,1)S(1)}, bf16[1,1024,128]{2,1,0:T(8,128)(2,1)}, u32[]{:S(2)}) copy-start(bf16[1,1024,128]{2,1,0:T(8,128)(2,1)} %param.23) | copy-start | bytes 786436
  344.7 2.0 copy-start.1
  344.7 14.4 %copy-start.5 = (bf16[1,128,1024]{2,1,0:T(8,128)(2,1)S(1)}, bf16[1,128,1024]{2,1,0:T(8,128)(2,1)}, u32[]{:S(2)}) copy-start(bf16[1,128,1024]{2,1,0:T(8,128)(2,1)} %param.25) | copy-start | bytes 786436
  344.7 14.4 %copy-start.6 = (bf16[1,1024,128]{2,1,0:T(8,128)(2,1)S(1)}, bf16[1,1024,128]{2,1,0:T(8,128)(2,1)}, u32[]{:S(2)}) copy-start(bf16[1,1024,128]{2,1,0:T(8,128)(2,1)} %param.24) | copy-start | bytes 786436
  346.6 9.2 %collective-permute-start.3 = (bf16[64,1,32,1024]{3,2,0,1:T(8,128)(2,1)S(1)}, bf16[64,1,32,1024]{3,2,0,1:T(8,128)(2,1)S(1)}, u32[]{:S(2)}, u32[]{:S(2)}) collective-permute-start(bf16[64,1,32,1024]{3,2,0,1:T(8,128)(2,1)S(1)} %bitcast.194), channel_id=1, source_target_pairs={{0,1},{1,0},{2,3},{3,2},{4,5},{5,4},{6,7},{7,6},{8,9},{9,8},{10,11... | collective-permute-start | bytes 12582920 | tf_op jit(solution)/shard_map/ppermute | solution.py:278
  355.8 2.0 copy-start.2
  367.4 17.3 %collective-permute-start.4 = (bf16[64,1,32,1024]{3,2,0,1:T(8,128)(2,1)}, bf16[64,1,32,1024]{3,2,0,1:T(8,128)(2,1)}, u32[]{:S(2)}, u32[]{:S(2)}) collective-permute-start(bf16[64,1,32,1024]{3,2,0,1:T(8,128)(2,1)} %convert_bitcast_fusion), channel_id=1, source_target_pairs={{0,1},{1,0},{2,3},{3,2},{4,5},{5,4},{6,7},{7,6},{8,9},{9,8},{10,11... | collective-permute-start | bytes 12582920 | tf_op jit(solution)/shard_map/ppermute | solution.py:286
  394.2 5.8 %copy-start.10 = (f32[256,8]{0,1:T(8,128)S(1)}, f32[256,8]{0,1:T(8,128)}, u32[]{:S(2)}) copy-start(f32[256,8]{0,1:T(8,128)} %param.16) | copy-start | bytes 24580
  394.2 99.4 %all-to-all-start.1 = ((bf16[64,1,32,1024]{3,2,1,0:T(8,128)(2,1)}), bf16[64,1,32,1024]{3,2,1,0:T(8,128)(2,1)}, u32[]{:S(2)}, u32[]{:S(2)}) async-start(bf16[64,1,32,1024]{3,2,1,0:T(8,128)(2,1)} %fusion.2), calls=%async_computation.1 | async-start | bytes 8388608 | tf_op jit(solution)/shard_map/all_to_all | solution.py:291
  499.9 24.5 %copy-start.8 = (bf16[256,128]{1,0:T(8,128)(2,1)S(1)}, bf16[256,128]{1,0:T(8,128)(2,1)}, u32[]{:S(2)}) copy-start(bf16[256,128]{1,0:T(8,128)(2,1)} %copy-done.7) | copy-start | bytes 196612
  501.8 3.6 collective-permute-start.5
  505.5 17.1 %collective-permute-start.6 = (bf16[256,512]{0,1:T(8,128)(2,1)S(1)}, bf16[256,512]{0,1:T(8,128)(2,1)S(1)}, u32[]{:S(2)}, u32[]{:S(2)}) collective-permute-start(bf16[256,512]{0,1:T(8,128)(2,1)S(1)} %fusion.58), channel_id=1, source_target_pairs={{0,2},{2,0},{1,3},{3,1},{4,6},{6,4},{5,7},{7,5},{8,10},{10,8},{9,1... | collective-permute-start | bytes 786440 | tf_op jit(solution)/shard_map/ppermute | solution.py:166
  522.9 2.5 collective-permute-start.7
Sparse Core Ops, SparseCore 0:
  33.2 54.4 all-gather.2
  89.5 85.5 all-gather.4

commit v14 on v10

--- a/solution.py
+++ b/solution.py
@@ -282,8 +282,9 @@
         group_part = jnp.einsum("jsrf,sfd->jsrd", activated, w_down, preferred_element_type=jnp.float32)
         return group_part.astype(jnp.bfloat16)
 
+    own_part = expert_rows(arrived_own)
+    arrived_other, own_part = lax.optimization_barrier((arrived_other, own_part))
     sibling_part = lax.ppermute(expert_rows(arrived_other), "tc", swap)
-    own_part = expert_rows(arrived_own)
     pair_sum = (own_part.astype(jnp.float32) + sibling_part.astype(jnp.float32)).astype(
         jnp.bfloat16
     )

time: 523 us -> 532 us (1.017); the launches traced: 523 us -> 522 us
  other arithmetic: 24.4 us -> 30.5 us
    ppermute x1, waiting for transfers between devices: 6.79 us -> 0.01 us  [per_device(): arrived_other = lax.ppermute(arrived_own, 'tc', swap)]
    convert_element_type x0 -> x1, other arithmetic: none -> 6.35 us  [per_device(): (own_part.astype(jnp.float32) + sibling_part.astype(jnp.float32)).astype(...]
  transfers between devices with their start and end apart: 11 -> 11, of which waited for: 11 -> 10; matrix products, arithmetic and copies ran while one was open for 4% -> 6% of each run, Pallas kernels for 0% -> 0%
where the time goes in v14:
time: 532 us; the launch traced here: 522 us
  waiting for transfers between devices  252 us (47%)
  blocking collectives  150 us (28%)
  matrix products  36.3 us (7%)
  other arithmetic  30.5 us (6%)
  starting transfers between devices  24.2 us (5%)
  between operations  14.9 us (3%)
  local copies, waits for them, and re-layouts  7.85 us (1%)
  Pallas kernels  7.05 us (1%)
    all_to_all x1, blocking collectives, per_device(): lax.all_to_all(outbound, SUB_AXES, split_axis=0, concat_axis=0, tiled=True)  137 us
    all_gather x2, waiting for transfers between devices, per_device(): joined = lax.all_gather(joined, axis_name, axis=0, tiled=True)  130 us
    all_to_all x1, waiting for transfers between devices, per_device(): lax.all_to_all(pair_sum, SUB_AXES, split_axis=0, concat_axis=0, tiled=True)  91.3 us
    ppermute x2, waiting for transfers between devices, tp_sum(): lax.ppermute(pair, 'tz', swap).astype(jnp.float32)  18.8 us
    dot_general x2, matrix products, expert_rows(): jnp.einsum('jsrf,sfd->jsrd', activated, w_down, preferred_element_type=jn...  16.5 us
    all_gather x1, blocking collectives, per_device(): joined = lax.all_gather(joined, axis_name, axis=0, tiled=True)  12.9 us
  transfers between devices with their start and end apart: 11, of which 10 were waited for; matrix products, arithmetic and copies ran while one was open for 6% of the time, Pallas kernels for 0%

profile of v14, /device:TPU:1, one launch (start us, length us, event | category | flops | bytes accessed | tf_op | source)
XLA Modules:
  0.0 522.1 jit_solution(17216122601305599705)
XLA Ops:
  7.3 1.1 convert_reduce_fusion
  8.4 0.7 fusion.89
  9.0 0.7 convert_element_type.163
  9.7 1.2 fusion.43
  10.9 5.7 %fusion.79 = (f32[256]{0:T(256)S(1)}, s32[256]{0:T(256)S(1)}) fusion(s32[]{:T(128)} %bitcast.4, s32[]{:T(128)} %bitcast.5, s32[]{:T(128)} %bitcast.6, s32[]{:T(128)} %bitcast.7, s32[]{:T(128)} %bitcast.8, s32[]{:T(128)} %bitcast.9, s32[]{:T(128)} %bitcast.10, s32[]{:T(128)} %bitcast.11, s32[]{:T(128)S(6)} %mul.169, s32[16384]{0:T(1024)} %param.14, ...), kind=kLoop, calls=%fused_computation.116 | loop fusion | flops 5120 | bytes 3112 | tf_op jit(solution)/shard_map/convert_element_type | solution.py:32
  16.6 0.2 multiply_cosine_fusion
  16.8 1.5 fusion.84
  18.4 0.1 copy.84
  18.5 1.5 convolution_convert_fusion.3
  20.0 12.9 %all_gather.9 = bf16[1024,256]{1,0:T(8,128)(2,1)} all-gather(bf16[256,256]{1,0:T(8,128)(2,1)S(1)} %pad_maximum_fusion), channel_id=1, replica_groups=mesh['sy'=4,'sz'=4,'sx'=4,'tz'=2,'tc'=2] {'sx'}, dimensions={0}, use_global_device_ids=true | all-gather | bytes 655360 | tf_op jit(solution)/shard_map/all_gather | solution.py:225
  33.0 54.5 %all-gather.3.cloned.1.call-done = bf16[4096,256]{1,0:T(8,128)(2,1)} async-done(((bf16[1024,256]{1,0:T(8,128)(2,1)}), bf16[4096,256]{1,0:T(8,128)(2,1)}) %all-gather.3.cloned.1.call-update) | async-done | bytes 2097168 | tf_op jit(solution)/shard_map/all_gather | solution.py:225
  87.5 0.9 slice.26
  88.5 0.1 copy.85
  88.6 0.1 eq.60
  88.7 0.6 fusion.40
  89.3 0.1 convert_element_type.172
  89.5 3.0 fusion
  92.6 0.2 convert_element_type.173
  92.8 1.5 fusion.86
  94.4 0.2 copy.82
  94.8 0.5 slice.27
  95.3 0.8 copy.91.qseg_ref
  96.1 1.2 fusion.80
  97.3 1.2 pad_add_fusion.bounds_ref
  98.5 0.7 iota_add_fusion.qidx_ref
  99.2 0.7 broadcast_select_fusion.q_ref
  99.9 75.0 %all-gather.5.cloned.1.call-done.k_ref.v_ref = bf16[16384,256]{1,0:T(8,128)(2,1)} async-done(((bf16[4096,256]{1,0:T(8,128)(2,1)}), bf16[16384,256]{1,0:T(8,128)(2,1)}) %all-gather.5.cloned.1.call-update) | async-done | bytes 8388624 | tf_op jit(solution)/shard_map/all_gather | solution.py:225
  174.9 7.0 %shard_map.140 = f32[4,256,128]{2,1,0:T(8,128)} custom-call(s32[2]{0:T(128)} %pad_add_fusion.bounds_ref, bf16[2,2,256,128]{3,2,1,0:T(8,128)(2,1)} %broadcast_select_fusion.q_ref, bf16[16384,256]{1,0:T(8,128)(2,1)} %all-gather.5.cloned.1.call-done.k_ref.v_ref, bf16[16384,256]{1,0:T(8,128)(2,1)} %all-gather.5.cloned.1.call-done.k_ref.v_ref, ...), custom_call_target="tpu_custom_call" | custom-call | tf_op jit(solution)/shard_map/pallas_call | solution.py:139
  182.0 1.1 convert.29
  183.1 0.1 copy.92
  183.3 0.3 convolution_convert_fusion.2
  183.6 0.4 reshape.203
  184.0 1.1 constant_dynamic-slice_fusion.3
  185.1 1.1 collective-permute-start
  186.2 1.2 collective-permute-done
  187.5 5.5 %collective-permute-start.1 = (bf16[256,512]{1,0:T(8,128)(2,1)S(1)}, bf16[256,512]{1,0:T(8,128)(2,1)S(1)}, u32[]{:S(2)}, u32[]{:S(2)}) collective-permute-start(bf16[256,512]{1,0:T(8,128)(2,1)S(1)} %fusion.55), channel_id=1, source_target_pairs={{0,2},{2,0},{1,3},{3,1},{4,6},{6,4},{5,7},{7,5},{8,10},{10,8},{9,1... | collective-permute-start | bytes 786440 | tf_op jit(solution)/shard_map/ppermute | solution.py:166
  193.0 6.1 %collective-permute-done.1 = bf16[256,512]{1,0:T(8,128)(2,1)S(1)} collective-permute-done((bf16[256,512]{1,0:T(8,128)(2,1)S(1)}, bf16[256,512]{1,0:T(8,128)(2,1)S(1)}, u32[]{:S(2)}, u32[]{:S(2)}) %collective-permute-start.1) | collective-permute-done | bytes 262176 | tf_op jit(solution)/shard_map/ppermute | solution.py:166
  199.2 1.3 collective-permute-start.2
  200.5 1.7 collective-permute-done.2
  202.2 1.5 fusion.47
  203.7 1.4 convolution_convert_fusion
  205.1 136.8 %all_to_all.10 = bf16[64,1,32,1024]{3,2,1,0:T(8,128)(2,1)} all-to-all(bf16[64,1,32,1024]{3,2,1,0:T(8,128)(2,1)S(1)} %bitcast.186), channel_id=1, replica_groups=mesh['sy'=4,'sz'=4,'sx'=4,'tz'=2,'tc'=2] {'sy','sz','sx'}, dimensions={0} | all-to-all | bytes 8388608 | tf_op jit(solution)/shard_map/all_to_all | solution.py:276
  341.9 2.6 collective-permute-start.3
  344.5 3.4 fusion.13
  347.9 8.2 %convert_bitcast_fusion.1 = bf16[64,1,32,1024]{3,2,0,1:T(8,128)(2,1)} fusion(bf16[64,1,32,1024]{3,2,1,0:T(8,128)(2,1)} %all_to_all.10, f32[64,1,32,128]{3,2,0,1:T(8,128)S(1)} %fusion.13, bf16[1,128,1024]{2,1,0:T(8,128)(2,1)S(1)} %copy-done.2, bf16[1,1024,128]{2,1,0:T(8,128)(2,1)S(1)} %copy-done.3), kind=kOutput, calls=%fused_computation.15 | convolution fusion | flops 1077411840 | bytes 9961472 | tf_op jit(solution)/shard_map/jsrf,sfd->jsrd/dot_general | solution.py:282
  356.2 3.4 fusion.19
  359.6 8.2 %convert_bitcast_fusion = bf16[64,1,32,1024]{3,2,0,1:T(8,128)(2,1)} fusion(f32[64,1,32,128]{3,2,0,1:T(8,128)S(1)} %fusion.19, bf16[64,1,32,1024]{3,2,1,0:T(8,128)(2,1)} %collective-permute-done.3, bf16[1,128,1024]{2,1,0:T(8,128)(2,1)S(1)} %copy-done.2, bf16[1,1024,128]{2,1,0:T(8,128)(2,1)S(1)} %copy-done.3), kind=kOutput, calls=%fused_computation.14 | convolution fusion | flops 1077411840 | bytes 9961472 | tf_op jit(solution)/shard_map/jsrf,sfd->jsrd/dot_general | solution.py:282
  367.9 7.3 %collective-permute-done.4 = bf16[64,1,32,1024]{3,2,0,1:T(8,128)(2,1)S(1)} collective-permute-done((bf16[64,1,32,1024]{3,2,0,1:T(8,128)(2,1)}, bf16[64,1,32,1024]{3,2,0,1:T(8,128)(2,1)S(1)}, u32[]{:S(2)}, u32[]{:S(2)}) %collective-permute-start.4) | collective-permute-done | bytes 4194336 | tf_op jit(solution)/shard_map/ppermute | solution.py:287
  375.2 6.4 %fusion.1 = bf16[64,1,32,1024]{3,2,1,0:T(8,128)(2,1)} fusion(bf16[64,1,32,1024]{3,2,0,1:T(8,128)(2,1)S(1)} %collective-permute-done.4, bf16[64,1,32,1024]{3,2,0,1:T(8,128)(2,1)} %convert_bitcast_fusion.1), kind=kLoop, calls=%fused_computation.5 | loop fusion | flops 8388608 | bytes 12582912 | tf_op jit(solution)/shard_map/convert_element_type | solution.py:288
  381.5 6.0 %all-to-all-start.1 = ((bf16[64,1,32,1024]{3,2,1,0:T(8,128)(2,1)}), bf16[64,1,32,1024]{3,2,1,0:T(8,128)(2,1)}, u32[]{:S(2)}, u32[]{:S(2)}) async-start(bf16[64,1,32,1024]{3,2,1,0:T(8,128)(2,1)} %fusion.1), calls=%async_computation.1 | async-start | bytes 8388608 | tf_op jit(solution)/shard_map/all_to_all | solution.py:291
  387.6 4.1 select_reduce_fusion
  391.7 91.3 %all-to-all-done.1 = bf16[64,1,32,1024]{3,2,1,0:T(8,128)(2,1)} async-done(((bf16[64,1,32,1024]{3,2,1,0:T(8,128)(2,1)}), bf16[64,1,32,1024]{3,2,1,0:T(8,128)(2,1)}, u32[]{:S(2)}, u32[]{:S(2)}) %all-to-all-start.1) | async-done | bytes 4194336 | tf_op jit(solution)/shard_map/all_to_all | solution.py:291
  483.0 6.3 %convolution_convert_fusion.1 = bf16[256,1024]{1,0:T(8,128)(2,1)S(1)} fusion(f32[256,2048]{1,0:T(8,128)} %select_reduce_fusion, bf16[2048,1024]{1,0:T(8,128)(2,1)} %bitcast.67), kind=kOutput, calls=%fused_computation.31 | convolution fusion | flops 6442713088 | bytes 6815744 | tf_op jit(solution)/shard_map/dot_general | solution.py:298
  489.2 0.4 reshape.213
  489.6 1.1 constant_dynamic-slice_fusion.1
  490.8 1.7 collective-permute-start.5
  492.4 1.2 collective-permute-done.5
  493.7 4.5 collective-permute-start.6
  498.1 12.6 %collective-permute-done.6 = bf16[256,512]{1,0:T(8,128)(2,1)S(1)} collective-permute-done((bf16[256,512]{1,0:T(8,128)(2,1)S(1)}, bf16[256,512]{1,0:T(8,128)(2,1)S(1)}, u32[]{:S(2)}, u32[]{:S(2)}) %collective-permute-start.6) | collective-permute-done | bytes 262176 | tf_op jit(solution)/shard_map/ppermute | solution.py:166
  510.9 1.4 collective-permute-start.7
  512.2 0.1 copy.99
  512.4 0.8 copy.100
  513.2 0.6 collective-permute-done.7
  513.8 1.0 fusion.50
  (48 shorter events, 1.0 us)
Async XLA Ops:
  7.2 176.1 %copy-start = (bf16[256,1024]{1,0:T(8,128)(2,1)S(1)}, bf16[256,1024]{1,0:T(8,128)(2,1)}, u32[]{:S(2)}) copy-start(bf16[256,1024]{1,0:T(8,128)(2,1)} %param.22) | copy-start | bytes 1572868
  7.2 81.3 %copy-start.5 = (s32[256,8]{0,1:T(8,128)S(1)}, s32[256,8]{0,1:T(8,128)}, u32[]{:S(2)}) copy-start(s32[256,8]{0,1:T(8,128)} %param.15) | copy-start | bytes 24580
  7.2 80.3 %all-gather.3.cloned.1.call-start = ((), (), s32[]{:S(2)}) async-start(), calls=%async_computation.2 | async-start | bytes 2621440 | tf_op jit(solution)/shard_map/all_gather | solution.py:225
  20.0 72.9 %copy-start.1 = (bf16[256,1024]{1,0:T(8,128)(2,1)S(1)}, bf16[256,1024]{1,0:T(8,128)(2,1)}, u32[]{:S(2)}) copy-start(bf16[256,1024]{1,0:T(8,128)(2,1)} %param.13) | copy-start | bytes 1572868
  32.9 142.0 %all-gather.5.cloned.1.call-start = ((), (), s32[]{:S(2)}) async-start(), calls=%async_computation.3 | async-start | bytes 10485760 | tf_op jit(solution)/shard_map/all_gather | solution.py:225
  183.1 17.5 %copy-start.7 = (bf16[1024]{0:T(1024)(128)(2,1)S(1)}, bf16[1024]{0:T(1024)(128)(2,1)}, u32[]{:S(2)}) copy-start(bf16[1024]{0:T(1024)(128)(2,1)} %param.18) | copy-start | bytes 6148
  185.1 2.3 collective-permute-start
  187.5 11.7 %collective-permute-start.1 = (bf16[256,512]{1,0:T(8,128)(2,1)S(1)}, bf16[256,512]{1,0:T(8,128)(2,1)S(1)}, u32[]{:S(2)}, u32[]{:S(2)}) collective-permute-start(bf16[256,512]{1,0:T(8,128)(2,1)S(1)} %fusion.55), channel_id=1, source_target_pairs={{0,2},{2,0},{1,3},{3,1},{4,6},{6,4},{5,7},{7,5},{8,10},{10,8},{9,1... | collective-permute-start | bytes 786440 | tf_op jit(solution)/shard_map/ppermute | solution.py:166
  199.2 3.0 collective-permute-start.2
  205.1 139.4 %copy-start.4 = (bf16[1,1024,128]{2,1,0:T(8,128)(2,1)S(1)}, bf16[1,1024,128]{2,1,0:T(8,128)(2,1)}, u32[]{:S(2)}) copy-start(bf16[1,1024,128]{2,1,0:T(8,128)(2,1)} %param.23) | copy-start | bytes 786436
  341.9 6.0 %copy-start.2 = (bf16[1,128,1024]{2,1,0:T(8,128)(2,1)S(1)}, bf16[1,128,1024]{2,1,0:T(8,128)(2,1)}, u32[]{:S(2)}) copy-start(bf16[1,128,1024]{2,1,0:T(8,128)(2,1)} %param.25) | copy-start | bytes 786436
  341.9 6.1 %copy-start.3 = (bf16[1,1024,128]{2,1,0:T(8,128)(2,1)S(1)}, bf16[1,1024,128]{2,1,0:T(8,128)(2,1)}, u32[]{:S(2)}) copy-start(bf16[1,1024,128]{2,1,0:T(8,128)(2,1)} %param.24) | copy-start | bytes 786436
  341.9 14.3 %collective-permute-start.3 = (bf16[64,1,32,1024]{3,2,1,0:T(8,128)(2,1)}, bf16[64,1,32,1024]{3,2,1,0:T(8,128)(2,1)}, u32[]{:S(2)}, u32[]{:S(2)}) collective-permute-start(bf16[64,1,32,1024]{3,2,1,0:T(8,128)(2,1)} %all_to_all.10), channel_id=1, source_target_pairs={{0,1},{1,0},{2,3},{3,2},{4,5},{5,4},{6,7},{7,6},{8,9},{9,8},{10,11... | collective-permute-start | bytes 12582920 | tf_op jit(solution)/shard_map/ppermute | solution.py:277
  367.8 7.4 %collective-permute-start.4 = (bf16[64,1,32,1024]{3,2,0,1:T(8,128)(2,1)}, bf16[64,1,32,1024]{3,2,0,1:T(8,128)(2,1)S(1)}, u32[]{:S(2)}, u32[]{:S(2)}) collective-permute-start(bf16[64,1,32,1024]{3,2,0,1:T(8,128)(2,1)} %convert_bitcast_fusion), channel_id=1, source_target_pairs={{0,1},{1,0},{2,3},{3,2},{4,5},{5,4},{6,7},{7,6},{8,9},{9,8},{10,11... | collective-permute-start | bytes 12582920 | tf_op jit(solution)/shard_map/ppermute | solution.py:287
  381.5 6.1 %copy-start.6 = (f32[256,8]{0,1:T(8,128)S(1)}, f32[256,8]{0,1:T(8,128)}, u32[]{:S(2)}) copy-start(f32[256,8]{0,1:T(8,128)} %param.16) | copy-start | bytes 24580
  381.5 101.4 %all-to-all-start.1 = ((bf16[64,1,32,1024]{3,2,1,0:T(8,128)(2,1)}), bf16[64,1,32,1024]{3,2,1,0:T(8,128)(2,1)}, u32[]{:S(2)}, u32[]{:S(2)}) async-start(bf16[64,1,32,1024]{3,2,1,0:T(8,128)(2,1)} %fusion.1), calls=%async_computation.1 | async-start | bytes 8388608 | tf_op jit(solution)/shard_map/all_to_all | solution.py:291
  490.8 2.8 collective-permute-start.5
  493.7 17.1 %collective-permute-start.6 = (bf16[256,512]{1,0:T(8,128)(2,1)S(1)}, bf16[256,512]{1,0:T(8,128)(2,1)S(1)}, u32[]{:S(2)}, u32[]{:S(2)}) collective-permute-start(bf16[256,512]{1,0:T(8,128)(2,1)S(1)} %fusion.54), channel_id=1, source_target_pairs={{0,2},{2,0},{1,3},{3,1},{4,6},{6,4},{5,7},{7,5},{8,10},{10,8},{9,1... | collective-permute-start | bytes 786440 | tf_op jit(solution)/shard_map/ppermute | solution.py:166
  510.9 2.9 collective-permute-start.7
Sparse Core Ops, SparseCore 0:
  33.1 54.4 all-gather.2
  89.3 85.5 all-gather.4
